TPU v7x, 256 devices: a whole 4x4x8 slice. The times are simulated.
256 devices in a mesh: row: 16 (over z, core), col: 16 (over y, x).
Axes of the slice: x: 4, y: 4, z: 8, core: 2. Of those that a mesh axis runs over, the one named last changes fastest.
Arguments:
- prior_window_motion: float32 [3, 128, 128, 256], P(None, 'row', 'col'), may hold values from -1.2 to 1.2
- prior_window_stress: float32 [128, 128, 256], P('row', 'col'), may hold values from -3 to 3
- heat_scalar: float32 [128, 128, 256], P('row', 'col'), may hold values from 0 to 1
Outputs:
- velocity: float32 [3, 128, 128, 256], P(None, 'row', 'col')
- pressure: float32 [128, 128, 256], P('row', 'col')
All inputs are finite; a program needn't handle non-finite values.
Results may differ from a plain program's by a relative error of at most 0.0003.
Values sent between devices are 32-bit elements; how exact they have to be, the bound alone decides.
No kernel may reach another device: no remote copies, remote signals or barrier semaphores. Data moves between devices by JAX's collectives and lax.ppermute only.
A program may use at most 64 MiB of HBM per device.

v0:
```python
import jax
import jax.numpy as jnp
from jax import lax
from jax.sharding import PartitionSpec as P

OUTER = 2
INNER = 2


PRECISE = lax.Precision.HIGHEST
ENABLE_SWITCH = 2.0
OFFSET_COUNT = 0.5
AUGMENT = 1.0
ANCHOR = 0.002
RAYLEIGH_NUMBER = 1.0
SMOOTHING = 2.0


def padded(cells, sides, width):
    for axis, dim in sides:
        count = lax.axis_size(axis)
        head = lax.slice_in_dim(cells, 0, width, axis=dim)
        tail = lax.slice_in_dim(cells, cells.shape[dim] - width, cells.shape[dim], axis=dim)
        cells = jnp.concatenate(
            [
                lax.ppermute(tail, axis, [(i, (i + 1) % count) for i in range(count)]),
                cells,
                lax.ppermute(head, axis, [((i + 1) % count, i) for i in range(count)]),
            ],
            axis=dim,
        )
    return cells


def from_behind(value, axis, steps):
    count = lax.axis_size(axis)
    pairs = [(source, (source + steps) % count) for source in range(count)]
    return lax.ppermute(value, axis, pairs)


def cas_matrix(extent):
    index = jnp.arange(extent, dtype=jnp.int32)
    phase = index[:, None] * index[None, :] % extent
    angle = 2.0 * jnp.pi / extent * phase.astype(jnp.float32)
    return jnp.cos(angle) + jnp.sin(angle)


def eigen_row(number, offset_index, extent):
    index = offset_index + jnp.arange(number, dtype=jnp.int32)
    return 2.0 - 2.0 * jnp.cos(2.0 * jnp.pi / extent * index.astype(jnp.float32))


def precondition(residual, tables):
    xtable, ytable, ztable = tables
    row_count = lax.axis_size("row")
    col_count = lax.axis_size("col")
    components, owned_height_lines, owned_depth_slices, period_extent_first = residual.shape
    ylength = owned_height_lines * row_count
    zlength = owned_depth_slices * col_count
    normal_factor = 1.0 / (period_extent_first * ylength * zlength)
    xpiece = period_extent_first // row_count
    ypiece = ylength // col_count
    spectrum = jnp.einsum("kx,cyzx->cykz", xtable, residual, precision=PRECISE).reshape(
        components, owned_height_lines, period_extent_first * owned_depth_slices
    )
    spectrum = lax.all_to_all(spectrum, "row", split_axis=2, concat_axis=1, tiled=True)
    spectrum = jnp.einsum(
        "ky,cyxz->czkx",
        ytable,
        spectrum.reshape(components, ylength, xpiece, owned_depth_slices),
        precision=PRECISE,
    ).reshape(components, owned_depth_slices, ylength * xpiece)
    spectrum = lax.all_to_all(spectrum, "col", split_axis=2, concat_axis=1, tiled=True)
    zeigen = eigen_row(zlength, 0, zlength)
    yeigen = eigen_row(ypiece, lax.axis_index("col") * ypiece, ylength)
    xeigen = eigen_row(xpiece, lax.axis_index("row") * xpiece, period_extent_first)
    mixed_eigen = (yeigen[:, None] + xeigen[None, :]).reshape(-1)
    symbol = normal_factor / (SMOOTHING * (zeigen[:, None] + mixed_eigen[None, :]) + ANCHOR)
    spectrum = jnp.einsum("kz,czm->ckm", ztable, spectrum, precision=PRECISE)
    spectrum = jnp.einsum("kz,czm->ckm", ztable, spectrum * symbol[None], precision=PRECISE)
    spectrum = lax.all_to_all(spectrum, "col", split_axis=1, concat_axis=2, tiled=True)
    spectrum = jnp.einsum(
        "ky,czyx->ckxz",
        ytable,
        spectrum.reshape(components, owned_depth_slices, ylength, xpiece),
        precision=PRECISE,
    ).reshape(components, ylength, xpiece * owned_depth_slices)
    spectrum = lax.all_to_all(spectrum, "row", split_axis=1, concat_axis=2, tiled=True)
    return jnp.einsum(
        "kx,cyxz->cyzk",
        xtable,
        spectrum.reshape(components, owned_height_lines, period_extent_first, owned_depth_slices),
        precision=PRECISE,
    )


def forward(extended, direction):
    owned_height_lines = extended.shape[-3] - 2
    owned_depth_slices = extended.shape[-2] - 2
    root = extended[..., : owned_height_lines + 1, : owned_depth_slices + 1, :]
    if direction == 0:
        return jnp.roll(root, -1, -1) - root
    if direction == 1:
        return extended[..., 1 : owned_height_lines + 2, : owned_depth_slices + 1, :] - root
    return extended[..., : owned_height_lines + 1, 1 : owned_depth_slices + 2, :] - root


def backward(region, direction):
    center = region[..., 1:, 1:, :]
    if direction == 0:
        return center - jnp.roll(center, 1, -1)
    if direction == 1:
        return center - region[..., :-1, 1:, :]
    return center - region[..., 1:, :-1, :]


def extend(field):
    return padded(field, (("row", 1), ("col", 2)), 1)


def lower_region(pressure):
    below_y = from_behind(pressure[-1:], "row", 1)
    below_z = from_behind(pressure[:, -1:], "col", 1)
    corner = jnp.zeros((1, 1, pressure.shape[2]), jnp.float32)
    upper_band = jnp.concatenate([corner, below_y], 1)
    main_band = jnp.concatenate([below_z, pressure], 1)
    return jnp.concatenate([upper_band, main_band], 0)


def operate(extended, shear_resistance_map):
    owned_height_lines = extended.shape[1] - 2
    owned_depth_slices = extended.shape[2] - 2
    gradients = [[forward(extended[target], source) for source in range(3)] for target in range(3)]
    spread = gradients[0][0] + gradients[1][1] + gradients[2][2]
    result = []
    for target in range(3):
        summed = (
            ANCHOR * extended[target, 1 : owned_height_lines + 1, 1 : owned_depth_slices + 1, :]
        )
        for source in range(3):
            fluxes = shear_resistance_map * (gradients[target][source] + gradients[source][target])
            if target == source:
                fluxes = fluxes + AUGMENT * spread
            summed = summed - backward(fluxes, source)
        result.append(summed)
    return jnp.stack(result)


def pressure_gradient(region):
    return jnp.stack([-backward(region, target) for target in range(3)])


def divergence_region(extended):
    return forward(extended[0], 0) + forward(extended[1], 1) + forward(extended[2], 2)


def per_device(prior_window_motion, prior_window_stress, heat_scalar):
    owned_height_lines, owned_depth_slices, period_extent_first = heat_scalar.shape
    tables = (
        cas_matrix(period_extent_first),
        cas_matrix(owned_height_lines * lax.axis_size("row")),
        cas_matrix(owned_depth_slices * lax.axis_size("col")),
    )
    stacked_fields = jnp.concatenate(
        [prior_window_motion, prior_window_stress[None], heat_scalar[None]], 0
    )
    extended = padded(stacked_fields, (("row", 1), ("col", 2)), 1)
    shear_resistance_map = jnp.exp(
        ENABLE_SWITCH
        * (
            1.0
            / (extended[4, : owned_height_lines + 1, : owned_depth_slices + 1, :] + OFFSET_COUNT)
            - 1.0 / (0.5 + OFFSET_COUNT)
        )
    )
    thermal_lift = RAYLEIGH_NUMBER * (heat_scalar - 0.5)
    zeroes = jnp.zeros_like(thermal_lift)
    forcing = jnp.stack([zeroes, zeroes, thermal_lift])
    velocity = prior_window_motion
    pressure = prior_window_stress
    velocity_ext = extended[0:3]
    pushing = pressure_gradient(extended[3, : owned_height_lines + 1, : owned_depth_slices + 1, :])
    spread_now = jnp.zeros_like(shear_resistance_map)
    for outer_step in range(OUTER):
        if outer_step > 0:
            pushing = pressure_gradient(lower_region(pressure))
        residual = forcing - pushing - operate(velocity_ext, shear_resistance_map)
        direction = residual
        image = residual
        energy_now = jnp.float32(1.0)
        step_size = jnp.float32(1.0)
        for inner_step in range(INNER):
            precond = precondition(residual, tables)
            energy_next = lax.psum(jnp.sum(residual * precond), ("row", "col"))
            if inner_step == 0:
                direction = precond
            else:
                direction = precond + energy_next / energy_now * direction
            energy_now = energy_next
            image = operate(extend(direction), shear_resistance_map)
            curvature = lax.psum(jnp.sum(direction * image), ("row", "col"))
            step_size = energy_now / curvature
            velocity = velocity + step_size * direction
            residual = residual - step_size * image
        velocity_ext = extend(velocity)
        spread_now = divergence_region(velocity_ext)
        pressure = pressure + AUGMENT * spread_now[1:, 1:, :]
    return (velocity, pressure)


def solution(mesh):
    placed = (P(None, "row", "col", None), P("row", "col", None), P("row", "col", None))
    return jax.shard_map(
        per_device,
        mesh=mesh,
        in_specs=placed,
        out_specs=(P(None, "row", "col", None), P("row", "col", None)),
        check_vma=False,
    )
```

profile of v0, /device:TPU:1, one launch (start us, length us, event | category | flops | bytes accessed | tf_op | source)
XLA Modules:
  0.0 1028.9 jit_solution(2103206964599574180)
XLA Ops:
  30.9 9.8 all-to-all-start
  42.0 8.7 all-to-all-done
  63.4 5.9 fusion.8
  78.9 5.6 all-to-all-start.1
  84.6 7.9 all-to-all-done.1
  102.4 10.5 %all_to_all.252 = f32[3,128,128]{2,0,1:T(4,128)S(1)} all-to-all(f32[3,128,128]{2,0,1:T(4,128)S(1)} %copy.219), channel_id=1, replica_groups=mesh['row'=16,'col'=16] {'col'}, dimensions={1} | all-to-all | bytes 393216 | tf_op jit(solution)/shard_map/all_to_all | solution.py:81
  116.3 16.6 %all_to_all.253 = f32[3,128,128]{2,0,1:T(4,128)S(1)} all-to-all(f32[3,128,128]{2,0,1:T(4,128)S(1)} %copy.224), channel_id=1, replica_groups=mesh['row'=16,'col'=16] {'row'}, dimensions={1} | all-to-all | bytes 393216 | tf_op jit(solution)/shard_map/all_to_all | solution.py:88
  136.3 5.6 fusion.36
  153.8 78.0 %all-reduce.3 = (f32[]{:T(128)}, f32[]{:T(128)}) all-reduce(f32[]{:T(128)} %get-tuple-element.5, f32[]{:T(128)} %get-tuple-element.4), channel_id=1, replica_groups=mesh['row'=16,'col'=16] {'row','col'}, use_global_device_ids=true, to_apply=%region_1.2 | all-reduce | flops 2 | bytes 16 | tf_op jit(solution)/shard_map/psum | solution.py:194
  243.4 14.7 %all_to_all.254 = f32[16,1,3072]{2,1,0:T(1,128)S(1)} all-to-all(f32[16,1,3072]{2,1,0:T(1,128)S(1)} %reshape.234), channel_id=1, replica_groups=mesh['row'=16,'col'=16] {'row'}, dimensions={0} | all-to-all | bytes 393216 | tf_op jit(solution)/shard_map/all_to_all | solution.py:66
  270.1 5.9 fusion.11
  285.0 11.3 %all_to_all.255 = f32[16,1,3072]{2,1,0:T(1,128)S(1)} all-to-all(f32[16,1,3072]{2,1,0:T(1,128)S(1)} %reshape.236), channel_id=1, replica_groups=mesh['row'=16,'col'=16] {'col'}, dimensions={0} | all-to-all | bytes 393216 | tf_op jit(solution)/shard_map/all_to_all | solution.py:73
  306.3 10.3 all_to_all.256
  319.9 16.6 %all_to_all.257 = f32[3,128,128]{2,0,1:T(4,128)S(1)} all-to-all(f32[3,128,128]{2,0,1:T(4,128)S(1)} %copy.243), channel_id=1, replica_groups=mesh['row'=16,'col'=16] {'row'}, dimensions={1} | all-to-all | bytes 393216 | tf_op jit(solution)/shard_map/all_to_all | solution.py:88
  339.9 8.0 multiply_reduce_fusion.3
  347.9 72.2 %psum.58 = f32[]{:T(128)} all-reduce(f32[]{:T(128)} %get-tuple-element.122), channel_id=1, replica_groups=mesh['row'=16,'col'=16] {'row','col'}, use_global_device_ids=true, to_apply=%region_5.6 | all-reduce | flops 1 | bytes 8 | tf_op jit(solution)/shard_map/psum | solution.py:194
  436.8 76.3 %psum.59 = f32[]{:T(128)} all-reduce(f32[]{:T(128)} %fusion.44), channel_id=1, replica_groups=mesh['row'=16,'col'=16] {'row','col'}, use_global_device_ids=true, to_apply=%region_7.8 | all-reduce | flops 1 | bytes 8 | tf_op jit(solution)/shard_map/psum | solution.py:201
  545.4 15.8 %all_to_all.258 = f32[16,1,3072]{2,1,0:T(1,128)S(1)} all-to-all(f32[16,1,3072]{2,1,0:T(1,128)S(1)} %reshape.238), channel_id=1, replica_groups=mesh['row'=16,'col'=16] {'row'}, dimensions={0} | all-to-all | bytes 393216 | tf_op jit(solution)/shard_map/all_to_all | solution.py:66
  571.4 5.2 fusion.14
  584.4 11.5 %all_to_all.259 = f32[16,1,3072]{2,1,0:T(1,128)S(1)} all-to-all(f32[16,1,3072]{2,1,0:T(1,128)S(1)} %reshape.240), channel_id=1, replica_groups=mesh['row'=16,'col'=16] {'col'}, dimensions={0} | all-to-all | bytes 393216 | tf_op jit(solution)/shard_map/all_to_all | solution.py:73
  605.8 10.8 %all_to_all.260 = f32[3,128,128]{2,0,1:T(4,128)S(1)} all-to-all(f32[3,128,128]{2,0,1:T(4,128)S(1)} %copy.257), channel_id=1, replica_groups=mesh['row'=16,'col'=16] {'col'}, dimensions={1} | all-to-all | bytes 393216 | tf_op jit(solution)/shard_map/all_to_all | solution.py:81
  619.9 16.6 %all_to_all.261 = f32[3,128,128]{2,0,1:T(4,128)S(1)} all-to-all(f32[3,128,128]{2,0,1:T(4,128)S(1)} %copy.262), channel_id=1, replica_groups=mesh['row'=16,'col'=16] {'row'}, dimensions={1} | all-to-all | bytes 393216 | tf_op jit(solution)/shard_map/all_to_all | solution.py:88
  638.3 5.6 fusion.30
  655.7 78.0 %all-reduce.2 = (f32[]{:T(128)}, f32[]{:T(128)}) all-reduce(f32[]{:T(128)} %get-tuple-element.3, f32[]{:T(128)} %get-tuple-element.2), channel_id=1, replica_groups=mesh['row'=16,'col'=16] {'row','col'}, use_global_device_ids=true, to_apply=%region_9.10 | all-reduce | flops 2 | bytes 16 | tf_op jit(solution)/shard_map/psum | solution.py:194
  745.3 14.7 %all_to_all.262 = f32[16,1,3072]{2,1,0:T(1,128)S(1)} all-to-all(f32[16,1,3072]{2,1,0:T(1,128)S(1)} %reshape.242), channel_id=1, replica_groups=mesh['row'=16,'col'=16] {'row'}, dimensions={0} | all-to-all | bytes 393216 | tf_op jit(solution)/shard_map/all_to_all | solution.py:66
  772.1 5.9 fusion.17
  786.9 11.1 %all_to_all.263 = f32[16,1,3072]{2,1,0:T(1,128)S(1)} all-to-all(f32[16,1,3072]{2,1,0:T(1,128)S(1)} %reshape.244), channel_id=1, replica_groups=mesh['row'=16,'col'=16] {'col'}, dimensions={0} | all-to-all | bytes 393216 | tf_op jit(solution)/shard_map/all_to_all | solution.py:73
  807.9 10.3 all_to_all.264
  821.5 16.6 %all_to_all.265 = f32[3,128,128]{2,0,1:T(4,128)S(1)} all-to-all(f32[3,128,128]{2,0,1:T(4,128)S(1)} %copy.281), channel_id=1, replica_groups=mesh['row'=16,'col'=16] {'row'}, dimensions={1} | all-to-all | bytes 393216 | tf_op jit(solution)/shard_map/all_to_all | solution.py:88
  841.6 7.9 multiply_reduce_fusion
  849.4 72.2 %psum.62 = f32[]{:T(128)} all-reduce(f32[]{:T(128)} %get-tuple-element.124), channel_id=1, replica_groups=mesh['row'=16,'col'=16] {'row','col'}, use_global_device_ids=true, to_apply=%region_13.14 | all-reduce | flops 1 | bytes 8 | tf_op jit(solution)/shard_map/psum | solution.py:194
  938.4 76.3 %psum.63 = f32[]{:T(128)} all-reduce(f32[]{:T(128)} %fusion.45), channel_id=1, replica_groups=mesh['row'=16,'col'=16] {'row','col'}, use_global_device_ids=true, to_apply=%region_15.16 | all-reduce | flops 1 | bytes 8 | tf_op jit(solution)/shard_map/psum | solution.py:201
  (421 shorter events, 296.2 us)
Async XLA Ops:
  1.5 4.1 collective-permute-start
  4.6 3.4 collective-permute-start.1
  9.2 6.5 collective-permute-start.2
  10.6 6.1 collective-permute-start.3
  30.9 19.9 %all-to-all-start = ((f32[16,1,3072]{2,1,0:T(1,128)}), f32[16,1,3072]{2,1,0:T(1,128)S(1)}, u32[]{:S(2)}, u32[]{:S(2)}) async-start(f32[16,1,3072]{2,1,0:T(1,128)} %reshape.230), calls=%async_computation | async-start | bytes 393216 | tf_op jit(solution)/shard_map/all_to_all | solution.py:66
  78.9 13.6 %all-to-all-start.1 = ((f32[16,1,3072]{2,1,0:T(1,128)}), f32[16,1,3072]{2,1,0:T(1,128)S(1)}, u32[]{:S(2)}, u32[]{:S(2)}) async-start(f32[16,1,3072]{2,1,0:T(1,128)} %reshape.232), calls=%async_computation.1 | async-start | bytes 393216 | tf_op jit(solution)/shard_map/all_to_all | solution.py:73
  141.9 1.2 collective-permute-start.4
  141.9 3.4 collective-permute-start.5
  145.4 6.1 collective-permute-start.6
  145.7 5.8 collective-permute-start.7
  422.3 3.3 collective-permute-start.8
  424.7 3.3 collective-permute-start.9
  428.0 6.9 collective-permute-start.10
  428.8 6.1 collective-permute-start.11
  514.5 2.9 collective-permute-start.12
  516.4 3.3 collective-permute-start.13
  519.8 6.1 collective-permute-start.14
  519.9 6.1 collective-permute-start.15
  527.0 2.2 collective-permute-start.16
  528.1 6.1 collective-permute-start.17
  643.9 1.2 collective-permute-start.18
  643.9 3.4 collective-permute-start.19
  647.4 6.1 collective-permute-start.20
  647.7 5.8 collective-permute-start.21
  923.9 3.3 collective-permute-start.22
  926.2 3.3 collective-permute-start.23
  929.5 7.0 collective-permute-start.24
  930.4 6.1 collective-permute-start.25
  1016.1 2.9 collective-permute-start.26
  1018.1 3.3 collective-permute-start.27
  1021.4 6.1 collective-permute-start.28
  1021.5 6.1 collective-permute-start.29
  (54 other events, 1257.5 us)
where the time goes:
time: 1040 us; the launch traced here: 1030 us
  blocking collectives  640 us (62%)
  local copies, waits for them, and re-layouts  164 us (16%)
  matrix products  71.2 us (7%)
  starting transfers between devices  64.1 us (6%)
  waiting for transfers between devices  53.8 us (5%)
  other arithmetic  25 us (2%)
  between operations  10.7 us (1%)
    psum x4, blocking collectives, per_device(): energy_next = lax.psum(jnp.sum(residual * precond), ('row', 'col'))  300 us
    psum x2, blocking collectives, per_device(): curvature = lax.psum(jnp.sum(direction * image), ('row', 'col'))  153 us
    unnamed x124, local copies, waits for them, and re-layouts  70.5 us
    all_to_all x4, blocking collectives, precondition(): lax.all_to_all(spectrum, 'row', split_axis=1, concat_axis=2, tiled=True)  66.4 us
    all_to_all x3, blocking collectives, precondition(): lax.all_to_all(spectrum, 'row', split_axis=2, concat_axis=1, tiled=True)  45.1 us
    all_to_all x4, blocking collectives, precondition(): lax.all_to_all(spectrum, 'col', split_axis=1, concat_axis=2, tiled=True)  41.9 us
    all_to_all x3, blocking collectives, precondition(): lax.all_to_all(spectrum, 'col', split_axis=2, concat_axis=1, tiled=True)  33.8 us
    ppermute x14, starting transfers between devices, padded(): lax.ppermute(head, axis, [((i + 1) % count, i) for i in range(count)])  32.1 us
  transfers between devices with their start and end apart: 32, of which 24 were waited for; matrix products, arithmetic and copies ran while one was open for 0% of the time, Pallas kernels for 0%

commit v1 on v0

--- a/solution.py
+++ b/solution.py
@@ -30,6 +30,13 @@
             axis=dim,
         )
     return cells
+
+
+def global_sum(value):
+    count = lax.axis_size("row") * lax.axis_size("col")
+    spread = jnp.broadcast_to(value.reshape(1), (count,))
+    gathered = lax.all_to_all(spread, ("row", "col"), 0, 0, tiled=True)
+    return jnp.sum(gathered)
 
 
 def from_behind(value, axis, steps):
@@ -191,14 +198,14 @@
         step_size = jnp.float32(1.0)
         for inner_step in range(INNER):
             precond = precondition(residual, tables)
-            energy_next = lax.psum(jnp.sum(residual * precond), ("row", "col"))
+            energy_next = global_sum(jnp.sum(residual * precond))
             if inner_step == 0:
                 direction = precond
             else:
                 direction = precond + energy_next / energy_now * direction
             energy_now = energy_next
             image = operate(extend(direction), shear_resistance_map)
-            curvature = lax.psum(jnp.sum(direction * image), ("row", "col"))
+            curvature = global_sum(jnp.sum(direction * image))
             step_size = energy_now / curvature
             velocity = velocity + step_size * direction
             residual = residual - step_size * image

time: 1040 us -> 750 us (0.72)
  blocking collectives: 640 us -> 309 us
  waiting for transfers between devices: 53.8 us -> 78.4 us
    psum x6 -> x0, blocking collectives: 453 us -> none  [the longest x4 300 us: per_device(): energy_next = lax.psum(jnp.sum(residual * precond), ('row', 'col'))]
    all_to_all x0 -> x6, blocking collectives: none -> 127 us  [global_sum(): gathered = lax.all_to_all(spread, ('row', 'col'), 0, 0, tiled=True)]
    all_to_all x0 -> x2, waiting for transfers between devices: none -> 24.6 us  [global_sum(): gathered = lax.all_to_all(spread, ('row', 'col'), 0, 0, tiled=True)]
    all_to_all x0 -> x2, starting transfers between devices: none -> 11.4 us  [global_sum(): gathered = lax.all_to_all(spread, ('row', 'col'), 0, 0, tiled=True)]
  transfers between devices with their start and end apart: 32 -> 34, of which waited for: 24 -> 26; matrix products, arithmetic and copies ran while one was open for 0% -> 1% of each run, Pallas kernels for 0% -> 0%
where the time goes in v1:
time: 750 us; the launch traced here: 742 us
  blocking collectives  309 us (41%)
  local copies, waits for them, and re-layouts  171 us (23%)
  waiting for transfers between devices  78.4 us (10%)
  matrix products  71.2 us (9%)
  starting transfers between devices  70 us (9%)
  other arithmetic  31.2 us (4%)
  between operations  11 us (1%)
    all_to_all x6, blocking collectives, global_sum(): gathered = lax.all_to_all(spread, ('row', 'col'), 0, 0, tiled=True)  127 us
    unnamed x124, local copies, waits for them, and re-layouts  70.6 us
    all_to_all x4, blocking collectives, precondition(): lax.all_to_all(spectrum, 'row', split_axis=1, concat_axis=2, tiled=True)  65.7 us
    all_to_all x4, blocking collectives, precondition(): lax.all_to_all(spectrum, 'col', split_axis=1, concat_axis=2, tiled=True)  42.9 us
    all_to_all x3, blocking collectives, precondition(): lax.all_to_all(spectrum, 'row', split_axis=2, concat_axis=1, tiled=True)  41.7 us
    all_to_all x3, blocking collectives, precondition(): lax.all_to_all(spectrum, 'col', split_axis=2, concat_axis=1, tiled=True)  32 us
    ppermute x14, starting transfers between devices, padded(): lax.ppermute(head, axis, [((i + 1) % count, i) for i in range(count)])  31.9 us
    dot_general x4, matrix products, precondition(): jnp.einsum('kx,cyxz->cyzk', xtable, spectrum.reshape(components, owned_he...  27.1 us
  transfers between devices with their start and end apart: 34, of which 26 were waited for; matrix products, arithmetic and copies ran while one was open for 1% of the time, Pallas kernels for 0%

profile of v1, /device:TPU:1, one launch (start us, length us, event | category | flops | bytes accessed | tf_op | source)
XLA Modules:
  0.0 742.2 jit_solution(7646809558216230969)
XLA Ops:
  30.9 9.5 %all-to-all-start = ((f32[16,1,3072]{2,1,0:T(1,128)}), f32[16,1,3072]{2,1,0:T(1,128)S(1)}, u32[]{:S(2)}, u32[]{:S(2)}) async-start(f32[16,1,3072]{2,1,0:T(1,128)} %reshape.262), calls=%async_computation | async-start | bytes 393216 | tf_op jit(solution)/shard_map/all_to_all | solution.py:73
  41.7 8.8 %all-to-all-done = f32[16,1,3072]{2,1,0:T(1,128)S(1)} async-done(((f32[16,1,3072]{2,1,0:T(1,128)}), f32[16,1,3072]{2,1,0:T(1,128)S(1)}, u32[]{:S(2)}, u32[]{:S(2)}) %all-to-all-start) | async-done | bytes 196640 | tf_op jit(solution)/shard_map/all_to_all | solution.py:73
  63.0 5.9 fusion.8
  84.2 7.9 %all-to-all-done.1 = f32[16,1,3072]{2,1,0:T(1,128)S(1)} async-done(((f32[16,1,3072]{2,1,0:T(1,128)}), f32[16,1,3072]{2,1,0:T(1,128)S(1)}, u32[]{:S(2)}, u32[]{:S(2)}) %all-to-all-start.1) | async-done | bytes 196640 | tf_op jit(solution)/shard_map/all_to_all | solution.py:80
  101.9 10.8 %all_to_all.300 = f32[3,128,128]{2,0,1:T(4,128)S(1)} all-to-all(f32[3,128,128]{2,0,1:T(4,128)S(1)} %copy.371), channel_id=1, replica_groups=mesh['row'=16,'col'=16] {'col'}, dimensions={1} | all-to-all | bytes 393216 | tf_op jit(solution)/shard_map/all_to_all | solution.py:88
  116.1 16.6 %all_to_all.301 = f32[3,128,128]{2,0,1:T(4,128)S(1)} all-to-all(f32[3,128,128]{2,0,1:T(4,128)S(1)} %copy.376), channel_id=1, replica_groups=mesh['row'=16,'col'=16] {'row'}, dimensions={1} | all-to-all | bytes 393216 | tf_op jit(solution)/shard_map/all_to_all | solution.py:95
  154.1 23.2 %all_to_all.302 = f32[256,1,1]{2,1,0:T(1,128)S(1)} all-to-all(f32[256,1,1]{2,1,0:T(1,128)S(1)} %broadcast_in_dim.23), channel_id=1, replica_groups=mesh['row'=16,'col'=16] {'row','col'}, dimensions={0} | all-to-all | bytes 2048 | tf_op jit(solution)/shard_map/all_to_all | solution.py:38
  178.7 5.7 all-to-all-start.4
  185.3 12.3 %all-to-all-done.4 = f32[256,1,1]{2,1,0:T(1,128)S(1)} async-done(((f32[256,1,1]{2,1,0:T(1,128)}), f32[256,1,1]{2,1,0:T(1,128)S(1)}, u32[]{:S(2)}, u32[]{:S(2)}) %all-to-all-start.4) | async-done | bytes 1056 | tf_op jit(solution)/shard_map/all_to_all | solution.py:38
  210.1 13.2 %all_to_all.303 = f32[16,1,3072]{2,1,0:T(1,128)S(1)} all-to-all(f32[16,1,3072]{2,1,0:T(1,128)S(1)} %reshape.266), channel_id=1, replica_groups=mesh['row'=16,'col'=16] {'row'}, dimensions={0} | all-to-all | bytes 393216 | tf_op jit(solution)/shard_map/all_to_all | solution.py:73
  235.3 5.9 fusion.11
  250.2 10.6 %all_to_all.304 = f32[16,1,3072]{2,1,0:T(1,128)S(1)} all-to-all(f32[16,1,3072]{2,1,0:T(1,128)S(1)} %reshape.268), channel_id=1, replica_groups=mesh['row'=16,'col'=16] {'col'}, dimensions={0} | all-to-all | bytes 393216 | tf_op jit(solution)/shard_map/all_to_all | solution.py:80
  270.7 10.8 %all_to_all.305 = f32[3,128,128]{2,0,1:T(4,128)S(1)} all-to-all(f32[3,128,128]{2,0,1:T(4,128)S(1)} %copy.392), channel_id=1, replica_groups=mesh['row'=16,'col'=16] {'col'}, dimensions={1} | all-to-all | bytes 393216 | tf_op jit(solution)/shard_map/all_to_all | solution.py:88
  284.8 16.4 %all_to_all.306 = f32[3,128,128]{2,0,1:T(4,128)S(1)} all-to-all(f32[3,128,128]{2,0,1:T(4,128)S(1)} %copy.397), channel_id=1, replica_groups=mesh['row'=16,'col'=16] {'row'}, dimensions={1} | all-to-all | bytes 393216 | tf_op jit(solution)/shard_map/all_to_all | solution.py:95
  304.5 8.0 %multiply_reduce_fusion.3 = (f32[]{:T(128)}, f32[3,8,8,256]{3,2,1,0:T(8,128)}) fusion(f32[3,8,8,256]{3,2,1,0:T(8,128)} %copy-done.17, f32[1,8,8,256]{3,2,1,0:T(8,128)} %copy-done.23, f32[1,8,8,256]{3,2,1,0:T(8,128)} %copy-done.27, f32[1,8,8,256]{3,2,1,0:T(8,128)} %copy-done.26, f32[]{:T(128)S(6)} %div.34, f32[3,8,256,8]{3,2,1,0:T(8,128)S(1)} %reshape.245), kind=kOutput, calls=%fused_computation.94 | convolution fusion | flops 152272896 | bytes 786440 | tf_op jit(solution)/shard_map/kx,cyxz->cyzk/dot_general | solution.py:96
  313.3 17.5 %all_to_all.307 = f32[256,1,1]{2,1,0:T(1,128)S(1)} all-to-all(f32[256,1,1]{2,1,0:T(1,128)S(1)} %broadcast_in_dim.24), channel_id=1, replica_groups=mesh['row'=16,'col'=16] {'row','col'}, dimensions={0} | all-to-all | bytes 2048 | tf_op jit(solution)/shard_map/all_to_all | solution.py:38
  347.4 22.7 %all_to_all.308 = f32[256,1,1]{2,1,0:T(1,128)S(1)} all-to-all(f32[256,1,1]{2,1,0:T(1,128)S(1)} %broadcast_in_dim.25), channel_id=1, replica_groups=mesh['row'=16,'col'=16] {'row','col'}, dimensions={0} | all-to-all | bytes 2048 | tf_op jit(solution)/shard_map/all_to_all | solution.py:38
  402.4 15.3 %all_to_all.309 = f32[16,1,3072]{2,1,0:T(1,128)S(1)} all-to-all(f32[16,1,3072]{2,1,0:T(1,128)S(1)} %reshape.270), channel_id=1, replica_groups=mesh['row'=16,'col'=16] {'row'}, dimensions={0} | all-to-all | bytes 393216 | tf_op jit(solution)/shard_map/all_to_all | solution.py:73
  440.8 10.8 %all_to_all.310 = f32[16,1,3072]{2,1,0:T(1,128)S(1)} all-to-all(f32[16,1,3072]{2,1,0:T(1,128)S(1)} %reshape.272), channel_id=1, replica_groups=mesh['row'=16,'col'=16] {'col'}, dimensions={0} | all-to-all | bytes 393216 | tf_op jit(solution)/shard_map/all_to_all | solution.py:80
  461.5 10.8 %all_to_all.311 = f32[3,128,128]{2,0,1:T(4,128)S(1)} all-to-all(f32[3,128,128]{2,0,1:T(4,128)S(1)} %copy.413), channel_id=1, replica_groups=mesh['row'=16,'col'=16] {'col'}, dimensions={1} | all-to-all | bytes 393216 | tf_op jit(solution)/shard_map/all_to_all | solution.py:88
  475.6 16.4 %all_to_all.312 = f32[3,128,128]{2,0,1:T(4,128)S(1)} all-to-all(f32[3,128,128]{2,0,1:T(4,128)S(1)} %copy.418), channel_id=1, replica_groups=mesh['row'=16,'col'=16] {'row'}, dimensions={1} | all-to-all | bytes 393216 | tf_op jit(solution)/shard_map/all_to_all | solution.py:95
  512.1 23.2 %all_to_all.313 = f32[256,1,1]{2,1,0:T(1,128)S(1)} all-to-all(f32[256,1,1]{2,1,0:T(1,128)S(1)} %broadcast_in_dim.27), channel_id=1, replica_groups=mesh['row'=16,'col'=16] {'row','col'}, dimensions={0} | all-to-all | bytes 2048 | tf_op jit(solution)/shard_map/all_to_all | solution.py:38
  536.7 5.7 all-to-all-start.16
  543.3 12.3 %all-to-all-done.16 = f32[256,1,1]{2,1,0:T(1,128)S(1)} async-done(((f32[256,1,1]{2,1,0:T(1,128)}), f32[256,1,1]{2,1,0:T(1,128)S(1)}, u32[]{:S(2)}, u32[]{:S(2)}) %all-to-all-start.16) | async-done | bytes 1056 | tf_op jit(solution)/shard_map/all_to_all | solution.py:38
  568.1 13.2 %all_to_all.314 = f32[16,1,3072]{2,1,0:T(1,128)S(1)} all-to-all(f32[16,1,3072]{2,1,0:T(1,128)S(1)} %reshape.274), channel_id=1, replica_groups=mesh['row'=16,'col'=16] {'row'}, dimensions={0} | all-to-all | bytes 393216 | tf_op jit(solution)/shard_map/all_to_all | solution.py:73
  593.3 5.9 fusion.17
  608.2 10.6 %all_to_all.315 = f32[16,1,3072]{2,1,0:T(1,128)S(1)} all-to-all(f32[16,1,3072]{2,1,0:T(1,128)S(1)} %reshape.276), channel_id=1, replica_groups=mesh['row'=16,'col'=16] {'col'}, dimensions={0} | all-to-all | bytes 393216 | tf_op jit(solution)/shard_map/all_to_all | solution.py:80
  628.6 10.6 %all_to_all.316 = f32[3,128,128]{2,0,1:T(4,128)S(1)} all-to-all(f32[3,128,128]{2,0,1:T(4,128)S(1)} %copy.434), channel_id=1, replica_groups=mesh['row'=16,'col'=16] {'col'}, dimensions={1} | all-to-all | bytes 393216 | tf_op jit(solution)/shard_map/all_to_all | solution.py:88
  642.5 16.3 %all_to_all.317 = f32[3,128,128]{2,0,1:T(4,128)S(1)} all-to-all(f32[3,128,128]{2,0,1:T(4,128)S(1)} %copy.439), channel_id=1, replica_groups=mesh['row'=16,'col'=16] {'row'}, dimensions={1} | all-to-all | bytes 393216 | tf_op jit(solution)/shard_map/all_to_all | solution.py:95
  662.3 7.9 %multiply_reduce_fusion = (f32[]{:T(128)}, f32[3,8,8,256]{3,2,1,0:T(8,128)}) fusion(f32[3,8,8,256]{3,2,1,0:T(8,128)} %copy-done.19, f32[1,8,8,256]{3,2,1,0:T(8,128)S(1)} %copy-done.22, f32[1,8,8,256]{3,2,1,0:T(8,128)} %copy-done.25, f32[1,8,8,256]{3,2,1,0:T(8,128)} %copy-done.24, f32[]{:T(128)S(6)} %div.37, f32[3,8,256,8]{3,2,1,0:T(8,128)S(1)} %reshape.257), kind=kOutput, calls=%fused_computation.88 | convolution fusion | flops 152272896 | bytes 786440 | tf_op jit(solution)/shard_map/kx,cyxz->cyzk/dot_general | solution.py:96
  670.9 17.6 %all_to_all.318 = f32[256,1,1]{2,1,0:T(1,128)S(1)} all-to-all(f32[256,1,1]{2,1,0:T(1,128)S(1)} %broadcast_in_dim.28), channel_id=1, replica_groups=mesh['row'=16,'col'=16] {'row','col'}, dimensions={0} | all-to-all | bytes 2048 | tf_op jit(solution)/shard_map/all_to_all | solution.py:38
  705.0 22.7 %all_to_all.319 = f32[256,1,1]{2,1,0:T(1,128)S(1)} all-to-all(f32[256,1,1]{2,1,0:T(1,128)S(1)} %broadcast_in_dim.29), channel_id=1, replica_groups=mesh['row'=16,'col'=16] {'row','col'}, dimensions={0} | all-to-all | bytes 2048 | tf_op jit(solution)/shard_map/all_to_all | solution.py:38
  (441 shorter events, 326.3 us)
Async XLA Ops:
  1.5 4.1 collective-permute-start
  4.6 3.4 collective-permute-start.1
  9.2 6.5 collective-permute-start.2
  10.6 6.1 collective-permute-start.3
  30.9 19.6 %all-to-all-start = ((f32[16,1,3072]{2,1,0:T(1,128)}), f32[16,1,3072]{2,1,0:T(1,128)S(1)}, u32[]{:S(2)}, u32[]{:S(2)}) async-start(f32[16,1,3072]{2,1,0:T(1,128)} %reshape.262), calls=%async_computation | async-start | bytes 393216 | tf_op jit(solution)/shard_map/all_to_all | solution.py:73
  78.4 13.6 %all-to-all-start.1 = ((f32[16,1,3072]{2,1,0:T(1,128)}), f32[16,1,3072]{2,1,0:T(1,128)S(1)}, u32[]{:S(2)}, u32[]{:S(2)}) async-start(f32[16,1,3072]{2,1,0:T(1,128)} %reshape.264), calls=%async_computation.1 | async-start | bytes 393216 | tf_op jit(solution)/shard_map/all_to_all | solution.py:80
  141.7 3.4 collective-permute-start.5
  145.1 6.1 collective-permute-start.6
  145.5 5.8 collective-permute-start.7
  178.7 18.9 %all-to-all-start.4 = ((f32[256,1,1]{2,1,0:T(1,128)}), f32[256,1,1]{2,1,0:T(1,128)S(1)}, u32[]{:S(2)}, u32[]{:S(2)}) async-start(f32[256,1,1]{2,1,0:T(1,128)} %broadcast_in_dim.22), calls=%async_computation.4 | async-start | bytes 262144 | tf_op jit(solution)/shard_map/all_to_all | solution.py:38
  334.0 1.9 collective-permute-start.8
  335.0 3.5 collective-permute-start.9
  338.6 6.1 collective-permute-start.10
  339.0 5.7 collective-permute-start.11
  372.4 1.9 collective-permute-start.12
  373.3 3.5 collective-permute-start.13
  376.9 6.1 collective-permute-start.14
  377.3 5.7 collective-permute-start.15
  384.2 2.3 collective-permute-start.16
  385.1 6.0 collective-permute-start.17
  499.5 3.5 collective-permute-start.19
  503.0 6.1 collective-permute-start.20
  503.4 5.8 collective-permute-start.21
  536.7 18.9 %all-to-all-start.16 = ((f32[256,1,1]{2,1,0:T(1,128)}), f32[256,1,1]{2,1,0:T(1,128)S(1)}, u32[]{:S(2)}, u32[]{:S(2)}) async-start(f32[256,1,1]{2,1,0:T(1,128)} %broadcast_in_dim.26), calls=%async_computation.16 | async-start | bytes 262144 | tf_op jit(solution)/shard_map/all_to_all | solution.py:38
  691.6 1.9 collective-permute-start.22
  692.6 3.5 collective-permute-start.23
  696.2 6.1 collective-permute-start.24
  696.6 5.7 collective-permute-start.25
  729.9 1.9 collective-permute-start.26
  730.9 3.5 collective-permute-start.27
  734.5 6.1 collective-permute-start.28
  734.9 5.7 collective-permute-start.29
  (56 other events, 836.9 us)

commit v2 on v1

--- a/solution.py
+++ b/solution.py
@@ -52,6 +52,14 @@
     return jnp.cos(angle) + jnp.sin(angle)
 
 
+def widened(table, pieces):
+    extent = table.shape[0]
+    width = extent // pieces
+    index = jnp.arange(pieces * (width + 2), dtype=jnp.int32)
+    rows = (index // (width + 2)) * width + index % (width + 2) - 1
+    return table[rows % extent]
+
+
 def eigen_row(number, offset_index, extent):
     index = offset_index + jnp.arange(number, dtype=jnp.int32)
     return 2.0 - 2.0 * jnp.cos(2.0 * jnp.pi / extent * index.astype(jnp.float32))
@@ -84,19 +92,23 @@
     mixed_eigen = (yeigen[:, None] + xeigen[None, :]).reshape(-1)
     symbol = normal_factor / (SMOOTHING * (zeigen[:, None] + mixed_eigen[None, :]) + ANCHOR)
     spectrum = jnp.einsum("kz,czm->ckm", ztable, spectrum, precision=PRECISE)
-    spectrum = jnp.einsum("kz,czm->ckm", ztable, spectrum * symbol[None], precision=PRECISE)
+    zwide = widened(ztable, col_count)
+    ywide = widened(ytable, row_count)
+    spectrum = jnp.einsum("kz,czm->ckm", zwide, spectrum * symbol[None], precision=PRECISE)
     spectrum = lax.all_to_all(spectrum, "col", split_axis=1, concat_axis=2, tiled=True)
     spectrum = jnp.einsum(
         "ky,czyx->ckxz",
-        ytable,
-        spectrum.reshape(components, owned_depth_slices, ylength, xpiece),
+        ywide,
+        spectrum.reshape(components, owned_depth_slices + 2, ylength, xpiece),
         precision=PRECISE,
-    ).reshape(components, ylength, xpiece * owned_depth_slices)
+    ).reshape(components, row_count * (owned_height_lines + 2), xpiece * (owned_depth_slices + 2))
     spectrum = lax.all_to_all(spectrum, "row", split_axis=1, concat_axis=2, tiled=True)
     return jnp.einsum(
         "kx,cyxz->cyzk",
         xtable,
-        spectrum.reshape(components, owned_height_lines, period_extent_first, owned_depth_slices),
+        spectrum.reshape(
+            components, owned_height_lines + 2, period_extent_first, owned_depth_slices + 2
+        ),
         precision=PRECISE,
     )
 
@@ -183,35 +195,32 @@
     thermal_lift = RAYLEIGH_NUMBER * (heat_scalar - 0.5)
     zeroes = jnp.zeros_like(thermal_lift)
     forcing = jnp.stack([zeroes, zeroes, thermal_lift])
-    velocity = prior_window_motion
-    pressure = prior_window_stress
     velocity_ext = extended[0:3]
-    pushing = pressure_gradient(extended[3, : owned_height_lines + 1, : owned_depth_slices + 1, :])
-    spread_now = jnp.zeros_like(shear_resistance_map)
+    pressure_low = extended[3, : owned_height_lines + 1, : owned_depth_slices + 1, :]
     for outer_step in range(OUTER):
-        if outer_step > 0:
-            pushing = pressure_gradient(lower_region(pressure))
+        pushing = pressure_gradient(pressure_low)
         residual = forcing - pushing - operate(velocity_ext, shear_resistance_map)
-        direction = residual
-        image = residual
+        direction_ext = None
         energy_now = jnp.float32(1.0)
-        step_size = jnp.float32(1.0)
         for inner_step in range(INNER):
-            precond = precondition(residual, tables)
+            precond_ext = precondition(residual, tables)
+            precond = precond_ext[:, 1 : owned_height_lines + 1, 1 : owned_depth_slices + 1, :]
             energy_next = global_sum(jnp.sum(residual * precond))
             if inner_step == 0:
-                direction = precond
+                direction_ext = precond_ext
             else:
-                direction = precond + energy_next / energy_now * direction
+                direction_ext = precond_ext + energy_next / energy_now * direction_ext
             energy_now = energy_next
-            image = operate(extend(direction), shear_resistance_map)
+            direction = direction_ext[:, 1 : owned_height_lines + 1, 1 : owned_depth_slices + 1, :]
+            image = operate(direction_ext, shear_resistance_map)
             curvature = global_sum(jnp.sum(direction * image))
             step_size = energy_now / curvature
-            velocity = velocity + step_size * direction
+            velocity_ext = velocity_ext + step_size * direction_ext
             residual = residual - step_size * image
-        velocity_ext = extend(velocity)
         spread_now = divergence_region(velocity_ext)
-        pressure = pressure + AUGMENT * spread_now[1:, 1:, :]
+        pressure_low = pressure_low + AUGMENT * spread_now
+    velocity = velocity_ext[:, 1 : owned_height_lines + 1, 1 : owned_depth_slices + 1, :]
+    pressure = pressure_low[1:, 1:, :]
     return (velocity, pressure)
 
 

time: 750 us -> 695 us (0.927)
  blocking collectives: 309 us -> 275 us
  starting transfers between devices: 70 us -> 41.5 us
  waiting for transfers between devices: 78.4 us -> 56.2 us
  local copies, waits for them, and re-layouts: 171 us -> 185 us
  matrix products: 71.2 us -> 82.6 us
    all_to_all x6 -> x5, blocking collectives: 127 us -> 87.8 us  [global_sum(): gathered = lax.all_to_all(spread, ('row', 'col'), 0, 0, tiled=True)]
    ppermute x14 -> x2, starting transfers between devices: 31.9 us -> 4.02 us  [padded(): lax.ppermute(head, axis, [((i + 1) % count, i) for i in range(count)])]
    ppermute x14 -> x2, waiting for transfers between devices: 17.3 us -> 2.26 us  [padded(): lax.ppermute(head, axis, [((i + 1) % count, i) for i in range(count)])]
    ppermute x14 -> x2, waiting for transfers between devices: 14.2 us -> 1.34 us  [padded(): lax.ppermute(tail, axis, [(i, (i + 1) % count) for i in range(count)])]
    all_to_all x2 -> x3, waiting for transfers between devices: 24.6 us -> 37.4 us  [global_sum(): gathered = lax.all_to_all(spread, ('row', 'col'), 0, 0, tiled=True)]
    dot_general x4, matrix products: 27.1 us -> 36.9 us  [precondition(): jnp.einsum('kx,cyxz->cyzk', xtable, spectrum.reshape(components, owned_he...]
    reshape x12 -> x16, local copies, waits for them, and re-layouts: 12 us -> 18.3 us  [the longest x4 14.4 us: precondition(): spectrum.reshape(components, owned_height_lines + 2, period_extent_first,...]
    all_to_all x2 -> x3, starting transfers between devices: 11.4 us -> 17.3 us  [global_sum(): gathered = lax.all_to_all(spread, ('row', 'col'), 0, 0, tiled=True)]
  transfers between devices with their start and end apart: 34 -> 9, of which waited for: 26 -> 7; matrix products, arithmetic and copies ran while one was open for 1% -> 1% of each run, Pallas kernels for 0% -> 0%
where the time goes in v2:
time: 695 us; the launch traced here: 687 us
  blocking collectives  275 us (40%)
  local copies, waits for them, and re-layouts  185 us (27%)
  matrix products  82.6 us (12%)
  waiting for transfers between devices  56.2 us (8%)
  starting transfers between devices  41.5 us (6%)
  other arithmetic  36.4 us (5%)
  between operations  11.3 us (2%)
    all_to_all x5, blocking collectives, global_sum(): gathered = lax.all_to_all(spread, ('row', 'col'), 0, 0, tiled=True)  87.8 us
    unnamed x194, local copies, waits for them, and re-layouts  75.8 us
    all_to_all x4, blocking collectives, precondition(): lax.all_to_all(spectrum, 'row', split_axis=1, concat_axis=2, tiled=True)  70.8 us
    all_to_all x4, blocking collectives, precondition(): lax.all_to_all(spectrum, 'col', split_axis=1, concat_axis=2, tiled=True)  43.9 us
    all_to_all x3, blocking collectives, precondition(): lax.all_to_all(spectrum, 'row', split_axis=2, concat_axis=1, tiled=True)  38.8 us
    all_to_all x3, waiting for transfers between devices, global_sum(): gathered = lax.all_to_all(spread, ('row', 'col'), 0, 0, tiled=True)  37.4 us
    dot_general x4, matrix products, precondition(): jnp.einsum('kx,cyxz->cyzk', xtable, spectrum.reshape(components, owned_he...  36.9 us
    all_to_all x3, blocking collectives, precondition(): lax.all_to_all(spectrum, 'col', split_axis=2, concat_axis=1, tiled=True)  33.3 us
  transfers between devices with their start and end apart: 9, of which 7 were waited for; matrix products, arithmetic and copies ran while one was open for 1% of the time, Pallas kernels for 0%

profile of v2, /device:TPU:1, one launch (start us, length us, event | category | flops | bytes accessed | tf_op | source)
XLA Modules:
  0.0 687.1 jit_solution(4443226051636925020)
XLA Ops:
  30.1 9.5 %all-to-all-start = ((f32[16,1,3072]{2,1,0:T(1,128)}), f32[16,1,3072]{2,1,0:T(1,128)S(1)}, u32[]{:S(2)}, u32[]{:S(2)}) async-start(f32[16,1,3072]{2,1,0:T(1,128)} %reshape.369), calls=%async_computation | async-start | bytes 393216 | tf_op jit(solution)/shard_map/all_to_all | solution.py:81
  42.5 7.3 %all-to-all-done = f32[16,1,3072]{2,1,0:T(1,128)S(1)} async-done(((f32[16,1,3072]{2,1,0:T(1,128)}), f32[16,1,3072]{2,1,0:T(1,128)S(1)}, u32[]{:S(2)}, u32[]{:S(2)}) %all-to-all-start) | async-done | bytes 196640 | tf_op jit(solution)/shard_map/all_to_all | solution.py:81
  62.3 5.9 fusion.8
  77.8 6.5 all-to-all-start.1
  84.4 7.9 %all-to-all-done.1 = f32[16,1,3072]{2,1,0:T(1,128)S(1)} async-done(((f32[16,1,3072]{2,1,0:T(1,128)}), f32[16,1,3072]{2,1,0:T(1,128)S(1)}, u32[]{:S(2)}, u32[]{:S(2)}) %all-to-all-start.1) | async-done | bytes 196640 | tf_op jit(solution)/shard_map/all_to_all | solution.py:88
  102.0 11.1 %all_to_all.300 = f32[3,160,128]{2,0,1:T(4,128)S(1)} all-to-all(f32[3,160,128]{2,0,1:T(4,128)S(1)} %copy.360), channel_id=1, replica_groups=mesh['row'=16,'col'=16] {'col'}, dimensions={1} | all-to-all | bytes 491520 | tf_op jit(solution)/shard_map/all_to_all | solution.py:98
  118.4 17.6 %all_to_all.301 = f32[16,1,4800]{2,1,0:T(1,128)S(1)} all-to-all(f32[16,1,4800]{2,1,0:T(1,128)S(1)} %reshape.373), channel_id=1, replica_groups=mesh['row'=16,'col'=16] {'row'}, dimensions={0} | all-to-all | bytes 614400 | tf_op jit(solution)/shard_map/all_to_all | solution.py:105
  141.6 9.2 %fusion.37 = f32[3,10,10,256]{3,2,1,0:T(8,128)S(1)} fusion(f32[3,10,256,10]{3,2,1,0:T(8,128)} %reshape.336), kind=kOutput, calls=%fused_computation.58 | convolution fusion | flops 236912640 | bytes 614400 | tf_op jit(solution)/shard_map/kx,cyxz->cyzk/dot_general | solution.py:106
  153.7 17.3 %all_to_all.302 = f32[256,1,1]{2,1,0:T(1,128)S(1)} all-to-all(f32[256,1,1]{2,1,0:T(1,128)S(1)} %broadcast_in_dim.22), channel_id=1, replica_groups=mesh['row'=16,'col'=16] {'row','col'}, dimensions={0} | all-to-all | bytes 2048 | tf_op jit(solution)/shard_map/all_to_all | solution.py:38
  179.0 12.2 %all-to-all-done.5 = f32[256,1,1]{2,1,0:T(1,128)S(1)} async-done(((f32[256,1,1]{2,1,0:T(1,128)}), f32[256,1,1]{2,1,0:T(1,128)S(1)}, u32[]{:S(2)}, u32[]{:S(2)}) %all-to-all-start.5) | async-done | bytes 1056 | tf_op jit(solution)/shard_map/all_to_all | solution.py:38
  203.7 12.9 %all_to_all.303 = f32[16,1,3072]{2,1,0:T(1,128)S(1)} all-to-all(f32[16,1,3072]{2,1,0:T(1,128)S(1)} %reshape.375), channel_id=1, replica_groups=mesh['row'=16,'col'=16] {'row'}, dimensions={0} | all-to-all | bytes 393216 | tf_op jit(solution)/shard_map/all_to_all | solution.py:81
  228.7 5.9 fusion.11
  243.5 11.3 %all_to_all.304 = f32[16,1,3072]{2,1,0:T(1,128)S(1)} all-to-all(f32[16,1,3072]{2,1,0:T(1,128)S(1)} %reshape.377), channel_id=1, replica_groups=mesh['row'=16,'col'=16] {'col'}, dimensions={0} | all-to-all | bytes 393216 | tf_op jit(solution)/shard_map/all_to_all | solution.py:88
  264.5 10.7 %all_to_all.305 = f32[3,160,128]{2,0,1:T(4,128)S(1)} all-to-all(f32[3,160,128]{2,0,1:T(4,128)S(1)} %copy.382), channel_id=1, replica_groups=mesh['row'=16,'col'=16] {'col'}, dimensions={1} | all-to-all | bytes 491520 | tf_op jit(solution)/shard_map/all_to_all | solution.py:98
  280.5 17.9 %all_to_all.306 = f32[16,1,4800]{2,1,0:T(1,128)S(1)} all-to-all(f32[16,1,4800]{2,1,0:T(1,128)S(1)} %reshape.379), channel_id=1, replica_groups=mesh['row'=16,'col'=16] {'row'}, dimensions={0} | all-to-all | bytes 614400 | tf_op jit(solution)/shard_map/all_to_all | solution.py:105
  304.1 9.3 %fusion.34 = f32[3,10,10,256]{3,2,1,0:T(8,128)S(1)} fusion(f32[3,10,256,10]{3,2,1,0:T(8,128)} %reshape.342), kind=kOutput, calls=%fused_computation.55 | convolution fusion | flops 236912640 | bytes 614400 | tf_op jit(solution)/shard_map/kx,cyxz->cyzk/dot_general | solution.py:106
  314.9 17.3 %all_to_all.307 = f32[256,1,1]{2,1,0:T(1,128)S(1)} all-to-all(f32[256,1,1]{2,1,0:T(1,128)S(1)} %broadcast_in_dim.24), channel_id=1, replica_groups=mesh['row'=16,'col'=16] {'row','col'}, dimensions={0} | all-to-all | bytes 2048 | tf_op jit(solution)/shard_map/all_to_all | solution.py:38
  343.8 12.9 %all-to-all-done.11 = f32[256,1,1]{2,1,0:T(1,128)S(1)} async-done(((f32[256,1,1]{2,1,0:T(1,128)}), f32[256,1,1]{2,1,0:T(1,128)S(1)}, u32[]{:S(2)}, u32[]{:S(2)}) %all-to-all-start.11) | async-done | bytes 1056 | tf_op jit(solution)/shard_map/all_to_all | solution.py:38
  372.0 13.1 %all_to_all.308 = f32[16,1,3072]{2,1,0:T(1,128)S(1)} all-to-all(f32[16,1,3072]{2,1,0:T(1,128)S(1)} %reshape.381), channel_id=1, replica_groups=mesh['row'=16,'col'=16] {'row'}, dimensions={0} | all-to-all | bytes 393216 | tf_op jit(solution)/shard_map/all_to_all | solution.py:81
  408.3 10.7 %all_to_all.309 = f32[16,1,3072]{2,1,0:T(1,128)S(1)} all-to-all(f32[16,1,3072]{2,1,0:T(1,128)S(1)} %reshape.383), channel_id=1, replica_groups=mesh['row'=16,'col'=16] {'col'}, dimensions={0} | all-to-all | bytes 393216 | tf_op jit(solution)/shard_map/all_to_all | solution.py:88
  428.8 11.3 %all_to_all.310 = f32[3,160,128]{2,0,1:T(4,128)S(1)} all-to-all(f32[3,160,128]{2,0,1:T(4,128)S(1)} %copy.404), channel_id=1, replica_groups=mesh['row'=16,'col'=16] {'col'}, dimensions={1} | all-to-all | bytes 491520 | tf_op jit(solution)/shard_map/all_to_all | solution.py:98
  445.3 17.4 %all_to_all.311 = f32[16,1,4800]{2,1,0:T(1,128)S(1)} all-to-all(f32[16,1,4800]{2,1,0:T(1,128)S(1)} %reshape.385), channel_id=1, replica_groups=mesh['row'=16,'col'=16] {'row'}, dimensions={0} | all-to-all | bytes 614400 | tf_op jit(solution)/shard_map/all_to_all | solution.py:105
  468.4 9.2 %fusion.31 = f32[3,10,10,256]{3,2,1,0:T(8,128)S(1)} fusion(f32[3,10,256,10]{3,2,1,0:T(8,128)} %reshape.348), kind=kOutput, calls=%fused_computation.52 | convolution fusion | flops 236912640 | bytes 614400 | tf_op jit(solution)/shard_map/kx,cyxz->cyzk/dot_general | solution.py:106
  480.3 17.3 %all_to_all.312 = f32[256,1,1]{2,1,0:T(1,128)S(1)} all-to-all(f32[256,1,1]{2,1,0:T(1,128)S(1)} %broadcast_in_dim.26), channel_id=1, replica_groups=mesh['row'=16,'col'=16] {'row','col'}, dimensions={0} | all-to-all | bytes 2048 | tf_op jit(solution)/shard_map/all_to_all | solution.py:38
  505.6 12.3 %all-to-all-done.17 = f32[256,1,1]{2,1,0:T(1,128)S(1)} async-done(((f32[256,1,1]{2,1,0:T(1,128)}), f32[256,1,1]{2,1,0:T(1,128)S(1)}, u32[]{:S(2)}, u32[]{:S(2)}) %all-to-all-start.17) | async-done | bytes 1056 | tf_op jit(solution)/shard_map/all_to_all | solution.py:38
  530.2 12.9 %all_to_all.313 = f32[16,1,3072]{2,1,0:T(1,128)S(1)} all-to-all(f32[16,1,3072]{2,1,0:T(1,128)S(1)} %reshape.387), channel_id=1, replica_groups=mesh['row'=16,'col'=16] {'row'}, dimensions={0} | all-to-all | bytes 393216 | tf_op jit(solution)/shard_map/all_to_all | solution.py:81
  570.0 11.3 %all_to_all.314 = f32[16,1,3072]{2,1,0:T(1,128)S(1)} all-to-all(f32[16,1,3072]{2,1,0:T(1,128)S(1)} %reshape.389), channel_id=1, replica_groups=mesh['row'=16,'col'=16] {'col'}, dimensions={0} | all-to-all | bytes 393216 | tf_op jit(solution)/shard_map/all_to_all | solution.py:88
  591.0 10.7 %all_to_all.315 = f32[3,160,128]{2,0,1:T(4,128)S(1)} all-to-all(f32[3,160,128]{2,0,1:T(4,128)S(1)} %copy.426), channel_id=1, replica_groups=mesh['row'=16,'col'=16] {'col'}, dimensions={1} | all-to-all | bytes 491520 | tf_op jit(solution)/shard_map/all_to_all | solution.py:98
  606.9 17.8 %all_to_all.316 = f32[16,1,4800]{2,1,0:T(1,128)S(1)} all-to-all(f32[16,1,4800]{2,1,0:T(1,128)S(1)} %reshape.391), channel_id=1, replica_groups=mesh['row'=16,'col'=16] {'row'}, dimensions={0} | all-to-all | bytes 614400 | tf_op jit(solution)/shard_map/all_to_all | solution.py:105
  630.4 9.3 %fusion.28 = f32[3,10,10,256]{3,2,1,0:T(8,128)S(1)} fusion(f32[3,10,256,10]{3,2,1,0:T(8,128)} %reshape.354), kind=kOutput, calls=%fused_computation.49 | convolution fusion | flops 236912640 | bytes 614400 | tf_op jit(solution)/shard_map/kx,cyxz->cyzk/dot_general | solution.py:106
  641.1 17.3 %all_to_all.317 = f32[256,1,1]{2,1,0:T(1,128)S(1)} all-to-all(f32[256,1,1]{2,1,0:T(1,128)S(1)} %broadcast_in_dim.28), channel_id=1, replica_groups=mesh['row'=16,'col'=16] {'row','col'}, dimensions={0} | all-to-all | bytes 2048 | tf_op jit(solution)/shard_map/all_to_all | solution.py:38
  663.3 18.4 %all_to_all.318 = f32[256,1,1]{2,1,0:T(1,128)S(1)} all-to-all(f32[256,1,1]{2,1,0:T(1,128)S(1)} %broadcast_in_dim.29), channel_id=1, replica_groups=mesh['row'=16,'col'=16] {'row','col'}, dimensions={0} | all-to-all | bytes 2048 | tf_op jit(solution)/shard_map/all_to_all | solution.py:38
  (448 shorter events, 284.0 us)
Async XLA Ops:
  0.6 17.3 %copy-start.11 = (f32[8,8,256]{2,1,0:T(8,128)S(1)}, f32[8,8,256]{2,1,0:T(8,128)}, u32[]{:S(2)}) copy-start(f32[8,8,256]{2,1,0:T(8,128)} %param.4) | copy-start | bytes 196612
  0.6 17.3 %copy-start.10 = (f32[8,8,256]{2,1,0:T(8,128)S(1)}, f32[8,8,256]{2,1,0:T(8,128)}, u32[]{:S(2)}) copy-start(f32[8,8,256]{2,1,0:T(8,128)} %param.5) | copy-start | bytes 196612
  0.7 17.3 %copy-start = (f32[3,8,8,256]{3,2,1,0:T(8,128)S(1)}, f32[3,8,8,256]{3,2,1,0:T(8,128)}, u32[]{:S(2)}) copy-start(f32[3,8,8,256]{3,2,1,0:T(8,128)} %param.3) | copy-start | bytes 589828
  1.5 4.2 collective-permute-start
  4.6 3.4 collective-permute-start.1
  5.6 13.5 %copy-start.13 = (f32[1,8,8,256]{3,2,1,0:T(8,128)}, f32[1,8,8,256]{3,2,1,0:T(8,128)S(1)}, u32[]{:S(2)}) copy-start(f32[1,8,8,256]{3,2,1,0:T(8,128)S(1)} %add_bitcast_fusion) | copy-start | bytes 196612
  5.7 12.9 %copy-start.23 = (f32[5,1,8,256]{3,2,1,0:T(8,128)}, f32[5,1,8,256]{3,2,1,0:T(8,128)S(1)}, u32[]{:S(2)}) copy-start(f32[5,1,8,256]{3,2,1,0:T(8,128)S(1)} %collective-permute-done) | copy-start | bytes 122884
  8.0 10.6 %copy-start.25 = (f32[5,1,8,256]{3,2,1,0:T(8,128)}, f32[5,1,8,256]{3,2,1,0:T(8,128)S(1)}, u32[]{:S(2)}) copy-start(f32[5,1,8,256]{3,2,1,0:T(8,128)S(1)} %collective-permute-done.1) | copy-start | bytes 122884
  9.2 6.5 collective-permute-start.2
  10.5 5.2 collective-permute-start.3
  19.1 11.0 %copy-start.41 = (f32[1,8,8,256]{3,2,1,0:T(8,128)}, f32[1,8,8,256]{3,2,1,0:T(8,128)S(1)}, u32[]{:S(2)}) copy-start(f32[1,8,8,256]{3,2,1,0:T(8,128)S(1)} %get-tuple-element.61) | copy-start | bytes 196612
  19.1 11.0 %copy-start.44 = (f32[1,8,8,256]{3,2,1,0:T(8,128)}, f32[1,8,8,256]{3,2,1,0:T(8,128)S(1)}, u32[]{:S(2)}) copy-start(f32[1,8,8,256]{3,2,1,0:T(8,128)S(1)} %get-tuple-element.62) | copy-start | bytes 196612
  19.2 10.9 %copy-start.79 = (f32[3,8,8,256]{3,2,1,0:T(8,128)}, f32[3,8,8,256]{3,2,1,0:T(8,128)S(1)}, u32[]{:S(2)}) copy-start(f32[3,8,8,256]{3,2,1,0:T(8,128)S(1)} %fusion.43) | copy-start | bytes 589828
  30.1 19.6 %all-to-all-start = ((f32[16,1,3072]{2,1,0:T(1,128)}), f32[16,1,3072]{2,1,0:T(1,128)S(1)}, u32[]{:S(2)}, u32[]{:S(2)}) async-start(f32[16,1,3072]{2,1,0:T(1,128)} %reshape.369), calls=%async_computation | async-start | bytes 393216 | tf_op jit(solution)/shard_map/all_to_all | solution.py:81
  72.7 11.5 %copy-start.83 = (f32[128]{0:T(128)S(1)}, f32[128]{0:T(128)}, u32[]{:S(2)}) copy-start(f32[128]{0:T(128)} %add.589) | copy-start | bytes 1540
  72.7 11.5 %copy-start.84 = (f32[128]{0:T(128)S(1)}, f32[128]{0:T(128)}, u32[]{:S(2)}) copy-start(f32[128]{0:T(128)} %multiply_subtract_fusion.6) | copy-start | bytes 1540
  77.8 14.5 %all-to-all-start.1 = ((f32[16,1,3072]{2,1,0:T(1,128)}), f32[16,1,3072]{2,1,0:T(1,128)S(1)}, u32[]{:S(2)}, u32[]{:S(2)}) async-start(f32[16,1,3072]{2,1,0:T(1,128)} %reshape.371), calls=%async_computation.1 | async-start | bytes 393216 | tf_op jit(solution)/shard_map/all_to_all | solution.py:88
  84.4 16.4 %copy-start.20 = (f32[128,128]{0,1:T(8,128)}, f32[128,128]{0,1:T(8,128)S(1)}, u32[]{:S(2)}) copy-start(f32[128,128]{0,1:T(8,128)S(1)} %add_divide_fusion) | copy-start | bytes 196612
  151.5 42.0 %copy-start.80 = (f32[3,8,8,256]{3,2,1,0:T(8,128)S(1)}, f32[3,8,8,256]{3,2,1,0:T(8,128)}, u32[]{:S(2)}) copy-start(f32[3,8,8,256]{3,2,1,0:T(8,128)} %copy-done.79) | copy-start | bytes 589828
  152.0 47.3 %copy-start.67 = (f32[1,8,8,256]{3,2,1,0:T(8,128)}, f32[1,8,8,256]{3,2,1,0:T(8,128)S(1)}, u32[]{:S(2)}) copy-start(f32[1,8,8,256]{3,2,1,0:T(8,128)S(1)} %fusion.174) | copy-start | bytes 196612
  152.1 47.2 %copy-start.73 = (f32[1,8,8,256]{3,2,1,0:T(8,128)}, f32[1,8,8,256]{3,2,1,0:T(8,128)S(1)}, u32[]{:S(2)}) copy-start(f32[1,8,8,256]{3,2,1,0:T(8,128)S(1)} %get-tuple-element.27) | copy-start | bytes 196612
  152.1 47.2 %copy-start.75 = (f32[1,8,8,256]{3,2,1,0:T(8,128)}, f32[1,8,8,256]{3,2,1,0:T(8,128)S(1)}, u32[]{:S(2)}) copy-start(f32[1,8,8,256]{3,2,1,0:T(8,128)S(1)} %get-tuple-element.28) | copy-start | bytes 196612
  172.4 18.9 %all-to-all-start.5 = ((f32[256,1,1]{2,1,0:T(1,128)}), f32[256,1,1]{2,1,0:T(1,128)S(1)}, u32[]{:S(2)}, u32[]{:S(2)}) async-start(f32[256,1,1]{2,1,0:T(1,128)} %broadcast_in_dim.23), calls=%async_computation.5 | async-start | bytes 262144 | tf_op jit(solution)/shard_map/all_to_all | solution.py:38
  304.1 30.3 %copy-start.2 = (f32[3,10,10,256]{3,2,1,0:T(8,128)S(1)}, f32[3,10,10,256]{3,2,1,0:T(8,128)}, u32[]{:S(2)}) copy-start(f32[3,10,10,256]{3,2,1,0:T(8,128)} %copy-done.1) | copy-start | bytes 921604
  337.8 18.9 %all-to-all-start.11 = ((f32[256,1,1]{2,1,0:T(1,128)}), f32[256,1,1]{2,1,0:T(1,128)S(1)}, u32[]{:S(2)}, u32[]{:S(2)}) async-start(f32[256,1,1]{2,1,0:T(1,128)} %broadcast_in_dim.25), calls=%async_computation.11 | async-start | bytes 262144 | tf_op jit(solution)/shard_map/all_to_all | solution.py:38
  478.2 41.8 %copy-start.82 = (f32[3,8,8,256]{3,2,1,0:T(8,128)S(1)}, f32[3,8,8,256]{3,2,1,0:T(8,128)}, u32[]{:S(2)}) copy-start(f32[3,8,8,256]{3,2,1,0:T(8,128)} %copy-done.81) | copy-start | bytes 589828
  478.7 47.1 %copy-start.65 = (f32[1,8,8,256]{3,2,1,0:T(8,128)}, f32[1,8,8,256]{3,2,1,0:T(8,128)S(1)}, u32[]{:S(2)}) copy-start(f32[1,8,8,256]{3,2,1,0:T(8,128)S(1)} %fusion.125) | copy-start | bytes 196612
  478.8 47.0 %copy-start.69 = (f32[1,8,8,256]{3,2,1,0:T(8,128)}, f32[1,8,8,256]{3,2,1,0:T(8,128)S(1)}, u32[]{:S(2)}) copy-start(f32[1,8,8,256]{3,2,1,0:T(8,128)S(1)} %get-tuple-element.21) | copy-start | bytes 196612
  478.8 47.0 %copy-start.71 = (f32[1,8,8,256]{3,2,1,0:T(8,128)}, f32[1,8,8,256]{3,2,1,0:T(8,128)S(1)}, u32[]{:S(2)}) copy-start(f32[1,8,8,256]{3,2,1,0:T(8,128)S(1)} %get-tuple-element.22) | copy-start | bytes 196612
  499.0 18.9 %all-to-all-start.17 = ((f32[256,1,1]{2,1,0:T(1,128)}), f32[256,1,1]{2,1,0:T(1,128)S(1)}, u32[]{:S(2)}, u32[]{:S(2)}) async-start(f32[256,1,1]{2,1,0:T(1,128)} %broadcast_in_dim.27), calls=%async_computation.17 | async-start | bytes 262144 | tf_op jit(solution)/shard_map/all_to_all | solution.py:38
  630.4 30.3 %copy-start.4 = (f32[3,10,10,256]{3,2,1,0:T(8,128)S(1)}, f32[3,10,10,256]{3,2,1,0:T(8,128)}, u32[]{:S(2)}) copy-start(f32[3,10,10,256]{3,2,1,0:T(8,128)} %copy-done.3) | copy-start | bytes 921604
  661.2 22.8 %copy-start.9 = (f32[3,10,10,256]{3,2,1,0:T(8,128)S(1)}, f32[3,10,10,256]{3,2,1,0:T(8,128)}, u32[]{:S(2)}) copy-start(f32[3,10,10,256]{3,2,1,0:T(8,128)} %copy-done.8) | copy-start | bytes 921604
  (62 other events, 299.2 us)

commit v3 on v2

--- a/solution.py
+++ b/solution.py
@@ -65,44 +65,71 @@
     return 2.0 - 2.0 * jnp.cos(2.0 * jnp.pi / extent * index.astype(jnp.float32))
 
 
-def precondition(residual, tables):
-    xtable, ytable, ztable = tables
+def exchange(cells, partial, axis, split_axis, concat_axis):
+    count = lax.axis_size(axis)
+    rider = jnp.broadcast_to(partial.astype(cells.dtype), (1,) + cells.shape[1:])
+    moved = lax.all_to_all(
+        jnp.concatenate([cells, rider], 0), axis, split_axis, concat_axis, tiled=True
+    )
+    arrived = jnp.moveaxis(moved[-1], concat_axis - 1, 0)
+    arrived = arrived.reshape(count, arrived.shape[0] // count, -1)[:, 0, 0]
+    return moved[:-1], jnp.sum(arrived)
+
+
+def spectral_symbol(shape):
     row_count = lax.axis_size("row")
     col_count = lax.axis_size("col")
-    components, owned_height_lines, owned_depth_slices, period_extent_first = residual.shape
+    components, owned_height_lines, owned_depth_slices, period_extent_first = shape
     ylength = owned_height_lines * row_count
     zlength = owned_depth_slices * col_count
     normal_factor = 1.0 / (period_extent_first * ylength * zlength)
     xpiece = period_extent_first // row_count
     ypiece = ylength // col_count
+    zeigen = eigen_row(zlength, 0, zlength)
+    yeigen = eigen_row(ypiece, lax.axis_index("col") * ypiece, ylength)
+    xeigen = eigen_row(xpiece, lax.axis_index("row") * xpiece, period_extent_first)
+    mixed_eigen = (yeigen[:, None] + xeigen[None, :]).reshape(-1)
+    return normal_factor / (SMOOTHING * (zeigen[:, None] + mixed_eigen[None, :]) + ANCHOR)
+
+
+def transform_forward(residual, tables, partial):
+    xtable, ytable, ztable = tables
+    row_count = lax.axis_size("row")
+    components, owned_height_lines, owned_depth_slices, period_extent_first = residual.shape
+    ylength = owned_height_lines * row_count
+    xpiece = period_extent_first // row_count
     spectrum = jnp.einsum("kx,cyzx->cykz", xtable, residual, precision=PRECISE).reshape(
         components, owned_height_lines, period_extent_first * owned_depth_slices
     )
-    spectrum = lax.all_to_all(spectrum, "row", split_axis=2, concat_axis=1, tiled=True)
+    spectrum, partial = exchange(spectrum, partial, "row", 2, 1)
     spectrum = jnp.einsum(
         "ky,cyxz->czkx",
         ytable,
         spectrum.reshape(components, ylength, xpiece, owned_depth_slices),
         precision=PRECISE,
     ).reshape(components, owned_depth_slices, ylength * xpiece)
-    spectrum = lax.all_to_all(spectrum, "col", split_axis=2, concat_axis=1, tiled=True)
-    zeigen = eigen_row(zlength, 0, zlength)
-    yeigen = eigen_row(ypiece, lax.axis_index("col") * ypiece, ylength)
-    xeigen = eigen_row(xpiece, lax.axis_index("row") * xpiece, period_extent_first)
-    mixed_eigen = (yeigen[:, None] + xeigen[None, :]).reshape(-1)
-    symbol = normal_factor / (SMOOTHING * (zeigen[:, None] + mixed_eigen[None, :]) + ANCHOR)
-    spectrum = jnp.einsum("kz,czm->ckm", ztable, spectrum, precision=PRECISE)
+    spectrum, partial = exchange(spectrum, partial, "col", 2, 1)
+    return jnp.einsum("kz,czm->ckm", ztable, spectrum, precision=PRECISE), partial
+
+
+def transform_inverse(filtered, tables, partial, shape):
+    xtable, ytable, ztable = tables
+    row_count = lax.axis_size("row")
+    col_count = lax.axis_size("col")
+    components, owned_height_lines, owned_depth_slices, period_extent_first = shape
+    ylength = owned_height_lines * row_count
+    xpiece = period_extent_first // row_count
     zwide = widened(ztable, col_count)
     ywide = widened(ytable, row_count)
-    spectrum = jnp.einsum("kz,czm->ckm", zwide, spectrum * symbol[None], precision=PRECISE)
-    spectrum = lax.all_to_all(spectrum, "col", split_axis=1, concat_axis=2, tiled=True)
+    spectrum = jnp.einsum("kz,czm->ckm", zwide, filtered, precision=PRECISE)
+    spectrum, partial = exchange(spectrum, partial, "col", 1, 2)
     spectrum = jnp.einsum(
         "ky,czyx->ckxz",
         ywide,
         spectrum.reshape(components, owned_depth_slices + 2, ylength, xpiece),
         precision=PRECISE,
     ).reshape(components, row_count * (owned_height_lines + 2), xpiece * (owned_depth_slices + 2))
-    spectrum = lax.all_to_all(spectrum, "row", split_axis=1, concat_axis=2, tiled=True)
+    spectrum, partial = exchange(spectrum, partial, "row", 1, 2)
     return jnp.einsum(
         "kx,cyxz->cyzk",
         xtable,
@@ -110,7 +137,7 @@
             components, owned_height_lines + 2, period_extent_first, owned_depth_slices + 2
         ),
         precision=PRECISE,
-    )
+    ), partial
 
 
 def forward(extended, direction):
@@ -197,26 +224,33 @@
     forcing = jnp.stack([zeroes, zeroes, thermal_lift])
     velocity_ext = extended[0:3]
     pressure_low = extended[3, : owned_height_lines + 1, : owned_depth_slices + 1, :]
+    symbol = spectral_symbol(prior_window_motion.shape)
+    inner_cells = (slice(None), slice(1, owned_height_lines + 1), slice(1, owned_depth_slices + 1))
     for outer_step in range(OUTER):
         pushing = pressure_gradient(pressure_low)
         residual = forcing - pushing - operate(velocity_ext, shear_resistance_map)
+        spectrum, _ = transform_forward(residual, tables, jnp.float32(0.0))
         direction_ext = None
         energy_now = jnp.float32(1.0)
         for inner_step in range(INNER):
-            precond_ext = precondition(residual, tables)
-            precond = precond_ext[:, 1 : owned_height_lines + 1, 1 : owned_depth_slices + 1, :]
-            energy_next = global_sum(jnp.sum(residual * precond))
+            if inner_step > 0:
+                image_spectrum, curvature = transform_forward(image, tables, curvature_part)
+                step_size = energy_now / curvature
+                velocity_ext = velocity_ext + step_size * direction_ext
+                spectrum = spectrum - step_size * image_spectrum
+            filtered = spectrum * symbol[None]
+            precond_ext, energy_next = transform_inverse(
+                filtered, tables, jnp.sum(spectrum * filtered), prior_window_motion.shape
+            )
             if inner_step == 0:
                 direction_ext = precond_ext
             else:
                 direction_ext = precond_ext + energy_next / energy_now * direction_ext
             energy_now = energy_next
-            direction = direction_ext[:, 1 : owned_height_lines + 1, 1 : owned_depth_slices + 1, :]
             image = operate(direction_ext, shear_resistance_map)
-            curvature = global_sum(jnp.sum(direction * image))
-            step_size = energy_now / curvature
-            velocity_ext = velocity_ext + step_size * direction_ext
-            residual = residual - step_size * image
+            curvature_part = jnp.sum(direction_ext[inner_cells] * image)
+        step_size = energy_now / global_sum(curvature_part)
+        velocity_ext = velocity_ext + step_size * direction_ext
         spread_now = divergence_region(velocity_ext)
         pressure_low = pressure_low + AUGMENT * spread_now
     velocity = velocity_ext[:, 1 : owned_height_lines + 1, 1 : owned_depth_slices + 1, :]

time: 695 us -> 676 us (0.973)
  local copies, waits for them, and re-layouts: 185 us -> 253 us
  blocking collectives: 275 us -> 217 us
  matrix products: 82.6 us -> 67.3 us
  waiting for transfers between devices: 56.2 us -> 46.3 us
    unnamed x194 -> x108, local copies, waits for them, and re-layouts: 75.8 us -> 176 us
    all_to_all x5 -> x1, blocking collectives: 87.8 us -> 17.5 us  [global_sum(): gathered = lax.all_to_all(spread, ('row', 'col'), 0, 0, tiled=True)]
    reshape x28, local copies, waits for them, and re-layouts: 62.1 us -> 32.6 us  [the longest x8 15.3 us: transform_forward(): spectrum.reshape(components, ylength, xpiece, owned_depth_slices)]
    all_to_all x3 -> x1, waiting for transfers between devices: 37.4 us -> 12.4 us  [global_sum(): gathered = lax.all_to_all(spread, ('row', 'col'), 0, 0, tiled=True)]
    dot_general x24, matrix products: 82.6 us -> 67.3 us  [the longest x4 36.7 us: transform_inverse(): jnp.einsum('kx,cyxz->cyzk', xtable, spectrum.reshape(components, owned_he...]
    all_to_all x2 -> x4, waiting for transfers between devices: 15.1 us -> 30.1 us  [exchange(): lax.all_to_all(jnp.concatenate([cells, rider], 0), axis, split_axis, conc...]
    all_to_all x14 -> x12, blocking collectives: 187 us -> 199 us  [exchange(): lax.all_to_all(jnp.concatenate([cells, rider], 0), axis, split_axis, conc...]
    all_to_all x3 -> x1, starting transfers between devices: 17.3 us -> 5.49 us  [global_sum(): gathered = lax.all_to_all(spread, ('row', 'col'), 0, 0, tiled=True)]
where the time goes in v3:
time: 676 us; the launch traced here: 668 us
  local copies, waits for them, and re-layouts  253 us (37%)
  blocking collectives  217 us (32%)
  matrix products  67.3 us (10%)
  waiting for transfers between devices  46.3 us (7%)
  starting transfers between devices  37.4 us (6%)
  other arithmetic  36.1 us (5%)
  between operations  10.8 us (2%)
    all_to_all x12, blocking collectives, exchange(): lax.all_to_all(jnp.concatenate([cells, rider], 0), axis, split_axis, conc...  199 us
    unnamed x108, local copies, waits for them, and re-layouts  176 us
    dot_general x4, matrix products, transform_inverse(): jnp.einsum('kx,cyxz->cyzk', xtable, spectrum.reshape(components, owned_he...  36.7 us
    all_to_all x4, waiting for transfers between devices, exchange(): lax.all_to_all(jnp.concatenate([cells, rider], 0), axis, split_axis, conc...  30.1 us
    all_to_all x4, starting transfers between devices, exchange(): lax.all_to_all(jnp.concatenate([cells, rider], 0), axis, split_axis, conc...  23.6 us
    all_to_all x9, local copies, waits for them, and re-layouts, exchange(): lax.all_to_all(jnp.concatenate([cells, rider], 0), axis, split_axis, conc...  22.9 us
    all_to_all x1, blocking collectives, global_sum(): gathered = lax.all_to_all(spread, ('row', 'col'), 0, 0, tiled=True)  17.5 us
    reshape x8, local copies, waits for them, and re-layouts, transform_forward(): spectrum.reshape(components, ylength, xpiece, owned_depth_slices)  15.3 us
  transfers between devices with their start and end apart: 9, of which 7 were waited for; matrix products, arithmetic and copies ran while one was open for 1% of the time, Pallas kernels for 0%

profile of v3, /device:TPU:1, one launch (start us, length us, event | category | flops | bytes accessed | tf_op | source)
XLA Modules:
  0.0 668.2 jit_solution(4534854033456943694)
XLA Ops:
  29.7 7.1 %reshape.425 = f32[16,1,4096]{2,1,0:T(1,128)} reshape(f32[2048,4,8]{2,1,0:T(4,128)} %pad_bitcast_fusion.7) | data formatting | bytes 524288
  36.9 9.6 %all-to-all-start = ((f32[16,1,4096]{2,1,0:T(1,128)}), f32[16,1,4096]{2,1,0:T(1,128)S(1)}, u32[]{:S(2)}, u32[]{:S(2)}) async-start(f32[16,1,4096]{2,1,0:T(1,128)} %reshape.425), calls=%async_computation | async-start | bytes 524288 | tf_op jit(solution)/shard_map/all_to_all | solution.py:71
  48.0 9.9 %all-to-all-done = f32[16,1,4096]{2,1,0:T(1,128)S(1)} async-done(((f32[16,1,4096]{2,1,0:T(1,128)}), f32[16,1,4096]{2,1,0:T(1,128)S(1)}, u32[]{:S(2)}, u32[]{:S(2)}) %all-to-all-start) | async-done | bytes 262176 | tf_op jit(solution)/shard_map/all_to_all | solution.py:71
  83.8 7.1 %reshape.427 = f32[16,1,4096]{2,1,0:T(1,128)} reshape(f32[2048,4,8]{2,1,0:T(4,128)} %pad_bitcast_fusion.6) | data formatting | bytes 524288
  98.1 7.5 %all-to-all-done.1 = f32[16,1,4096]{2,1,0:T(1,128)S(1)} async-done(((f32[16,1,4096]{2,1,0:T(1,128)}), f32[16,1,4096]{2,1,0:T(1,128)S(1)}, u32[]{:S(2)}, u32[]{:S(2)}) %all-to-all-start.1) | async-done | bytes 262176 | tf_op jit(solution)/shard_map/all_to_all | solution.py:71
  106.9 6.3 reshape.428
  119.5 11.1 %all_to_all.252 = f32[4,160,128]{2,0,1:T(4,128)S(1)} all-to-all(f32[4,160,128]{2,0,1:T(4,128)S(1)} %concatenate.194.clone), channel_id=1, replica_groups=mesh['row'=16,'col'=16] {'col'}, dimensions={1} | all-to-all | bytes 655360 | tf_op jit(solution)/shard_map/all_to_all | solution.py:71
  136.8 25.0 %all_to_all.253 = f32[4,160,160]{2,0,1:T(4,128)S(1)} all-to-all(f32[4,160,160]{2,0,1:T(4,128)S(1)} %concatenate.195.clone), channel_id=1, replica_groups=mesh['row'=16,'col'=16] {'row'}, dimensions={1} | all-to-all | bytes 819200 | tf_op jit(solution)/shard_map/all_to_all | solution.py:71
  166.4 9.2 %fusion.19 = f32[3,10,10,256]{3,2,1,0:T(8,128)S(1)} fusion(f32[3,10,256,10]{3,2,1,0:T(8,128)} %reshape.382), kind=kOutput, calls=%fused_computation.52 | convolution fusion | flops 236912640 | bytes 614400 | tf_op jit(solution)/shard_map/kx,cyxz->cyzk/dot_general | solution.py:133
  187.9 6.5 reshape.429
  194.4 14.0 %all_to_all.254 = f32[16,1,4096]{2,1,0:T(1,128)S(1)} all-to-all(f32[16,1,4096]{2,1,0:T(1,128)S(1)} %reshape.429), channel_id=1, replica_groups=mesh['row'=16,'col'=16] {'row'}, dimensions={0} | all-to-all | bytes 524288 | tf_op jit(solution)/shard_map/all_to_all | solution.py:71
  233.8 7.1 %reshape.431 = f32[16,1,4096]{2,1,0:T(1,128)} reshape(f32[2048,4,8]{2,1,0:T(4,128)} %pad_bitcast_fusion.4) | data formatting | bytes 524288
  247.0 6.4 all-to-all-done.5
  268.4 11.1 %all_to_all.255 = f32[4,160,128]{2,0,1:T(4,128)S(1)} all-to-all(f32[4,160,128]{2,0,1:T(4,128)S(1)} %concatenate.204.clone), channel_id=1, replica_groups=mesh['row'=16,'col'=16] {'col'}, dimensions={1} | all-to-all | bytes 655360 | tf_op jit(solution)/shard_map/all_to_all | solution.py:71
  285.6 25.1 %all_to_all.256 = f32[4,160,160]{2,0,1:T(4,128)S(1)} all-to-all(f32[4,160,160]{2,0,1:T(4,128)S(1)} %concatenate.205.clone), channel_id=1, replica_groups=mesh['row'=16,'col'=16] {'row'}, dimensions={1} | all-to-all | bytes 819200 | tf_op jit(solution)/shard_map/all_to_all | solution.py:71
  316.9 9.2 %convolution_add_fusion.1 = f32[3,10,10,256]{3,2,1,0:T(8,128)S(1)} fusion(f32[3,10,256,10]{3,2,1,0:T(8,128)} %reshape.390, f32[3,10,10,256]{3,2,1,0:T(8,128)S(1)} %copy-done.2, f32[]{:T(128)S(6)} %div.64), kind=kOutput, calls=%fused_computation.6 | convolution fusion | flops 237066240 | bytes 921604 | tf_op jit(solution)/shard_map/kx,cyxz->cyzk/dot_general | solution.py:133
  335.0 12.4 %all-to-all-done.8 = f32[256,1,1]{2,1,0:T(1,128)S(1)} async-done(((f32[256,1,1]{2,1,0:T(1,128)}), f32[256,1,1]{2,1,0:T(1,128)S(1)}, u32[]{:S(2)}, u32[]{:S(2)}) %all-to-all-start.8) | async-done | bytes 1056 | tf_op jit(solution)/shard_map/all_to_all | solution.py:38
  361.0 6.5 reshape.433
  367.5 14.8 %all_to_all.257 = f32[16,1,4096]{2,1,0:T(1,128)S(1)} all-to-all(f32[16,1,4096]{2,1,0:T(1,128)S(1)} %reshape.433), channel_id=1, replica_groups=mesh['row'=16,'col'=16] {'row'}, dimensions={0} | all-to-all | bytes 524288 | tf_op jit(solution)/shard_map/all_to_all | solution.py:71
  404.6 6.5 reshape.435
  411.1 11.9 %all_to_all.258 = f32[16,1,4096]{2,1,0:T(1,128)S(1)} all-to-all(f32[16,1,4096]{2,1,0:T(1,128)S(1)} %reshape.435), channel_id=1, replica_groups=mesh['row'=16,'col'=16] {'col'}, dimensions={0} | all-to-all | bytes 524288 | tf_op jit(solution)/shard_map/all_to_all | solution.py:71
  436.7 11.1 %all_to_all.259 = f32[4,160,128]{2,0,1:T(4,128)S(1)} all-to-all(f32[4,160,128]{2,0,1:T(4,128)S(1)} %concatenate.221.clone), channel_id=1, replica_groups=mesh['row'=16,'col'=16] {'col'}, dimensions={1} | all-to-all | bytes 655360 | tf_op jit(solution)/shard_map/all_to_all | solution.py:71
  453.8 25.0 %all_to_all.260 = f32[4,160,160]{2,0,1:T(4,128)S(1)} all-to-all(f32[4,160,160]{2,0,1:T(4,128)S(1)} %concatenate.222.clone), channel_id=1, replica_groups=mesh['row'=16,'col'=16] {'row'}, dimensions={1} | all-to-all | bytes 819200 | tf_op jit(solution)/shard_map/all_to_all | solution.py:71
  483.5 9.2 %fusion.14 = f32[3,10,10,256]{3,2,1,0:T(8,128)S(1)} fusion(f32[3,10,256,10]{3,2,1,0:T(8,128)} %reshape.398), kind=kOutput, calls=%fused_computation.47 | convolution fusion | flops 236912640 | bytes 614400 | tf_op jit(solution)/shard_map/kx,cyxz->cyzk/dot_general | solution.py:133
  504.9 6.5 reshape.437
  511.4 14.0 %all_to_all.261 = f32[16,1,4096]{2,1,0:T(1,128)S(1)} all-to-all(f32[16,1,4096]{2,1,0:T(1,128)S(1)} %reshape.437), channel_id=1, replica_groups=mesh['row'=16,'col'=16] {'row'}, dimensions={0} | all-to-all | bytes 524288 | tf_op jit(solution)/shard_map/all_to_all | solution.py:71
  550.6 7.1 %reshape.439 = f32[16,1,4096]{2,1,0:T(1,128)} reshape(f32[2048,4,8]{2,1,0:T(4,128)} %pad_bitcast_fusion) | data formatting | bytes 524288
  563.9 6.4 all-to-all-done.14
  585.3 11.1 %all_to_all.262 = f32[4,160,128]{2,0,1:T(4,128)S(1)} all-to-all(f32[4,160,128]{2,0,1:T(4,128)S(1)} %concatenate.231.clone), channel_id=1, replica_groups=mesh['row'=16,'col'=16] {'col'}, dimensions={1} | all-to-all | bytes 655360 | tf_op jit(solution)/shard_map/all_to_all | solution.py:71
  602.5 25.1 %all_to_all.263 = f32[4,160,160]{2,0,1:T(4,128)S(1)} all-to-all(f32[4,160,160]{2,0,1:T(4,128)S(1)} %concatenate.232.clone), channel_id=1, replica_groups=mesh['row'=16,'col'=16] {'row'}, dimensions={1} | all-to-all | bytes 819200 | tf_op jit(solution)/shard_map/all_to_all | solution.py:71
  633.8 9.2 %convolution_add_fusion = f32[3,10,10,256]{3,2,1,0:T(8,128)S(1)} fusion(f32[3,10,256,10]{3,2,1,0:T(8,128)} %reshape.406, f32[3,10,10,256]{3,2,1,0:T(8,128)S(1)} %copy-done.4, f32[]{:T(128)S(6)} %div.67), kind=kOutput, calls=%fused_computation.5 | convolution fusion | flops 237066240 | bytes 921604 | tf_op jit(solution)/shard_map/kx,cyxz->cyzk/dot_general | solution.py:133
  645.5 17.5 %all_to_all.264 = f32[256,1,1]{2,1,0:T(1,128)S(1)} all-to-all(f32[256,1,1]{2,1,0:T(1,128)S(1)} %broadcast_in_dim.11), channel_id=1, replica_groups=mesh['row'=16,'col'=16] {'row','col'}, dimensions={0} | all-to-all | bytes 2048 | tf_op jit(solution)/shard_map/all_to_all | solution.py:38
  (386 shorter events, 290.7 us)
Async XLA Ops:
  0.6 18.3 %copy-start = (f32[3,8,8,256]{3,2,1,0:T(8,128)S(1)}, f32[3,8,8,256]{3,2,1,0:T(8,128)}, u32[]{:S(2)}) copy-start(f32[3,8,8,256]{3,2,1,0:T(8,128)} %param.3) | copy-start | bytes 589828
  0.6 18.3 %copy-start.10 = (f32[8,8,256]{2,1,0:T(8,128)S(1)}, f32[8,8,256]{2,1,0:T(8,128)}, u32[]{:S(2)}) copy-start(f32[8,8,256]{2,1,0:T(8,128)} %param.5) | copy-start | bytes 196612
  0.7 18.3 %copy-start.14 = (f32[8,8,256]{2,1,0:T(8,128)S(1)}, f32[8,8,256]{2,1,0:T(8,128)}, u32[]{:S(2)}) copy-start(f32[8,8,256]{2,1,0:T(8,128)} %param.4) | copy-start | bytes 196612
  1.5 4.1 collective-permute-start
  4.6 3.4 collective-permute-start.1
  5.6 14.3 %copy-start.31 = (f32[1,8,8,256]{3,2,1,0:T(8,128)}, f32[1,8,8,256]{3,2,1,0:T(8,128)S(1)}, u32[]{:S(2)}) copy-start(f32[1,8,8,256]{3,2,1,0:T(8,128)S(1)} %add_bitcast_fusion) | copy-start | bytes 196612
  5.7 13.7 %copy-start.19 = (f32[5,1,8,256]{3,2,1,0:T(8,128)}, f32[5,1,8,256]{3,2,1,0:T(8,128)S(1)}, u32[]{:S(2)}) copy-start(f32[5,1,8,256]{3,2,1,0:T(8,128)S(1)} %collective-permute-done) | copy-start | bytes 122884
  8.0 11.4 %copy-start.21 = (f32[5,1,8,256]{3,2,1,0:T(8,128)}, f32[5,1,8,256]{3,2,1,0:T(8,128)S(1)}, u32[]{:S(2)}) copy-start(f32[5,1,8,256]{3,2,1,0:T(8,128)S(1)} %collective-permute-done.1) | copy-start | bytes 122884
  9.2 6.5 collective-permute-start.2
  10.6 6.2 collective-permute-start.3
  36.9 21.0 %all-to-all-start = ((f32[16,1,4096]{2,1,0:T(1,128)}), f32[16,1,4096]{2,1,0:T(1,128)S(1)}, u32[]{:S(2)}, u32[]{:S(2)}) async-start(f32[16,1,4096]{2,1,0:T(1,128)} %reshape.425), calls=%async_computation | async-start | bytes 524288 | tf_op jit(solution)/shard_map/all_to_all | solution.py:71
  83.8 13.3 %copy-start.33 = (f32[8,16]{1,0:T(8,128)S(1)}, f32[8,16]{1,0:T(8,128)}, u32[]{:S(2)}) copy-start(f32[8,16]{1,0:T(8,128)} %broadcast_add_fusion) | copy-start | bytes 1540
  90.9 14.7 %all-to-all-start.1 = ((f32[16,1,4096]{2,1,0:T(1,128)}), f32[16,1,4096]{2,1,0:T(1,128)S(1)}, u32[]{:S(2)}, u32[]{:S(2)}) async-start(f32[16,1,4096]{2,1,0:T(1,128)} %reshape.427), calls=%async_computation.1 | async-start | bytes 524288 | tf_op jit(solution)/shard_map/all_to_all | solution.py:71
  98.0 34.0 %copy-start.5 = (f32[160,128]{1,0:T(8,128)}, f32[160,128]{1,0:T(8,128)S(1)}, u32[]{:S(2)}) copy-start(f32[160,128]{1,0:T(8,128)S(1)} %gather_fusion) | copy-start | bytes 245764
  240.9 12.4 %all-to-all-start.5 = ((f32[16,1,4096]{2,1,0:T(1,128)}), f32[16,1,4096]{2,1,0:T(1,128)S(1)}, u32[]{:S(2)}, u32[]{:S(2)}) async-start(f32[16,1,4096]{2,1,0:T(1,128)} %reshape.431), calls=%async_computation.5 | async-start | bytes 524288 | tf_op jit(solution)/shard_map/all_to_all | solution.py:71
  254.7 11.1 %copy-start.28 = (f32[3,128,128]{1,2,0:T(8,128)S(1)}, f32[3,128,128]{1,2,0:T(8,128)}, u32[]{:S(2)}) copy-start(f32[3,128,128]{1,2,0:T(8,128)} %copy-done.27) | copy-start | bytes 589828
  254.7 12.4 %copy-start.6 = (f32[160,128]{1,0:T(8,128)S(1)}, f32[160,128]{1,0:T(8,128)}, u32[]{:S(2)}) copy-start(f32[160,128]{1,0:T(8,128)} %copy-done.5) | copy-start | bytes 245764
  285.6 31.3 %copy-start.2 = (f32[3,10,10,256]{3,2,1,0:T(8,128)S(1)}, f32[3,10,10,256]{3,2,1,0:T(8,128)}, u32[]{:S(2)}) copy-start(f32[3,10,10,256]{3,2,1,0:T(8,128)} %copy-done.1) | copy-start | bytes 921604
  326.2 8.6 %copy-start.11 = (f32[8,8,256]{2,1,0:T(8,128)S(1)}, f32[8,8,256]{2,1,0:T(8,128)}, u32[]{:S(2)}) copy-start(f32[8,8,256]{2,1,0:T(8,128)} %param.5) | copy-start | bytes 196612
  326.2 8.6 %copy-start.15 = (f32[8,8,256]{2,1,0:T(8,128)S(1)}, f32[8,8,256]{2,1,0:T(8,128)}, u32[]{:S(2)}) copy-start(f32[8,8,256]{2,1,0:T(8,128)} %param.4) | copy-start | bytes 196612
  326.2 8.6 %copy-start.20 = (f32[5,1,8,256]{3,2,1,0:T(8,128)S(1)}, f32[5,1,8,256]{3,2,1,0:T(8,128)}, u32[]{:S(2)}) copy-start(f32[5,1,8,256]{3,2,1,0:T(8,128)} %copy-done.19) | copy-start | bytes 122884
  326.2 8.6 %copy-start.22 = (f32[5,1,8,256]{3,2,1,0:T(8,128)S(1)}, f32[5,1,8,256]{3,2,1,0:T(8,128)}, u32[]{:S(2)}) copy-start(f32[5,1,8,256]{3,2,1,0:T(8,128)} %copy-done.21) | copy-start | bytes 122884
  326.2 8.6 %copy-start.24 = (f32[5,10,1,256]{3,2,1,0:T(1,128)S(1)}, f32[5,10,1,256]{3,2,1,0:T(1,128)}, u32[]{:S(2)}) copy-start(f32[5,10,1,256]{3,2,1,0:T(1,128)} %copy-done.23) | copy-start | bytes 153604
  326.2 8.6 %copy-start.30 = (f32[5,10,1,256]{3,2,1,0:T(1,128)S(1)}, f32[5,10,1,256]{3,2,1,0:T(1,128)}, u32[]{:S(2)}) copy-start(f32[5,10,1,256]{3,2,1,0:T(1,128)} %copy-done.29) | copy-start | bytes 153604
  329.3 21.1 %copy-start.17 = (f32[9,9,256]{2,1,0:T(8,128)S(1)}, f32[9,9,256]{2,1,0:T(8,128)}, u32[]{:S(2)}) copy-start(f32[9,9,256]{2,1,0:T(8,128)} %copy-done.16) | copy-start | bytes 248836
  329.3 18.2 %all-to-all-start.8 = ((f32[256,1,1]{2,1,0:T(1,128)}), f32[256,1,1]{2,1,0:T(1,128)S(1)}, u32[]{:S(2)}, u32[]{:S(2)}) async-start(f32[256,1,1]{2,1,0:T(1,128)} %broadcast_in_dim.10), calls=%async_computation.8 | async-start | bytes 262144 | tf_op jit(solution)/shard_map/all_to_all | solution.py:38
  350.6 6.4 copy-start.18
  424.3 11.1 %copy-start.7 = (f32[160,128]{1,0:T(8,128)S(1)}, f32[160,128]{1,0:T(8,128)}, u32[]{:S(2)}) copy-start(f32[160,128]{1,0:T(8,128)} %copy-done.5) | copy-start | bytes 245764
  557.8 12.4 %all-to-all-start.14 = ((f32[16,1,4096]{2,1,0:T(1,128)}), f32[16,1,4096]{2,1,0:T(1,128)S(1)}, u32[]{:S(2)}, u32[]{:S(2)}) async-start(f32[16,1,4096]{2,1,0:T(1,128)} %reshape.439), calls=%async_computation.14 | async-start | bytes 524288 | tf_op jit(solution)/shard_map/all_to_all | solution.py:71
  571.5 11.2 %copy-start.26 = (f32[3,128,128]{1,2,0:T(8,128)S(1)}, f32[3,128,128]{1,2,0:T(8,128)}, u32[]{:S(2)}) copy-start(f32[3,128,128]{1,2,0:T(8,128)} %copy-done.25) | copy-start | bytes 589828
  602.5 31.3 %copy-start.4 = (f32[3,10,10,256]{3,2,1,0:T(8,128)S(1)}, f32[3,10,10,256]{3,2,1,0:T(8,128)}, u32[]{:S(2)}) copy-start(f32[3,10,10,256]{3,2,1,0:T(8,128)} %copy-done.3) | copy-start | bytes 921604
  643.1 22.2 %copy-start.9 = (f32[3,10,10,256]{3,2,1,0:T(8,128)S(1)}, f32[3,10,10,256]{3,2,1,0:T(8,128)}, u32[]{:S(2)}) copy-start(f32[3,10,10,256]{3,2,1,0:T(8,128)} %copy-done.8) | copy-start | bytes 921604
  (11 other events, 16.4 us)

commit v4 on v3

--- a/solution.py
+++ b/solution.py
@@ -66,6 +66,9 @@
 
 
 def exchange(cells, partial, axis, split_axis, concat_axis):
+    if partial is None:
+        moved = lax.all_to_all(cells, axis, split_axis, concat_axis, tiled=True)
+        return moved, None
     count = lax.axis_size(axis)
     rider = jnp.broadcast_to(partial.astype(cells.dtype), (1,) + cells.shape[1:])
     moved = lax.all_to_all(
@@ -229,7 +232,7 @@
     for outer_step in range(OUTER):
         pushing = pressure_gradient(pressure_low)
         residual = forcing - pushing - operate(velocity_ext, shear_resistance_map)
-        spectrum, _ = transform_forward(residual, tables, jnp.float32(0.0))
+        spectrum, _ = transform_forward(residual, tables, None)
         direction_ext = None
         energy_now = jnp.float32(1.0)
         for inner_step in range(INNER):

time: 676 us -> 643 us (0.951)
  local copies, waits for them, and re-layouts: 253 us -> 220 us
  matrix products: 67.3 us -> 76.2 us
    unnamed x108 -> x102, local copies, waits for them, and re-layouts: 176 us -> 126 us
    all_to_all x12 -> x10, blocking collectives: 199 us -> 172 us  [exchange(): lax.all_to_all(jnp.concatenate([cells, rider], 0), axis, split_axis, conc...]
    all_to_all x0 -> x2, blocking collectives: none -> 24.2 us  [exchange(): moved = lax.all_to_all(cells, axis, split_axis, concat_axis, tiled=True)]
    all_to_all x4 -> x2, waiting for transfers between devices: 30.1 us -> 12.7 us  [exchange(): lax.all_to_all(jnp.concatenate([cells, rider], 0), axis, split_axis, conc...]
    reshape x0 -> x4, local copies, waits for them, and re-layouts: none -> 16.5 us  [the longest x2 8.64 us: transform_forward(): jnp.einsum('kx,cyzx->cykz', xtable, residual, precision=PRECISE)]
    all_to_all x4 -> x2, starting transfers between devices: 23.6 us -> 7.87 us  [exchange(): lax.all_to_all(jnp.concatenate([cells, rider], 0), axis, split_axis, conc...]
    all_to_all x0 -> x2, starting transfers between devices: none -> 15.3 us  [exchange(): moved = lax.all_to_all(cells, axis, split_axis, concat_axis, tiled=True)]
    all_to_all x0 -> x2, waiting for transfers between devices: none -> 15.1 us  [exchange(): moved = lax.all_to_all(cells, axis, split_axis, concat_axis, tiled=True)]
where the time goes in v4:
time: 643 us; the launch traced here: 635 us
  local copies, waits for them, and re-layouts  220 us (34%)
  blocking collectives  214 us (33%)
  matrix products  76.2 us (12%)
  waiting for transfers between devices  43.9 us (7%)
  starting transfers between devices  36.6 us (6%)
  other arithmetic  33.6 us (5%)
  between operations  10.7 us (2%)
    all_to_all x10, blocking collectives, exchange(): lax.all_to_all(jnp.concatenate([cells, rider], 0), axis, split_axis, conc...  172 us
    unnamed x102, local copies, waits for them, and re-layouts  126 us
    dot_general x4, matrix products, transform_inverse(): jnp.einsum('kx,cyxz->cyzk', xtable, spectrum.reshape(components, owned_he...  36.7 us
    all_to_all x2, blocking collectives, exchange(): moved = lax.all_to_all(cells, axis, split_axis, concat_axis, tiled=True)  24.2 us
    all_to_all x1, blocking collectives, global_sum(): gathered = lax.all_to_all(spread, ('row', 'col'), 0, 0, tiled=True)  17.5 us
    all_to_all x2, starting transfers between devices, exchange(): moved = lax.all_to_all(cells, axis, split_axis, concat_axis, tiled=True)  15.3 us
    all_to_all x2, waiting for transfers between devices, exchange(): moved = lax.all_to_all(cells, axis, split_axis, concat_axis, tiled=True)  15.1 us
    all_to_all x5, local copies, waits for them, and re-layouts, exchange(): moved = lax.all_to_all(cells, axis, split_axis, concat_axis, tiled=True)  14.7 us
  transfers between devices with their start and end apart: 9, of which 7 were waited for; matrix products, arithmetic and copies ran while one was open for 1% of the time, Pallas kernels for 0%

profile of v4, /device:TPU:1, one launch (start us, length us, event | category | flops | bytes accessed | tf_op | source)
XLA Modules:
  0.0 635.3 jit_solution(5646666024793061528)
XLA Ops:
  30.8 9.7 %all-to-all-start = ((f32[16,1,3072]{2,1,0:T(1,128)}), f32[16,1,3072]{2,1,0:T(1,128)S(1)}, u32[]{:S(2)}, u32[]{:S(2)}) async-start(f32[16,1,3072]{2,1,0:T(1,128)} %reshape.415), calls=%async_computation | async-start | bytes 393216 | tf_op jit(solution)/shard_map/all_to_all | solution.py:70
  43.4 7.3 %all-to-all-done = f32[16,1,3072]{2,1,0:T(1,128)S(1)} async-done(((f32[16,1,3072]{2,1,0:T(1,128)}), f32[16,1,3072]{2,1,0:T(1,128)S(1)}, u32[]{:S(2)}, u32[]{:S(2)}) %all-to-all-start) | async-done | bytes 196640 | tf_op jit(solution)/shard_map/all_to_all | solution.py:70
  63.3 5.9 fusion.8
  84.4 7.9 %all-to-all-done.1 = f32[16,1,3072]{2,1,0:T(1,128)S(1)} async-done(((f32[16,1,3072]{2,1,0:T(1,128)}), f32[16,1,3072]{2,1,0:T(1,128)S(1)}, u32[]{:S(2)}, u32[]{:S(2)}) %all-to-all-start.1) | async-done | bytes 196640 | tf_op jit(solution)/shard_map/all_to_all | solution.py:70
  103.4 10.7 %all_to_all.258 = f32[4,160,128]{2,0,1:T(4,128)S(1)} all-to-all(f32[4,160,128]{2,0,1:T(4,128)S(1)} %concatenate.180.clone), channel_id=1, replica_groups=mesh['row'=16,'col'=16] {'col'}, dimensions={1} | all-to-all | bytes 655360 | tf_op jit(solution)/shard_map/all_to_all | solution.py:74
  120.3 25.2 %all_to_all.259 = f32[4,160,160]{2,0,1:T(4,128)S(1)} all-to-all(f32[4,160,160]{2,0,1:T(4,128)S(1)} %concatenate.181.clone), channel_id=1, replica_groups=mesh['row'=16,'col'=16] {'row'}, dimensions={1} | all-to-all | bytes 819200 | tf_op jit(solution)/shard_map/all_to_all | solution.py:74
  150.2 9.2 %fusion.29 = f32[3,10,10,256]{3,2,1,0:T(8,128)S(1)} fusion(f32[3,10,256,10]{3,2,1,0:T(8,128)} %reshape.374), kind=kOutput, calls=%fused_computation.56 | convolution fusion | flops 236912640 | bytes 614400 | tf_op jit(solution)/shard_map/kx,cyxz->cyzk/dot_general | solution.py:136
  171.7 6.5 %reshape.419 = f32[16,1,4096]{2,1,0:T(1,128)S(1)} reshape(f32[2048,4,8]{2,1,0:T(4,128)} %pad_bitcast_fusion.3) | data formatting | bytes 524288
  178.3 14.0 %all_to_all.260 = f32[16,1,4096]{2,1,0:T(1,128)S(1)} all-to-all(f32[16,1,4096]{2,1,0:T(1,128)S(1)} %reshape.419), channel_id=1, replica_groups=mesh['row'=16,'col'=16] {'row'}, dimensions={0} | all-to-all | bytes 524288 | tf_op jit(solution)/shard_map/all_to_all | solution.py:74
  193.5 6.3 reshape.420
  217.6 7.1 %reshape.421 = f32[16,1,4096]{2,1,0:T(1,128)} reshape(f32[2048,4,8]{2,1,0:T(4,128)} %pad_bitcast_fusion.2) | data formatting | bytes 524288
  230.8 6.4 %all-to-all-done.5 = f32[16,1,4096]{2,1,0:T(1,128)S(1)} async-done(((f32[16,1,4096]{2,1,0:T(1,128)}), f32[16,1,4096]{2,1,0:T(1,128)S(1)}, u32[]{:S(2)}, u32[]{:S(2)}) %all-to-all-start.5) | async-done | bytes 262176 | tf_op jit(solution)/shard_map/all_to_all | solution.py:74
  238.5 6.3 reshape.422
  252.3 11.1 %all_to_all.261 = f32[4,160,128]{2,0,1:T(4,128)S(1)} all-to-all(f32[4,160,128]{2,0,1:T(4,128)S(1)} %concatenate.190.clone), channel_id=1, replica_groups=mesh['row'=16,'col'=16] {'col'}, dimensions={1} | all-to-all | bytes 655360 | tf_op jit(solution)/shard_map/all_to_all | solution.py:74
  269.5 25.2 %all_to_all.262 = f32[4,160,160]{2,0,1:T(4,128)S(1)} all-to-all(f32[4,160,160]{2,0,1:T(4,128)S(1)} %concatenate.191.clone), channel_id=1, replica_groups=mesh['row'=16,'col'=16] {'row'}, dimensions={1} | all-to-all | bytes 819200 | tf_op jit(solution)/shard_map/all_to_all | solution.py:74
  300.8 9.2 %convolution_add_fusion.1 = f32[3,10,10,256]{3,2,1,0:T(8,128)S(1)} fusion(f32[3,10,256,10]{3,2,1,0:T(8,128)} %reshape.382, f32[3,10,10,256]{3,2,1,0:T(8,128)S(1)} %copy-done.2, f32[]{:T(128)S(6)} %div.64), kind=kOutput, calls=%fused_computation.10 | convolution fusion | flops 237066240 | bytes 921604 | tf_op jit(solution)/shard_map/kx,cyxz->cyzk/dot_general | solution.py:136
  318.5 12.4 %all-to-all-done.8 = f32[256,1,1]{2,1,0:T(1,128)S(1)} async-done(((f32[256,1,1]{2,1,0:T(1,128)}), f32[256,1,1]{2,1,0:T(1,128)S(1)}, u32[]{:S(2)}, u32[]{:S(2)}) %all-to-all-start.8) | async-done | bytes 1056 | tf_op jit(solution)/shard_map/all_to_all | solution.py:38
  344.9 13.6 %all_to_all.263 = f32[16,1,3072]{2,1,0:T(1,128)S(1)} all-to-all(f32[16,1,3072]{2,1,0:T(1,128)S(1)} %reshape.423), channel_id=1, replica_groups=mesh['row'=16,'col'=16] {'row'}, dimensions={0} | all-to-all | bytes 393216 | tf_op jit(solution)/shard_map/all_to_all | solution.py:70
  381.6 10.6 %all_to_all.264 = f32[16,1,3072]{2,1,0:T(1,128)S(1)} all-to-all(f32[16,1,3072]{2,1,0:T(1,128)S(1)} %reshape.425), channel_id=1, replica_groups=mesh['row'=16,'col'=16] {'col'}, dimensions={0} | all-to-all | bytes 393216 | tf_op jit(solution)/shard_map/all_to_all | solution.py:70
  404.0 10.9 %all_to_all.265 = f32[4,160,128]{2,0,1:T(4,128)S(1)} all-to-all(f32[4,160,128]{2,0,1:T(4,128)S(1)} %concatenate.205.clone), channel_id=1, replica_groups=mesh['row'=16,'col'=16] {'col'}, dimensions={1} | all-to-all | bytes 655360 | tf_op jit(solution)/shard_map/all_to_all | solution.py:74
  420.8 25.1 %all_to_all.266 = f32[4,160,160]{2,0,1:T(4,128)S(1)} all-to-all(f32[4,160,160]{2,0,1:T(4,128)S(1)} %concatenate.206.clone), channel_id=1, replica_groups=mesh['row'=16,'col'=16] {'row'}, dimensions={1} | all-to-all | bytes 819200 | tf_op jit(solution)/shard_map/all_to_all | solution.py:74
  450.6 9.2 %fusion.24 = f32[3,10,10,256]{3,2,1,0:T(8,128)S(1)} fusion(f32[3,10,256,10]{3,2,1,0:T(8,128)} %reshape.390), kind=kOutput, calls=%fused_computation.51 | convolution fusion | flops 236912640 | bytes 614400 | tf_op jit(solution)/shard_map/kx,cyxz->cyzk/dot_general | solution.py:136
  472.0 6.5 %reshape.427 = f32[16,1,4096]{2,1,0:T(1,128)S(1)} reshape(f32[2048,4,8]{2,1,0:T(4,128)} %pad_bitcast_fusion.1) | data formatting | bytes 524288
  478.5 14.0 %all_to_all.267 = f32[16,1,4096]{2,1,0:T(1,128)S(1)} all-to-all(f32[16,1,4096]{2,1,0:T(1,128)S(1)} %reshape.427), channel_id=1, replica_groups=mesh['row'=16,'col'=16] {'row'}, dimensions={0} | all-to-all | bytes 524288 | tf_op jit(solution)/shard_map/all_to_all | solution.py:74
  493.8 6.3 reshape.428
  517.8 7.1 %reshape.429 = f32[16,1,4096]{2,1,0:T(1,128)} reshape(f32[2048,4,8]{2,1,0:T(4,128)} %pad_bitcast_fusion) | data formatting | bytes 524288
  531.0 6.4 %all-to-all-done.14 = f32[16,1,4096]{2,1,0:T(1,128)S(1)} async-done(((f32[16,1,4096]{2,1,0:T(1,128)}), f32[16,1,4096]{2,1,0:T(1,128)S(1)}, u32[]{:S(2)}, u32[]{:S(2)}) %all-to-all-start.14) | async-done | bytes 262176 | tf_op jit(solution)/shard_map/all_to_all | solution.py:74
  538.7 6.3 reshape.430
  552.5 11.1 %all_to_all.268 = f32[4,160,128]{2,0,1:T(4,128)S(1)} all-to-all(f32[4,160,128]{2,0,1:T(4,128)S(1)} %concatenate.215.clone), channel_id=1, replica_groups=mesh['row'=16,'col'=16] {'col'}, dimensions={1} | all-to-all | bytes 655360 | tf_op jit(solution)/shard_map/all_to_all | solution.py:74
  569.6 25.1 %all_to_all.269 = f32[4,160,160]{2,0,1:T(4,128)S(1)} all-to-all(f32[4,160,160]{2,0,1:T(4,128)S(1)} %concatenate.216.clone), channel_id=1, replica_groups=mesh['row'=16,'col'=16] {'row'}, dimensions={1} | all-to-all | bytes 819200 | tf_op jit(solution)/shard_map/all_to_all | solution.py:74
  600.9 9.2 %convolution_add_fusion = f32[3,10,10,256]{3,2,1,0:T(8,128)S(1)} fusion(f32[3,10,256,10]{3,2,1,0:T(8,128)} %reshape.398, f32[3,10,10,256]{3,2,1,0:T(8,128)S(1)} %copy-done.4, f32[]{:T(128)S(6)} %div.67), kind=kOutput, calls=%fused_computation.9 | convolution fusion | flops 237066240 | bytes 921604 | tf_op jit(solution)/shard_map/kx,cyxz->cyzk/dot_general | solution.py:136
  612.7 17.5 %all_to_all.270 = f32[256,1,1]{2,1,0:T(1,128)S(1)} all-to-all(f32[256,1,1]{2,1,0:T(1,128)S(1)} %broadcast_in_dim.11), channel_id=1, replica_groups=mesh['row'=16,'col'=16] {'row','col'}, dimensions={0} | all-to-all | bytes 2048 | tf_op jit(solution)/shard_map/all_to_all | solution.py:38
  (374 shorter events, 265.4 us)
Async XLA Ops:
  0.6 18.3 %copy-start = (f32[3,8,8,256]{3,2,1,0:T(8,128)S(1)}, f32[3,8,8,256]{3,2,1,0:T(8,128)}, u32[]{:S(2)}) copy-start(f32[3,8,8,256]{3,2,1,0:T(8,128)} %param.3) | copy-start | bytes 589828
  0.6 18.3 %copy-start.10 = (f32[8,8,256]{2,1,0:T(8,128)S(1)}, f32[8,8,256]{2,1,0:T(8,128)}, u32[]{:S(2)}) copy-start(f32[8,8,256]{2,1,0:T(8,128)} %param.5) | copy-start | bytes 196612
  0.7 18.3 %copy-start.14 = (f32[8,8,256]{2,1,0:T(8,128)S(1)}, f32[8,8,256]{2,1,0:T(8,128)}, u32[]{:S(2)}) copy-start(f32[8,8,256]{2,1,0:T(8,128)} %param.4) | copy-start | bytes 196612
  1.5 4.2 collective-permute-start
  4.6 3.4 collective-permute-start.1
  5.6 14.3 %copy-start.31 = (f32[1,8,8,256]{3,2,1,0:T(8,128)}, f32[1,8,8,256]{3,2,1,0:T(8,128)S(1)}, u32[]{:S(2)}) copy-start(f32[1,8,8,256]{3,2,1,0:T(8,128)S(1)} %add_bitcast_fusion) | copy-start | bytes 196612
  5.7 13.6 %copy-start.23 = (f32[5,1,8,256]{3,2,1,0:T(8,128)}, f32[5,1,8,256]{3,2,1,0:T(8,128)S(1)}, u32[]{:S(2)}) copy-start(f32[5,1,8,256]{3,2,1,0:T(8,128)S(1)} %collective-permute-done) | copy-start | bytes 122884
  8.0 11.4 %copy-start.25 = (f32[5,1,8,256]{3,2,1,0:T(8,128)}, f32[5,1,8,256]{3,2,1,0:T(8,128)S(1)}, u32[]{:S(2)}) copy-start(f32[5,1,8,256]{3,2,1,0:T(8,128)S(1)} %collective-permute-done.1) | copy-start | bytes 122884
  9.2 6.5 %collective-permute-start.2 = (f32[5,10,1,256]{3,2,1,0:T(1,128)S(1)}, f32[5,10,1,256]{3,2,1,0:T(1,128)S(1)}, u32[]{:S(2)}, u32[]{:S(2)}) collective-permute-start(f32[5,10,1,256]{3,2,1,0:T(1,128)S(1)} %get-tuple-element.56), channel_id=1, source_target_pairs={{0,1},{1,2},{2,3},{3,4},{4,5},{5,6},{6,7},{7,8},{8,9},{9,10},{10,1... | collective-permute-start | bytes 153608 | tf_op jit(solution)/shard_map/ppermute | solution.py:26
  10.6 6.1 collective-permute-start.3
  30.8 19.8 %all-to-all-start = ((f32[16,1,3072]{2,1,0:T(1,128)}), f32[16,1,3072]{2,1,0:T(1,128)S(1)}, u32[]{:S(2)}, u32[]{:S(2)}) async-start(f32[16,1,3072]{2,1,0:T(1,128)} %reshape.415), calls=%async_computation | async-start | bytes 393216 | tf_op jit(solution)/shard_map/all_to_all | solution.py:70
  69.2 15.1 %copy-start.33 = (f32[128]{0:T(128)S(1)}, f32[128]{0:T(128)}, u32[]{:S(2)}) copy-start(f32[128]{0:T(128)} %add.559) | copy-start | bytes 1540
  69.2 15.1 %copy-start.34 = (f32[128]{0:T(128)S(1)}, f32[128]{0:T(128)}, u32[]{:S(2)}) copy-start(f32[128]{0:T(128)} %multiply_subtract_fusion.2) | copy-start | bytes 1540
  78.7 13.5 %all-to-all-start.1 = ((f32[16,1,3072]{2,1,0:T(1,128)}), f32[16,1,3072]{2,1,0:T(1,128)S(1)}, u32[]{:S(2)}, u32[]{:S(2)}) async-start(f32[16,1,3072]{2,1,0:T(1,128)} %reshape.417), calls=%async_computation.1 | async-start | bytes 393216 | tf_op jit(solution)/shard_map/all_to_all | solution.py:70
  93.4 8.7 %copy-start.5 = (f32[160,128]{1,0:T(8,128)S(1)}, f32[160,128]{1,0:T(8,128)}, u32[]{:S(2)}) copy-start(f32[160,128]{1,0:T(8,128)} %gather_fusion) | copy-start | bytes 245764
  102.1 12.9 %copy-start.20 = (f32[3,128,128]{1,2,0:T(8,128)}, f32[3,128,128]{1,2,0:T(8,128)S(1)}, u32[]{:S(2)}) copy-start(f32[3,128,128]{1,2,0:T(8,128)S(1)} %get-tuple-element.92) | copy-start | bytes 589828
  224.8 12.4 %all-to-all-start.5 = ((f32[16,1,4096]{2,1,0:T(1,128)}), f32[16,1,4096]{2,1,0:T(1,128)S(1)}, u32[]{:S(2)}, u32[]{:S(2)}) async-start(f32[16,1,4096]{2,1,0:T(1,128)} %reshape.421), calls=%async_computation.5 | async-start | bytes 524288 | tf_op jit(solution)/shard_map/all_to_all | solution.py:74
  238.5 11.2 %copy-start.21 = (f32[3,128,128]{1,2,0:T(8,128)S(1)}, f32[3,128,128]{1,2,0:T(8,128)}, u32[]{:S(2)}) copy-start(f32[3,128,128]{1,2,0:T(8,128)} %copy-done.20) | copy-start | bytes 589828
  269.4 31.3 %copy-start.2 = (f32[3,10,10,256]{3,2,1,0:T(8,128)S(1)}, f32[3,10,10,256]{3,2,1,0:T(8,128)}, u32[]{:S(2)}) copy-start(f32[3,10,10,256]{3,2,1,0:T(8,128)} %copy-done.1) | copy-start | bytes 921604
  310.1 8.1 %copy-start.11 = (f32[8,8,256]{2,1,0:T(8,128)S(1)}, f32[8,8,256]{2,1,0:T(8,128)}, u32[]{:S(2)}) copy-start(f32[8,8,256]{2,1,0:T(8,128)} %param.5) | copy-start | bytes 196612
  310.2 8.1 %copy-start.15 = (f32[8,8,256]{2,1,0:T(8,128)S(1)}, f32[8,8,256]{2,1,0:T(8,128)}, u32[]{:S(2)}) copy-start(f32[8,8,256]{2,1,0:T(8,128)} %param.4) | copy-start | bytes 196612
  310.2 8.1 %copy-start.24 = (f32[5,1,8,256]{3,2,1,0:T(8,128)S(1)}, f32[5,1,8,256]{3,2,1,0:T(8,128)}, u32[]{:S(2)}) copy-start(f32[5,1,8,256]{3,2,1,0:T(8,128)} %copy-done.23) | copy-start | bytes 122884
  310.2 8.1 %copy-start.26 = (f32[5,1,8,256]{3,2,1,0:T(8,128)S(1)}, f32[5,1,8,256]{3,2,1,0:T(8,128)}, u32[]{:S(2)}) copy-start(f32[5,1,8,256]{3,2,1,0:T(8,128)} %copy-done.25) | copy-start | bytes 122884
  310.2 8.1 %copy-start.28 = (f32[5,10,1,256]{3,2,1,0:T(1,128)S(1)}, f32[5,10,1,256]{3,2,1,0:T(1,128)}, u32[]{:S(2)}) copy-start(f32[5,10,1,256]{3,2,1,0:T(1,128)} %copy-done.27) | copy-start | bytes 153604
  310.2 8.1 %copy-start.30 = (f32[5,10,1,256]{3,2,1,0:T(1,128)S(1)}, f32[5,10,1,256]{3,2,1,0:T(1,128)}, u32[]{:S(2)}) copy-start(f32[5,10,1,256]{3,2,1,0:T(1,128)} %copy-done.29) | copy-start | bytes 153604
  313.1 17.7 %all-to-all-start.8 = ((f32[256,1,1]{2,1,0:T(1,128)}), f32[256,1,1]{2,1,0:T(1,128)S(1)}, u32[]{:S(2)}, u32[]{:S(2)}) async-start(f32[256,1,1]{2,1,0:T(1,128)} %broadcast_in_dim.10), calls=%async_computation.8 | async-start | bytes 262144 | tf_op jit(solution)/shard_map/all_to_all | solution.py:38
  318.4 15.5 %copy-start.17 = (f32[9,9,256]{2,1,0:T(8,128)S(1)}, f32[9,9,256]{2,1,0:T(8,128)}, u32[]{:S(2)}) copy-start(f32[9,9,256]{2,1,0:T(8,128)} %copy-done.16) | copy-start | bytes 248836
  393.4 9.3 %copy-start.7 = (f32[160,128]{1,0:T(8,128)S(1)}, f32[160,128]{1,0:T(8,128)}, u32[]{:S(2)}) copy-start(f32[160,128]{1,0:T(8,128)} %gather_fusion) | copy-start | bytes 245764
  524.9 12.4 %all-to-all-start.14 = ((f32[16,1,4096]{2,1,0:T(1,128)}), f32[16,1,4096]{2,1,0:T(1,128)S(1)}, u32[]{:S(2)}, u32[]{:S(2)}) async-start(f32[16,1,4096]{2,1,0:T(1,128)} %reshape.429), calls=%async_computation.14 | async-start | bytes 524288 | tf_op jit(solution)/shard_map/all_to_all | solution.py:74
  538.6 11.2 %copy-start.19 = (f32[3,128,128]{1,2,0:T(8,128)S(1)}, f32[3,128,128]{1,2,0:T(8,128)}, u32[]{:S(2)}) copy-start(f32[3,128,128]{1,2,0:T(8,128)} %copy-done.18) | copy-start | bytes 589828
  569.6 31.3 %copy-start.4 = (f32[3,10,10,256]{3,2,1,0:T(8,128)S(1)}, f32[3,10,10,256]{3,2,1,0:T(8,128)}, u32[]{:S(2)}) copy-start(f32[3,10,10,256]{3,2,1,0:T(8,128)} %copy-done.3) | copy-start | bytes 921604
  610.4 22.0 %copy-start.9 = (f32[3,10,10,256]{3,2,1,0:T(8,128)S(1)}, f32[3,10,10,256]{3,2,1,0:T(8,128)}, u32[]{:S(2)}) copy-start(f32[3,10,10,256]{3,2,1,0:T(8,128)} %copy-done.8) | copy-start | bytes 921604
  (12 other events, 28.1 us)

commit v5 on v4

--- a/solution.py
+++ b/solution.py
@@ -229,10 +229,11 @@
     pressure_low = extended[3, : owned_height_lines + 1, : owned_depth_slices + 1, :]
     symbol = spectral_symbol(prior_window_motion.shape)
     inner_cells = (slice(None), slice(1, owned_height_lines + 1), slice(1, owned_depth_slices + 1))
+    pushing = pressure_gradient(pressure_low)
+    residual = forcing - pushing - operate(velocity_ext, shear_resistance_map)
+    spectrum, _ = transform_forward(residual, tables, None)
+    components = residual.shape[0]
     for outer_step in range(OUTER):
-        pushing = pressure_gradient(pressure_low)
-        residual = forcing - pushing - operate(velocity_ext, shear_resistance_map)
-        spectrum, _ = transform_forward(residual, tables, None)
         direction_ext = None
         energy_now = jnp.float32(1.0)
         for inner_step in range(INNER):
@@ -252,7 +253,21 @@
             energy_now = energy_next
             image = operate(direction_ext, shear_resistance_map)
             curvature_part = jnp.sum(direction_ext[inner_cells] * image)
-        step_size = energy_now / global_sum(curvature_part)
+        if outer_step < OUTER - 1:
+            base_pressure = pressure_low + AUGMENT * divergence_region(velocity_ext)
+            held = forcing - pressure_gradient(base_pressure) - operate(
+                velocity_ext, shear_resistance_map
+            )
+            moving = (
+                -pressure_gradient(AUGMENT * divergence_region(direction_ext)) - image
+            )
+            both, curvature = transform_forward(
+                jnp.concatenate([held, moving], 0), tables, curvature_part
+            )
+            step_size = energy_now / curvature
+            spectrum = both[:components] + step_size * both[components:]
+        else:
+            step_size = energy_now / global_sum(curvature_part)
         velocity_ext = velocity_ext + step_size * direction_ext
         spread_now = divergence_region(velocity_ext)
         pressure_low = pressure_low + AUGMENT * spread_now

time: 643 us -> 668 us (1.039)
  local copies, waits for them, and re-layouts: 220 us -> 261 us
  blocking collectives: 214 us -> 187 us
  other arithmetic: 33.6 us -> 40.9 us
    unnamed x102 -> x124, local copies, waits for them, and re-layouts: 126 us -> 158 us
    all_to_all x2 -> x0, blocking collectives: 24.2 us -> none  [exchange(): moved = lax.all_to_all(cells, axis, split_axis, concat_axis, tiled=True)]
    all_to_all x2 -> x4, waiting for transfers between devices: 12.7 us -> 31.1 us  [exchange(): lax.all_to_all(jnp.concatenate([cells, rider], 0), axis, split_axis, conc...]
    all_to_all x1 -> x0, waiting for transfers between devices: 12.4 us -> none  [global_sum(): gathered = lax.all_to_all(spread, ('row', 'col'), 0, 0, tiled=True)]
    all_to_all x4 -> x6, local copies, waits for them, and re-layouts: 11.2 us -> 20.1 us  [exchange(): lax.all_to_all(jnp.concatenate([cells, rider], 0), axis, split_axis, conc...]
    all_to_all x2 -> x4, starting transfers between devices: 7.87 us -> 16.5 us  [exchange(): lax.all_to_all(jnp.concatenate([cells, rider], 0), axis, split_axis, conc...]
    reshape x6 -> x7, local copies, waits for them, and re-layouts: 12.7 us -> 20.4 us  [transform_forward(): spectrum.reshape(components, ylength, xpiece, owned_depth_slices)]
    all_to_all x5 -> x3, local copies, waits for them, and re-layouts: 14.7 us -> 8.13 us  [exchange(): moved = lax.all_to_all(cells, axis, split_axis, concat_axis, tiled=True)]
  transfers between devices with their start and end apart: 9 -> 10, of which waited for: 7 -> 8; matrix products, arithmetic and copies ran while one was open for 1% -> 3% of each run, Pallas kernels for 0% -> 0%
where the time goes in v5:
time: 668 us; the launch traced here: 661 us
  local copies, waits for them, and re-layouts  261 us (39%)
  blocking collectives  187 us (28%)
  matrix products  71.5 us (11%)
  waiting for transfers between devices  49.9 us (7%)
  other arithmetic  40.9 us (6%)
  starting transfers between devices  39.8 us (6%)
  between operations  10.9 us (2%)
    all_to_all x10, blocking collectives, exchange(): lax.all_to_all(jnp.concatenate([cells, rider], 0), axis, split_axis, conc...  170 us
    unnamed x124, local copies, waits for them, and re-layouts  158 us
    dot_general x4, matrix products, transform_inverse(): jnp.einsum('kx,cyxz->cyzk', xtable, spectrum.reshape(components, owned_he...  36.7 us
    all_to_all x4, waiting for transfers between devices, exchange(): lax.all_to_all(jnp.concatenate([cells, rider], 0), axis, split_axis, conc...  31.1 us
    reshape x7, local copies, waits for them, and re-layouts, transform_forward(): spectrum.reshape(components, ylength, xpiece, owned_depth_slices)  20.4 us
    all_to_all x6, local copies, waits for them, and re-layouts, exchange(): lax.all_to_all(jnp.concatenate([cells, rider], 0), axis, split_axis, conc...  20.1 us
    all_to_all x1, blocking collectives, global_sum(): gathered = lax.all_to_all(spread, ('row', 'col'), 0, 0, tiled=True)  17.5 us
    all_to_all x4, starting transfers between devices, exchange(): lax.all_to_all(jnp.concatenate([cells, rider], 0), axis, split_axis, conc...  16.5 us
  transfers between devices with their start and end apart: 10, of which 8 were waited for; matrix products, arithmetic and copies ran while one was open for 3% of the time, Pallas kernels for 0%

profile of v5, /device:TPU:1, one launch (start us, length us, event | category | flops | bytes accessed | tf_op | source)
XLA Modules:
  0.0 660.9 jit_solution(839041579599646530)
XLA Ops:
  30.8 9.4 %all-to-all-start = ((f32[16,1,3072]{2,1,0:T(1,128)}), f32[16,1,3072]{2,1,0:T(1,128)S(1)}, u32[]{:S(2)}, u32[]{:S(2)}) async-start(f32[16,1,3072]{2,1,0:T(1,128)} %reshape.418), calls=%async_computation | async-start | bytes 393216 | tf_op jit(solution)/shard_map/all_to_all | solution.py:70
  43.1 7.3 %all-to-all-done = f32[16,1,3072]{2,1,0:T(1,128)S(1)} async-done(((f32[16,1,3072]{2,1,0:T(1,128)}), f32[16,1,3072]{2,1,0:T(1,128)S(1)}, u32[]{:S(2)}, u32[]{:S(2)}) %all-to-all-start) | async-done | bytes 196640 | tf_op jit(solution)/shard_map/all_to_all | solution.py:70
  84.2 7.9 %all-to-all-done.1 = f32[16,1,3072]{2,1,0:T(1,128)S(1)} async-done(((f32[16,1,3072]{2,1,0:T(1,128)}), f32[16,1,3072]{2,1,0:T(1,128)S(1)}, u32[]{:S(2)}, u32[]{:S(2)}) %all-to-all-start.1) | async-done | bytes 196640 | tf_op jit(solution)/shard_map/all_to_all | solution.py:70
  103.1 10.7 %all_to_all.249 = f32[4,160,128]{2,0,1:T(4,128)S(1)} all-to-all(f32[4,160,128]{2,0,1:T(4,128)S(1)} %concatenate.196.clone), channel_id=1, replica_groups=mesh['row'=16,'col'=16] {'col'}, dimensions={1} | all-to-all | bytes 655360 | tf_op jit(solution)/shard_map/all_to_all | solution.py:74
  119.9 25.3 %all_to_all.250 = f32[4,160,160]{2,0,1:T(4,128)S(1)} all-to-all(f32[4,160,160]{2,0,1:T(4,128)S(1)} %concatenate.197.clone), channel_id=1, replica_groups=mesh['row'=16,'col'=16] {'row'}, dimensions={1} | all-to-all | bytes 819200 | tf_op jit(solution)/shard_map/all_to_all | solution.py:74
  149.6 9.2 %fusion.28 = f32[3,10,10,256]{3,2,1,0:T(8,128)S(1)} fusion(f32[3,10,256,10]{3,2,1,0:T(8,128)} %reshape.376), kind=kOutput, calls=%fused_computation.59 | convolution fusion | flops 236912640 | bytes 614400 | tf_op jit(solution)/shard_map/kx,cyxz->cyzk/dot_general | solution.py:136
  171.0 6.5 reshape.422
  177.5 14.0 %all_to_all.251 = f32[16,1,4096]{2,1,0:T(1,128)S(1)} all-to-all(f32[16,1,4096]{2,1,0:T(1,128)S(1)} %reshape.422), channel_id=1, replica_groups=mesh['row'=16,'col'=16] {'row'}, dimensions={0} | all-to-all | bytes 524288 | tf_op jit(solution)/shard_map/all_to_all | solution.py:74
  192.9 6.3 reshape.423
  216.9 7.2 %reshape.424 = f32[16,1,4096]{2,1,0:T(1,128)} reshape(f32[2048,4,8]{2,1,0:T(4,128)} %pad_bitcast_fusion.4) | data formatting | bytes 524288
  237.7 6.3 reshape.425
  282.7 16.0 %all-to-all-done.7 = f32[4,160,160]{2,0,1:T(4,128)S(1)} async-done(((f32[4,160,160]{2,0,1:T(4,128)}), f32[4,160,160]{2,0,1:T(4,128)S(1)}, u32[]{:S(2)}, u32[]{:S(2)}) %all-to-all-start.7) | async-done | bytes 409632 | tf_op jit(solution)/shard_map/all_to_all | solution.py:74
  304.9 9.2 %convolution_add_fusion.1 = f32[3,10,10,256]{3,2,1,0:T(8,128)S(1)} fusion(f32[3,10,256,10]{3,2,1,0:T(8,128)} %reshape.384, f32[3,10,10,256]{3,2,1,0:T(8,128)S(1)} %copy-done.4, f32[]{:T(128)S(6)} %div.64), kind=kOutput, calls=%fused_computation.8 | convolution fusion | flops 237066240 | bytes 921604 | tf_op jit(solution)/shard_map/kx,cyxz->cyzk/dot_general | solution.py:136
  317.5 7.8 %copy.370 = f32[6,8,256,8]{1,0,3,2:T(8,128)} copy(f32[6,8,256,8]{2,3,1,0:T(8,128)S(1)} %convolution_bitcast_fusion.6) | data formatting | bytes 786432
  325.4 6.4 pad_bitcast_fusion.1
  337.7 18.6 %all_to_all.252 = f32[16,1,7168]{2,1,0:T(1,128)S(1)} all-to-all(f32[16,1,7168]{2,1,0:T(1,128)S(1)} %reshape.426), channel_id=1, replica_groups=mesh['row'=16,'col'=16] {'row'}, dimensions={0} | all-to-all | bytes 917504 | tf_op jit(solution)/shard_map/all_to_all | solution.py:74
  379.2 7.4 %copy.371 = f32[6,8,128,16]{1,0,3,2:T(8,128)} copy(f32[6,8,128,16]{2,1,3,0:T(8,128)S(1)} %convolution_bitcast_fusion.5) | data formatting | bytes 786432
  386.6 6.4 pad_bitcast_fusion
  398.5 14.4 %all_to_all.253 = f32[16,1,7168]{2,1,0:T(1,128)S(1)} all-to-all(f32[16,1,7168]{2,1,0:T(1,128)S(1)} %reshape.428), channel_id=1, replica_groups=mesh['row'=16,'col'=16] {'col'}, dimensions={0} | all-to-all | bytes 917504 | tf_op jit(solution)/shard_map/all_to_all | solution.py:74
  429.9 11.4 %all_to_all.254 = f32[4,160,128]{2,0,1:T(4,128)S(1)} all-to-all(f32[4,160,128]{2,0,1:T(4,128)S(1)} %concatenate.225.clone), channel_id=1, replica_groups=mesh['row'=16,'col'=16] {'col'}, dimensions={1} | all-to-all | bytes 655360 | tf_op jit(solution)/shard_map/all_to_all | solution.py:74
  447.3 24.8 %all_to_all.255 = f32[4,160,160]{2,0,1:T(4,128)S(1)} all-to-all(f32[4,160,160]{2,0,1:T(4,128)S(1)} %concatenate.226.clone), channel_id=1, replica_groups=mesh['row'=16,'col'=16] {'row'}, dimensions={1} | all-to-all | bytes 819200 | tf_op jit(solution)/shard_map/all_to_all | solution.py:74
  475.9 9.2 %fusion.23 = f32[3,10,10,256]{3,2,1,0:T(8,128)S(1)} fusion(f32[3,10,256,10]{3,2,1,0:T(8,128)} %reshape.392), kind=kOutput, calls=%fused_computation.54 | convolution fusion | flops 236912640 | bytes 614400 | tf_op jit(solution)/shard_map/kx,cyxz->cyzk/dot_general | solution.py:136
  497.2 6.5 reshape.430
  503.8 14.0 %all_to_all.256 = f32[16,1,4096]{2,1,0:T(1,128)S(1)} all-to-all(f32[16,1,4096]{2,1,0:T(1,128)S(1)} %reshape.430), channel_id=1, replica_groups=mesh['row'=16,'col'=16] {'row'}, dimensions={0} | all-to-all | bytes 524288 | tf_op jit(solution)/shard_map/all_to_all | solution.py:74
  519.1 6.3 reshape.431
  543.1 7.2 %reshape.432 = f32[16,1,4096]{2,1,0:T(1,128)} reshape(f32[2048,4,8]{2,1,0:T(4,128)} %pad_bitcast_fusion.2) | data formatting | bytes 524288
  556.1 6.4 all-to-all-done.13
  563.9 6.3 reshape.433
  577.6 11.1 %all_to_all.257 = f32[4,160,128]{2,0,1:T(4,128)S(1)} all-to-all(f32[4,160,128]{2,0,1:T(4,128)S(1)} %concatenate.235.clone), channel_id=1, replica_groups=mesh['row'=16,'col'=16] {'col'}, dimensions={1} | all-to-all | bytes 655360 | tf_op jit(solution)/shard_map/all_to_all | solution.py:74
  594.7 25.2 %all_to_all.258 = f32[4,160,160]{2,0,1:T(4,128)S(1)} all-to-all(f32[4,160,160]{2,0,1:T(4,128)S(1)} %concatenate.236.clone), channel_id=1, replica_groups=mesh['row'=16,'col'=16] {'row'}, dimensions={1} | all-to-all | bytes 819200 | tf_op jit(solution)/shard_map/all_to_all | solution.py:74
  626.1 9.2 %convolution_add_fusion = f32[3,10,10,256]{3,2,1,0:T(8,128)S(1)} fusion(f32[3,10,256,10]{3,2,1,0:T(8,128)} %reshape.400, f32[3,10,10,256]{3,2,1,0:T(8,128)S(1)} %copy-done.2, f32[]{:T(128)S(6)} %div.67), kind=kOutput, calls=%fused_computation.7 | convolution fusion | flops 237066240 | bytes 921604 | tf_op jit(solution)/shard_map/kx,cyxz->cyzk/dot_general | solution.py:136
  637.8 17.5 %all_to_all.259 = f32[256,1,1]{2,1,0:T(1,128)S(1)} all-to-all(f32[256,1,1]{2,1,0:T(1,128)S(1)} %broadcast_in_dim.8), channel_id=1, replica_groups=mesh['row'=16,'col'=16] {'row','col'}, dimensions={0} | all-to-all | bytes 2048 | tf_op jit(solution)/shard_map/all_to_all | solution.py:38
  (410 shorter events, 298.6 us)
Async XLA Ops:
  0.6 18.3 %copy-start = (f32[3,8,8,256]{3,2,1,0:T(8,128)S(1)}, f32[3,8,8,256]{3,2,1,0:T(8,128)}, u32[]{:S(2)}) copy-start(f32[3,8,8,256]{3,2,1,0:T(8,128)} %param.3) | copy-start | bytes 589828
  0.6 18.3 %copy-start.11 = (f32[8,8,256]{2,1,0:T(8,128)S(1)}, f32[8,8,256]{2,1,0:T(8,128)}, u32[]{:S(2)}) copy-start(f32[8,8,256]{2,1,0:T(8,128)} %param.5) | copy-start | bytes 196612
  0.7 18.3 %copy-start.15 = (f32[8,8,256]{2,1,0:T(8,128)S(1)}, f32[8,8,256]{2,1,0:T(8,128)}, u32[]{:S(2)}) copy-start(f32[8,8,256]{2,1,0:T(8,128)} %param.4) | copy-start | bytes 196612
  1.5 4.2 collective-permute-start
  4.6 3.4 collective-permute-start.1
  5.6 14.3 %copy-start.40 = (f32[1,8,8,256]{3,2,1,0:T(8,128)}, f32[1,8,8,256]{3,2,1,0:T(8,128)S(1)}, u32[]{:S(2)}) copy-start(f32[1,8,8,256]{3,2,1,0:T(8,128)S(1)} %add_bitcast_fusion) | copy-start | bytes 196612
  5.7 13.6 %copy-start.23 = (f32[5,1,8,256]{3,2,1,0:T(8,128)}, f32[5,1,8,256]{3,2,1,0:T(8,128)S(1)}, u32[]{:S(2)}) copy-start(f32[5,1,8,256]{3,2,1,0:T(8,128)S(1)} %collective-permute-done) | copy-start | bytes 122884
  8.0 11.4 %copy-start.25 = (f32[5,1,8,256]{3,2,1,0:T(8,128)}, f32[5,1,8,256]{3,2,1,0:T(8,128)S(1)}, u32[]{:S(2)}) copy-start(f32[5,1,8,256]{3,2,1,0:T(8,128)S(1)} %collective-permute-done.1) | copy-start | bytes 122884
  9.2 6.5 collective-permute-start.2
  10.6 6.1 collective-permute-start.3
  30.8 19.5 %all-to-all-start = ((f32[16,1,3072]{2,1,0:T(1,128)}), f32[16,1,3072]{2,1,0:T(1,128)S(1)}, u32[]{:S(2)}, u32[]{:S(2)}) async-start(f32[16,1,3072]{2,1,0:T(1,128)} %reshape.418), calls=%async_computation | async-start | bytes 393216 | tf_op jit(solution)/shard_map/all_to_all | solution.py:70
  68.9 15.1 %copy-start.42 = (f32[128]{0:T(128)S(1)}, f32[128]{0:T(128)}, u32[]{:S(2)}) copy-start(f32[128]{0:T(128)} %add.577) | copy-start | bytes 1540
  68.9 15.1 %copy-start.43 = (f32[128]{0:T(128)S(1)}, f32[128]{0:T(128)}, u32[]{:S(2)}) copy-start(f32[128]{0:T(128)} %multiply_subtract_fusion.2) | copy-start | bytes 1540
  78.5 13.5 %all-to-all-start.1 = ((f32[16,1,3072]{2,1,0:T(1,128)}), f32[16,1,3072]{2,1,0:T(1,128)S(1)}, u32[]{:S(2)}, u32[]{:S(2)}) async-start(f32[16,1,3072]{2,1,0:T(1,128)} %reshape.420), calls=%async_computation.1 | async-start | bytes 393216 | tf_op jit(solution)/shard_map/all_to_all | solution.py:70
  101.8 12.8 %copy-start.19 = (f32[3,128,128]{1,2,0:T(8,128)}, f32[3,128,128]{1,2,0:T(8,128)S(1)}, u32[]{:S(2)}) copy-start(f32[3,128,128]{1,2,0:T(8,128)S(1)} %get-tuple-element.108) | copy-start | bytes 589828
  216.9 11.0 %copy-start.16 = (f32[8,8,256]{2,1,0:T(8,128)S(1)}, f32[8,8,256]{2,1,0:T(8,128)}, u32[]{:S(2)}) copy-start(f32[8,8,256]{2,1,0:T(8,128)} %param.4) | copy-start | bytes 196612
  216.9 11.0 %copy-start.24 = (f32[5,1,8,256]{3,2,1,0:T(8,128)S(1)}, f32[5,1,8,256]{3,2,1,0:T(8,128)}, u32[]{:S(2)}) copy-start(f32[5,1,8,256]{3,2,1,0:T(8,128)} %copy-done.23) | copy-start | bytes 122884
  216.9 11.0 %copy-start.26 = (f32[5,1,8,256]{3,2,1,0:T(8,128)S(1)}, f32[5,1,8,256]{3,2,1,0:T(8,128)}, u32[]{:S(2)}) copy-start(f32[5,1,8,256]{3,2,1,0:T(8,128)} %copy-done.25) | copy-start | bytes 122884
  216.9 11.0 %copy-start.32 = (f32[5,10,1,256]{3,2,1,0:T(1,128)S(1)}, f32[5,10,1,256]{3,2,1,0:T(1,128)}, u32[]{:S(2)}) copy-start(f32[5,10,1,256]{3,2,1,0:T(1,128)} %copy-done.31) | copy-start | bytes 153604
  216.9 11.0 %copy-start.39 = (f32[5,10,1,256]{3,2,1,0:T(1,128)S(1)}, f32[5,10,1,256]{3,2,1,0:T(1,128)}, u32[]{:S(2)}) copy-start(f32[5,10,1,256]{3,2,1,0:T(1,128)} %copy-done.38) | copy-start | bytes 153604
  224.1 12.3 %all-to-all-start.5 = ((f32[16,1,4096]{2,1,0:T(1,128)}), f32[16,1,4096]{2,1,0:T(1,128)S(1)}, u32[]{:S(2)}, u32[]{:S(2)}) async-start(f32[16,1,4096]{2,1,0:T(1,128)} %reshape.424), calls=%async_computation.5 | async-start | bytes 524288 | tf_op jit(solution)/shard_map/all_to_all | solution.py:74
  237.7 11.1 %copy-start.4 = (f32[3,10,10,256]{3,2,1,0:T(8,128)S(1)}, f32[3,10,10,256]{3,2,1,0:T(8,128)}, u32[]{:S(2)}) copy-start(f32[3,10,10,256]{3,2,1,0:T(8,128)} %copy-done.3) | copy-start | bytes 921604
  249.0 31.7 %copy-start.9 = (f32[3,10,10,256]{3,2,1,0:T(8,128)}, f32[3,10,10,256]{3,2,1,0:T(8,128)S(1)}, u32[]{:S(2)}) copy-start(f32[3,10,10,256]{3,2,1,0:T(8,128)S(1)} %slice_add_fusion) | copy-start | bytes 921604
  252.6 12.0 %all-to-all-start.6 = ((f32[4,160,128]{2,0,1:T(4,128)}), f32[4,160,128]{2,0,1:T(4,128)S(1)}, u32[]{:S(2)}, u32[]{:S(2)}) async-start(f32[4,160,128]{2,0,1:T(4,128)} %concatenate.206.clone), calls=%async_computation.6 | async-start | bytes 655360 | tf_op jit(solution)/shard_map/all_to_all | solution.py:74
  267.7 11.1 %copy-start.28 = (f32[9,9,256]{2,1,0:T(8,128)S(1)}, f32[9,9,256]{2,1,0:T(8,128)}, u32[]{:S(2)}) copy-start(f32[9,9,256]{2,1,0:T(8,128)} %copy-done.27) | copy-start | bytes 248836
  273.2 25.5 %all-to-all-start.7 = ((f32[4,160,160]{2,0,1:T(4,128)}), f32[4,160,160]{2,0,1:T(4,128)S(1)}, u32[]{:S(2)}, u32[]{:S(2)}) async-start(f32[4,160,160]{2,0,1:T(4,128)} %concatenate.207.clone), calls=%async_computation.7 | async-start | bytes 1310720 | tf_op jit(solution)/shard_map/all_to_all | solution.py:74
  428.6 13.4 %copy-start.21 = (f32[3,128,128]{1,2,0:T(8,128)}, f32[3,128,128]{1,2,0:T(8,128)S(1)}, u32[]{:S(2)}) copy-start(f32[3,128,128]{1,2,0:T(8,128)S(1)} %get-tuple-element.9) | copy-start | bytes 589828
  550.3 12.3 %all-to-all-start.13 = ((f32[16,1,4096]{2,1,0:T(1,128)}), f32[16,1,4096]{2,1,0:T(1,128)S(1)}, u32[]{:S(2)}, u32[]{:S(2)}) async-start(f32[16,1,4096]{2,1,0:T(1,128)} %reshape.432), calls=%async_computation.13 | async-start | bytes 524288 | tf_op jit(solution)/shard_map/all_to_all | solution.py:74
  563.9 11.1 %copy-start.22 = (f32[3,128,128]{1,2,0:T(8,128)S(1)}, f32[3,128,128]{1,2,0:T(8,128)}, u32[]{:S(2)}) copy-start(f32[3,128,128]{1,2,0:T(8,128)} %copy-done.21) | copy-start | bytes 589828
  594.7 31.4 %copy-start.2 = (f32[3,10,10,256]{3,2,1,0:T(8,128)S(1)}, f32[3,10,10,256]{3,2,1,0:T(8,128)}, u32[]{:S(2)}) copy-start(f32[3,10,10,256]{3,2,1,0:T(8,128)} %copy-done.1) | copy-start | bytes 921604
  635.5 22.0 %copy-start.6 = (f32[3,10,10,256]{3,2,1,0:T(8,128)S(1)}, f32[3,10,10,256]{3,2,1,0:T(8,128)}, u32[]{:S(2)}) copy-start(f32[3,10,10,256]{3,2,1,0:T(8,128)} %copy-done.5) | copy-start | bytes 921604
  635.5 22.0 %copy-start.10 = (f32[3,10,10,256]{3,2,1,0:T(8,128)S(1)}, f32[3,10,10,256]{3,2,1,0:T(8,128)}, u32[]{:S(2)}) copy-start(f32[3,10,10,256]{3,2,1,0:T(8,128)} %copy-done.9) | copy-start | bytes 921604
  (22 other events, 133.5 us)

commit v6 on v4

--- a/solution.py
+++ b/solution.py
@@ -32,6 +32,32 @@
     return cells
 
 
+def surrounded(cells):
+    rows = lax.axis_size("row")
+    cols = lax.axis_size("col")
+
+    def shifted(value, down, right):
+        pairs = [
+            (i * cols + j, ((i + down) % rows) * cols + (j + right) % cols)
+            for i in range(rows)
+            for j in range(cols)
+        ]
+        return lax.ppermute(value, ("row", "col"), pairs)
+
+    low_y = from_behind(cells[:, -1:], "row", 1)
+    high_y = from_behind(cells[:, :1], "row", -1)
+    low_z = from_behind(cells[:, :, -1:], "col", 1)
+    high_z = from_behind(cells[:, :, :1], "col", -1)
+    low_low = shifted(cells[:, -1:, -1:], 1, 1)
+    low_high = shifted(cells[:, -1:, :1], 1, -1)
+    high_low = shifted(cells[:, :1, -1:], -1, 1)
+    high_high = shifted(cells[:, :1, :1], -1, -1)
+    top = jnp.concatenate([low_low, low_y, low_high], 2)
+    middle = jnp.concatenate([low_z, cells, high_z], 2)
+    bottom = jnp.concatenate([high_low, high_y, high_high], 2)
+    return jnp.concatenate([top, middle, bottom], 1)
+
+
 def global_sum(value):
     count = lax.axis_size("row") * lax.axis_size("col")
     spread = jnp.broadcast_to(value.reshape(1), (count,))
@@ -74,9 +100,13 @@
     moved = lax.all_to_all(
         jnp.concatenate([cells, rider], 0), axis, split_axis, concat_axis, tiled=True
     )
-    arrived = jnp.moveaxis(moved[-1], concat_axis - 1, 0)
-    arrived = arrived.reshape(count, arrived.shape[0] // count, -1)[:, 0, 0]
-    return moved[:-1], jnp.sum(arrived)
+    rider = moved[-1]
+    pieces = rider.shape[concat_axis - 1] // count
+    picks = tuple(
+        slice(0, None, pieces) if dim == concat_axis - 1 else slice(0, 1)
+        for dim in range(rider.ndim)
+    )
+    return moved[:-1], jnp.sum(rider[picks])
 
 
 def spectral_symbol(shape):
@@ -213,7 +243,7 @@
     stacked_fields = jnp.concatenate(
         [prior_window_motion, prior_window_stress[None], heat_scalar[None]], 0
     )
-    extended = padded(stacked_fields, (("row", 1), ("col", 2)), 1)
+    extended = surrounded(stacked_fields)
     shear_resistance_map = jnp.exp(
         ENABLE_SWITCH
         * (

time: 643 us -> 653 us (1.016)
  starting transfers between devices: 36.6 us -> 47.6 us
    ppermute x4 -> x8, starting transfers between devices: 8.26 us -> 22 us  [the longest x4 13.6 us: shifted(): return lax.ppermute(value, ('row', 'col'), pairs)]
    unnamed x102 -> x132, local copies, waits for them, and re-layouts: 126 us -> 126 us
  transfers between devices with their start and end apart: 9 -> 13, of which waited for: 7 -> 6; matrix products, arithmetic and copies ran while one was open for 1% -> 2% of each run, Pallas kernels for 0% -> 0%
where the time goes in v6:
time: 653 us; the launch traced here: 643 us
  local copies, waits for them, and re-layouts  220 us (34%)
  blocking collectives  214 us (33%)
  matrix products  76.2 us (12%)
  starting transfers between devices  47.6 us (7%)
  waiting for transfers between devices  41 us (6%)
  other arithmetic  33.7 us (5%)
  between operations  10.9 us (2%)
    all_to_all x10, blocking collectives, exchange(): lax.all_to_all(jnp.concatenate([cells, rider], 0), axis, split_axis, conc...  173 us
    unnamed x132, local copies, waits for them, and re-layouts  126 us
    dot_general x4, matrix products, transform_inverse(): jnp.einsum('kx,cyxz->cyzk', xtable, spectrum.reshape(components, owned_he...  36.7 us
    all_to_all x2, blocking collectives, exchange(): moved = lax.all_to_all(cells, axis, split_axis, concat_axis, tiled=True)  24.2 us
    all_to_all x1, blocking collectives, global_sum(): gathered = lax.all_to_all(spread, ('row', 'col'), 0, 0, tiled=True)  17.5 us
    all_to_all x2, waiting for transfers between devices, exchange(): moved = lax.all_to_all(cells, axis, split_axis, concat_axis, tiled=True)  15.2 us
    all_to_all x5, local copies, waits for them, and re-layouts, exchange(): moved = lax.all_to_all(cells, axis, split_axis, concat_axis, tiled=True)  14.6 us
    reshape x4, local copies, waits for them, and re-layouts, transform_inverse(): spectrum.reshape(components, owned_height_lines + 2, period_extent_first,...  14.3 us
  transfers between devices with their start and end apart: 13, of which 6 were waited for; matrix products, arithmetic and copies ran while one was open for 2% of the time, Pallas kernels for 0%

profile of v6, /device:TPU:1, one launch (start us, length us, event | category | flops | bytes accessed | tf_op | source)
XLA Modules:
  0.0 643.2 jit_solution(4080983562705078370)
XLA Ops:
  1.6 7.7 %collective-permute-start.2 = (f32[5,1,1,256]{3,2,1,0:T(1,128)S(1)}, f32[5,1,1,256]{3,2,1,0:T(1,128)S(1)}, u32[]{:S(2)}, u32[]{:S(2)}) collective-permute-start(f32[5,1,1,256]{3,2,1,0:T(1,128)S(1)} %get-tuple-element.57), channel_id=1, source_target_pairs={{0,31},{1,16},{2,17},{3,18},{4,19},{5,20},{6,21},{7,22},{8,23},{9,... | collective-permute-start | bytes 15368 | tf_op jit(solution)/shard_map/ppermute | solution.py:45
  11.5 6.8 %collective-permute-start.4 = (f32[5,8,1,256]{3,2,1,0:T(1,128)S(1)}, f32[5,8,1,256]{3,2,1,0:T(1,128)S(1)}, u32[]{:S(2)}, u32[]{:S(2)}) collective-permute-start(f32[5,8,1,256]{3,2,1,0:T(1,128)S(1)} %get-tuple-element.62), channel_id=1, source_target_pairs={{0,15},{1,0},{2,1},{3,2},{4,3},{5,4},{6,5},{7,6},{8,7},{9,8},{10,9... | collective-permute-start | bytes 122888 | tf_op jit(solution)/shard_map/ppermute | solution.py:71
  42.7 8.2 %all-to-all-start = ((f32[16,1,3072]{2,1,0:T(1,128)}), f32[16,1,3072]{2,1,0:T(1,128)S(1)}, u32[]{:S(2)}, u32[]{:S(2)}) async-start(f32[16,1,3072]{2,1,0:T(1,128)} %reshape.383), calls=%async_computation | async-start | bytes 393216 | tf_op jit(solution)/shard_map/all_to_all | solution.py:96
  53.7 7.3 %all-to-all-done = f32[16,1,3072]{2,1,0:T(1,128)S(1)} async-done(((f32[16,1,3072]{2,1,0:T(1,128)}), f32[16,1,3072]{2,1,0:T(1,128)S(1)}, u32[]{:S(2)}, u32[]{:S(2)}) %all-to-all-start) | async-done | bytes 196640 | tf_op jit(solution)/shard_map/all_to_all | solution.py:96
  93.5 7.9 %all-to-all-done.1 = f32[16,1,3072]{2,1,0:T(1,128)S(1)} async-done(((f32[16,1,3072]{2,1,0:T(1,128)}), f32[16,1,3072]{2,1,0:T(1,128)S(1)}, u32[]{:S(2)}, u32[]{:S(2)}) %all-to-all-start.1) | async-done | bytes 196640 | tf_op jit(solution)/shard_map/all_to_all | solution.py:96
  112.3 10.8 %all_to_all.258 = f32[4,160,128]{2,0,1:T(4,128)S(1)} all-to-all(f32[4,160,128]{2,0,1:T(4,128)S(1)} %concatenate.188.clone), channel_id=1, replica_groups=mesh['row'=16,'col'=16] {'col'}, dimensions={1} | all-to-all | bytes 655360 | tf_op jit(solution)/shard_map/all_to_all | solution.py:100
  129.4 25.2 %all_to_all.259 = f32[4,160,160]{2,0,1:T(4,128)S(1)} all-to-all(f32[4,160,160]{2,0,1:T(4,128)S(1)} %concatenate.189.clone), channel_id=1, replica_groups=mesh['row'=16,'col'=16] {'row'}, dimensions={1} | all-to-all | bytes 819200 | tf_op jit(solution)/shard_map/all_to_all | solution.py:100
  159.3 9.2 %fusion.29 = f32[3,10,10,256]{3,2,1,0:T(8,128)S(1)} fusion(f32[3,10,256,10]{3,2,1,0:T(8,128)} %reshape.348), kind=kOutput, calls=%fused_computation.56 | convolution fusion | flops 236912640 | bytes 614400 | tf_op jit(solution)/shard_map/kx,cyxz->cyzk/dot_general | solution.py:166
  180.7 6.5 %reshape.387 = f32[16,1,4096]{2,1,0:T(1,128)S(1)} reshape(f32[2048,4,8]{2,1,0:T(4,128)} %pad_bitcast_fusion.3) | data formatting | bytes 524288
  187.3 14.0 %all_to_all.260 = f32[16,1,4096]{2,1,0:T(1,128)S(1)} all-to-all(f32[16,1,4096]{2,1,0:T(1,128)S(1)} %reshape.387), channel_id=1, replica_groups=mesh['row'=16,'col'=16] {'row'}, dimensions={0} | all-to-all | bytes 524288 | tf_op jit(solution)/shard_map/all_to_all | solution.py:100
  202.4 6.3 reshape.388
  226.6 7.2 %reshape.389 = f32[16,1,4096]{2,1,0:T(1,128)} reshape(f32[2048,4,8]{2,1,0:T(4,128)} %pad_bitcast_fusion.2) | data formatting | bytes 524288
  239.8 6.3 all-to-all-done.5
  247.4 6.3 reshape.390
  261.3 11.1 %all_to_all.261 = f32[4,160,128]{2,0,1:T(4,128)S(1)} all-to-all(f32[4,160,128]{2,0,1:T(4,128)S(1)} %concatenate.198.clone), channel_id=1, replica_groups=mesh['row'=16,'col'=16] {'col'}, dimensions={1} | all-to-all | bytes 655360 | tf_op jit(solution)/shard_map/all_to_all | solution.py:100
  278.6 25.2 %all_to_all.262 = f32[4,160,160]{2,0,1:T(4,128)S(1)} all-to-all(f32[4,160,160]{2,0,1:T(4,128)S(1)} %concatenate.199.clone), channel_id=1, replica_groups=mesh['row'=16,'col'=16] {'row'}, dimensions={1} | all-to-all | bytes 819200 | tf_op jit(solution)/shard_map/all_to_all | solution.py:100
  309.9 9.2 %convolution_add_fusion.1 = f32[3,10,10,256]{3,2,1,0:T(8,128)S(1)} fusion(f32[3,10,256,10]{3,2,1,0:T(8,128)} %reshape.354, f32[3,10,10,256]{3,2,1,0:T(8,128)S(1)} %copy-done.2, f32[]{:T(128)S(6)} %div.64), kind=kOutput, calls=%fused_computation.10 | convolution fusion | flops 237066240 | bytes 921604 | tf_op jit(solution)/shard_map/kx,cyxz->cyzk/dot_general | solution.py:166
  327.9 12.3 %all-to-all-done.8 = f32[256,1,1]{2,1,0:T(1,128)S(1)} async-done(((f32[256,1,1]{2,1,0:T(1,128)}), f32[256,1,1]{2,1,0:T(1,128)S(1)}, u32[]{:S(2)}, u32[]{:S(2)}) %all-to-all-start.8) | async-done | bytes 1056 | tf_op jit(solution)/shard_map/all_to_all | solution.py:64
  354.2 13.6 %all_to_all.263 = f32[16,1,3072]{2,1,0:T(1,128)S(1)} all-to-all(f32[16,1,3072]{2,1,0:T(1,128)S(1)} %reshape.391), channel_id=1, replica_groups=mesh['row'=16,'col'=16] {'row'}, dimensions={0} | all-to-all | bytes 393216 | tf_op jit(solution)/shard_map/all_to_all | solution.py:96
  390.9 10.6 %all_to_all.264 = f32[16,1,3072]{2,1,0:T(1,128)S(1)} all-to-all(f32[16,1,3072]{2,1,0:T(1,128)S(1)} %reshape.393), channel_id=1, replica_groups=mesh['row'=16,'col'=16] {'col'}, dimensions={0} | all-to-all | bytes 393216 | tf_op jit(solution)/shard_map/all_to_all | solution.py:96
  413.1 10.9 %all_to_all.265 = f32[4,160,128]{2,0,1:T(4,128)S(1)} all-to-all(f32[4,160,128]{2,0,1:T(4,128)S(1)} %concatenate.213.clone), channel_id=1, replica_groups=mesh['row'=16,'col'=16] {'col'}, dimensions={1} | all-to-all | bytes 655360 | tf_op jit(solution)/shard_map/all_to_all | solution.py:100
  430.2 25.1 %all_to_all.266 = f32[4,160,160]{2,0,1:T(4,128)S(1)} all-to-all(f32[4,160,160]{2,0,1:T(4,128)S(1)} %concatenate.214.clone), channel_id=1, replica_groups=mesh['row'=16,'col'=16] {'row'}, dimensions={1} | all-to-all | bytes 819200 | tf_op jit(solution)/shard_map/all_to_all | solution.py:100
  460.0 9.2 %fusion.24 = f32[3,10,10,256]{3,2,1,0:T(8,128)S(1)} fusion(f32[3,10,256,10]{3,2,1,0:T(8,128)} %reshape.360), kind=kOutput, calls=%fused_computation.51 | convolution fusion | flops 236912640 | bytes 614400 | tf_op jit(solution)/shard_map/kx,cyxz->cyzk/dot_general | solution.py:166
  481.4 6.5 %reshape.395 = f32[16,1,4096]{2,1,0:T(1,128)S(1)} reshape(f32[2048,4,8]{2,1,0:T(4,128)} %pad_bitcast_fusion.1) | data formatting | bytes 524288
  487.9 14.0 %all_to_all.267 = f32[16,1,4096]{2,1,0:T(1,128)S(1)} all-to-all(f32[16,1,4096]{2,1,0:T(1,128)S(1)} %reshape.395), channel_id=1, replica_groups=mesh['row'=16,'col'=16] {'row'}, dimensions={0} | all-to-all | bytes 524288 | tf_op jit(solution)/shard_map/all_to_all | solution.py:100
  503.0 6.3 reshape.396
  525.6 7.2 %reshape.397 = f32[16,1,4096]{2,1,0:T(1,128)} reshape(f32[2048,4,8]{2,1,0:T(4,128)} %pad_bitcast_fusion) | data formatting | bytes 524288
  538.8 6.4 all-to-all-done.14
  560.2 11.1 %all_to_all.268 = f32[4,160,128]{2,0,1:T(4,128)S(1)} all-to-all(f32[4,160,128]{2,0,1:T(4,128)S(1)} %concatenate.223.clone), channel_id=1, replica_groups=mesh['row'=16,'col'=16] {'col'}, dimensions={1} | all-to-all | bytes 655360 | tf_op jit(solution)/shard_map/all_to_all | solution.py:100
  577.5 25.1 %all_to_all.269 = f32[4,160,160]{2,0,1:T(4,128)S(1)} all-to-all(f32[4,160,160]{2,0,1:T(4,128)S(1)} %concatenate.224.clone), channel_id=1, replica_groups=mesh['row'=16,'col'=16] {'row'}, dimensions={1} | all-to-all | bytes 819200 | tf_op jit(solution)/shard_map/all_to_all | solution.py:100
  608.8 9.2 %convolution_add_fusion = f32[3,10,10,256]{3,2,1,0:T(8,128)S(1)} fusion(f32[3,10,256,10]{3,2,1,0:T(8,128)} %reshape.366, f32[3,10,10,256]{3,2,1,0:T(8,128)S(1)} %copy-done.4, f32[]{:T(128)S(6)} %div.67), kind=kOutput, calls=%fused_computation.9 | convolution fusion | flops 237066240 | bytes 921604 | tf_op jit(solution)/shard_map/kx,cyxz->cyzk/dot_general | solution.py:166
  620.5 17.5 %all_to_all.270 = f32[256,1,1]{2,1,0:T(1,128)S(1)} all-to-all(f32[256,1,1]{2,1,0:T(1,128)S(1)} %broadcast_in_dim.11), channel_id=1, replica_groups=mesh['row'=16,'col'=16] {'row','col'}, dimensions={0} | all-to-all | bytes 2048 | tf_op jit(solution)/shard_map/all_to_all | solution.py:64
  (422 shorter events, 272.1 us)
Async XLA Ops:
  0.6 29.9 %copy-start = (f32[3,8,8,256]{3,2,1,0:T(8,128)S(1)}, f32[3,8,8,256]{3,2,1,0:T(8,128)}, u32[]{:S(2)}) copy-start(f32[3,8,8,256]{3,2,1,0:T(8,128)} %param.3) | copy-start | bytes 589828
  0.6 29.9 %copy-start.9 = (f32[8,8,256]{2,1,0:T(8,128)S(1)}, f32[8,8,256]{2,1,0:T(8,128)}, u32[]{:S(2)}) copy-start(f32[8,8,256]{2,1,0:T(8,128)} %param.5) | copy-start | bytes 196612
  0.7 29.9 %copy-start.15 = (f32[8,8,256]{2,1,0:T(8,128)S(1)}, f32[8,8,256]{2,1,0:T(8,128)}, u32[]{:S(2)}) copy-start(f32[8,8,256]{2,1,0:T(8,128)} %param.4) | copy-start | bytes 196612
  1.6 17.7 %collective-permute-start.2 = (f32[5,1,1,256]{3,2,1,0:T(1,128)S(1)}, f32[5,1,1,256]{3,2,1,0:T(1,128)S(1)}, u32[]{:S(2)}, u32[]{:S(2)}) collective-permute-start(f32[5,1,1,256]{3,2,1,0:T(1,128)S(1)} %get-tuple-element.57), channel_id=1, source_target_pairs={{0,31},{1,16},{2,17},{3,18},{4,19},{5,20},{6,21},{7,22},{8,23},{9,... | collective-permute-start | bytes 15368 | tf_op jit(solution)/shard_map/ppermute | solution.py:45
  9.3 10.0 %collective-permute-start = (f32[5,1,1,256]{3,2,1,0:T(1,128)S(1)}, f32[5,1,1,256]{3,2,1,0:T(1,128)S(1)}, u32[]{:S(2)}, u32[]{:S(2)}) collective-permute-start(f32[5,1,1,256]{3,2,1,0:T(1,128)S(1)} %get-tuple-element.58), channel_id=1, source_target_pairs={{0,17},{1,18},{2,19},{3,20},{4,21},{5,22},{6,23},{7,24},{8,25},{9,... | collective-permute-start | bytes 15368 | tf_op jit(solution)/shard_map/ppermute | solution.py:45
  10.2 15.0 %collective-permute-start.1 = (f32[5,1,8,256]{3,2,1,0:T(8,128)S(1)}, f32[5,1,8,256]{3,2,1,0:T(8,128)S(1)}, u32[]{:S(2)}, u32[]{:S(2)}) collective-permute-start(f32[5,1,8,256]{3,2,1,0:T(8,128)S(1)} %get-tuple-element.60), channel_id=1, source_target_pairs={{0,16},{16,32},{32,48},{48,64},{64,80},{80,96},{96,112},{112,128},... | collective-permute-start | bytes 122888 | tf_op jit(solution)/shard_map/ppermute | solution.py:71
  11.4 15.3 %collective-permute-start.3 = (f32[5,8,1,256]{3,2,1,0:T(1,128)S(1)}, f32[5,8,1,256]{3,2,1,0:T(1,128)S(1)}, u32[]{:S(2)}, u32[]{:S(2)}) collective-permute-start(f32[5,8,1,256]{3,2,1,0:T(1,128)S(1)} %get-tuple-element.61), channel_id=1, source_target_pairs={{0,1},{1,2},{2,3},{3,4},{4,5},{5,6},{6,7},{7,8},{8,9},{9,10},{10,1... | collective-permute-start | bytes 122888 | tf_op jit(solution)/shard_map/ppermute | solution.py:71
  11.5 15.2 %collective-permute-start.4 = (f32[5,8,1,256]{3,2,1,0:T(1,128)S(1)}, f32[5,8,1,256]{3,2,1,0:T(1,128)S(1)}, u32[]{:S(2)}, u32[]{:S(2)}) collective-permute-start(f32[5,8,1,256]{3,2,1,0:T(1,128)S(1)} %get-tuple-element.62), channel_id=1, source_target_pairs={{0,15},{1,0},{2,1},{3,2},{4,3},{5,4},{6,5},{7,6},{8,7},{9,8},{10,9... | collective-permute-start | bytes 122888 | tf_op jit(solution)/shard_map/ppermute | solution.py:71
  19.1 12.7 %copy-start.42 = (f32[1,8,8,256]{3,2,1,0:T(8,128)}, f32[1,8,8,256]{3,2,1,0:T(8,128)S(1)}, u32[]{:S(2)}) copy-start(f32[1,8,8,256]{3,2,1,0:T(8,128)S(1)} %add_bitcast_fusion) | copy-start | bytes 196612
  19.3 11.7 %copy-start.34 = (f32[5,1,1,256]{3,2,1,0:T(1,128)}, f32[5,1,1,256]{3,2,1,0:T(1,128)S(1)}, u32[]{:S(2)}) copy-start(f32[5,1,1,256]{3,2,1,0:T(1,128)S(1)} %collective-permute-done.2) | copy-start | bytes 15364
  19.3 8.5 %collective-permute-start.5 = (f32[5,1,1,256]{3,2,1,0:T(1,128)S(1)}, f32[5,1,1,256]{3,2,1,0:T(1,128)S(1)}, u32[]{:S(2)}, u32[]{:S(2)}) collective-permute-start(f32[5,1,1,256]{3,2,1,0:T(1,128)S(1)} %get-tuple-element.55), channel_id=1, source_target_pairs={{0,241},{1,242},{2,243},{3,244},{4,245},{5,246},{6,247},{7,248},{8... | collective-permute-start | bytes 15368 | tf_op jit(solution)/shard_map/ppermute | solution.py:45
  19.3 11.6 %copy-start.36 = (f32[5,1,1,256]{3,2,1,0:T(1,128)}, f32[5,1,1,256]{3,2,1,0:T(1,128)S(1)}, u32[]{:S(2)}) copy-start(f32[5,1,1,256]{3,2,1,0:T(1,128)S(1)} %collective-permute-done) | copy-start | bytes 15364
  19.3 8.4 %collective-permute-start.7 = (f32[5,1,1,256]{3,2,1,0:T(1,128)S(1)}, f32[5,1,1,256]{3,2,1,0:T(1,128)S(1)}, u32[]{:S(2)}, u32[]{:S(2)}) collective-permute-start(f32[5,1,1,256]{3,2,1,0:T(1,128)S(1)} %get-tuple-element.56), channel_id=1, source_target_pairs={{0,255},{1,240},{2,241},{3,242},{4,243},{5,244},{6,245},{7,246},{8... | collective-permute-start | bytes 15368 | tf_op jit(solution)/shard_map/ppermute | solution.py:45
  25.1 3.4 collective-permute-start.6
  42.7 18.3 %all-to-all-start = ((f32[16,1,3072]{2,1,0:T(1,128)}), f32[16,1,3072]{2,1,0:T(1,128)S(1)}, u32[]{:S(2)}, u32[]{:S(2)}) async-start(f32[16,1,3072]{2,1,0:T(1,128)} %reshape.383), calls=%async_computation | async-start | bytes 393216 | tf_op jit(solution)/shard_map/all_to_all | solution.py:96
  79.4 13.9 %copy-start.44 = (f32[128]{0:T(128)S(1)}, f32[128]{0:T(128)}, u32[]{:S(2)}) copy-start(f32[128]{0:T(128)} %add.559) | copy-start | bytes 1540
  79.4 13.9 %copy-start.45 = (f32[128]{0:T(128)S(1)}, f32[128]{0:T(128)}, u32[]{:S(2)}) copy-start(f32[128]{0:T(128)} %multiply_subtract_fusion.2) | copy-start | bytes 1540
  89.0 12.3 %all-to-all-start.1 = ((f32[16,1,3072]{2,1,0:T(1,128)}), f32[16,1,3072]{2,1,0:T(1,128)S(1)}, u32[]{:S(2)}, u32[]{:S(2)}) async-start(f32[16,1,3072]{2,1,0:T(1,128)} %reshape.385), calls=%async_computation.1 | async-start | bytes 393216 | tf_op jit(solution)/shard_map/all_to_all | solution.py:96
  93.4 17.6 %copy-start.12 = (f32[128,128]{0,1:T(8,128)}, f32[128,128]{0,1:T(8,128)S(1)}, u32[]{:S(2)}) copy-start(f32[128,128]{0,1:T(8,128)S(1)} %add_divide_fusion) | copy-start | bytes 196612
  102.3 8.7 %copy-start.5 = (f32[160,128]{1,0:T(8,128)S(1)}, f32[160,128]{1,0:T(8,128)}, u32[]{:S(2)}) copy-start(f32[160,128]{1,0:T(8,128)} %gather_fusion) | copy-start | bytes 245764
  111.0 13.1 %copy-start.23 = (f32[3,128,128]{1,2,0:T(8,128)}, f32[3,128,128]{1,2,0:T(8,128)S(1)}, u32[]{:S(2)}) copy-start(f32[3,128,128]{1,2,0:T(8,128)S(1)} %get-tuple-element.94) | copy-start | bytes 589828
  233.7 12.4 %all-to-all-start.5 = ((f32[16,1,4096]{2,1,0:T(1,128)}), f32[16,1,4096]{2,1,0:T(1,128)S(1)}, u32[]{:S(2)}, u32[]{:S(2)}) async-start(f32[16,1,4096]{2,1,0:T(1,128)} %reshape.389), calls=%async_computation.5 | async-start | bytes 524288 | tf_op jit(solution)/shard_map/all_to_all | solution.py:100
  247.3 11.3 %copy-start.13 = (f32[128,128]{0,1:T(8,128)S(1)}, f32[128,128]{0,1:T(8,128)}, u32[]{:S(2)}) copy-start(f32[128,128]{0,1:T(8,128)} %copy-done.12) | copy-start | bytes 196612
  247.4 11.3 %copy-start.24 = (f32[3,128,128]{1,2,0:T(8,128)S(1)}, f32[3,128,128]{1,2,0:T(8,128)}, u32[]{:S(2)}) copy-start(f32[3,128,128]{1,2,0:T(8,128)} %copy-done.23) | copy-start | bytes 589828
  278.6 31.4 %copy-start.2 = (f32[3,10,10,256]{3,2,1,0:T(8,128)S(1)}, f32[3,10,10,256]{3,2,1,0:T(8,128)}, u32[]{:S(2)}) copy-start(f32[3,10,10,256]{3,2,1,0:T(8,128)} %copy-done.1) | copy-start | bytes 921604
  322.5 17.7 %all-to-all-start.8 = ((f32[256,1,1]{2,1,0:T(1,128)}), f32[256,1,1]{2,1,0:T(1,128)S(1)}, u32[]{:S(2)}, u32[]{:S(2)}) async-start(f32[256,1,1]{2,1,0:T(1,128)} %broadcast_in_dim.10), calls=%async_computation.8 | async-start | bytes 262144 | tf_op jit(solution)/shard_map/all_to_all | solution.py:64
  327.7 15.5 %copy-start.20 = (f32[9,9,256]{2,1,0:T(8,128)S(1)}, f32[9,9,256]{2,1,0:T(8,128)}, u32[]{:S(2)}) copy-start(f32[9,9,256]{2,1,0:T(8,128)} %copy-done.19) | copy-start | bytes 248836
  402.5 9.3 %copy-start.7 = (f32[160,128]{1,0:T(8,128)S(1)}, f32[160,128]{1,0:T(8,128)}, u32[]{:S(2)}) copy-start(f32[160,128]{1,0:T(8,128)} %gather_fusion) | copy-start | bytes 245764
  532.7 12.4 %all-to-all-start.14 = ((f32[16,1,4096]{2,1,0:T(1,128)}), f32[16,1,4096]{2,1,0:T(1,128)S(1)}, u32[]{:S(2)}, u32[]{:S(2)}) async-start(f32[16,1,4096]{2,1,0:T(1,128)} %reshape.397), calls=%async_computation.14 | async-start | bytes 524288 | tf_op jit(solution)/shard_map/all_to_all | solution.py:100
  546.3 11.2 %copy-start.22 = (f32[3,128,128]{1,2,0:T(8,128)S(1)}, f32[3,128,128]{1,2,0:T(8,128)}, u32[]{:S(2)}) copy-start(f32[3,128,128]{1,2,0:T(8,128)} %copy-done.21) | copy-start | bytes 589828
  577.5 31.3 %copy-start.4 = (f32[3,10,10,256]{3,2,1,0:T(8,128)S(1)}, f32[3,10,10,256]{3,2,1,0:T(8,128)}, u32[]{:S(2)}) copy-start(f32[3,10,10,256]{3,2,1,0:T(8,128)} %copy-done.3) | copy-start | bytes 921604
  618.3 22.0 %copy-start.11 = (f32[3,10,10,256]{3,2,1,0:T(8,128)S(1)}, f32[3,10,10,256]{3,2,1,0:T(8,128)}, u32[]{:S(2)}) copy-start(f32[3,10,10,256]{3,2,1,0:T(8,128)} %copy-done.10) | copy-start | bytes 921604
  (27 other events, 129.0 us)

commit v7 on v4

--- a/solution.py
+++ b/solution.py
@@ -79,6 +79,20 @@
     return moved[:-1], jnp.sum(arrived)
 
 
+def carried(cells, axis, split_axis, concat_axis):
+    count = lax.axis_size(axis)
+    moved = lax.all_to_all(cells, axis, split_axis, concat_axis, tiled=True)
+    arrived = jnp.moveaxis(moved[-1], concat_axis - 1, 0)
+    arrived = arrived.reshape(count, arrived.shape[0] // count, -1)[:, 0, 0]
+    return moved[:-1], jnp.sum(arrived)
+
+
+def with_pulse(cells, partial, dim):
+    place = lax.broadcasted_iota(jnp.int32, (1,) + cells.shape[1:], dim)
+    pulse = jnp.where(place == 0, partial.astype(cells.dtype), jnp.zeros((), cells.dtype))
+    return jnp.concatenate([cells, pulse], 0)
+
+
 def spectral_symbol(shape):
     row_count = lax.axis_size("row")
     col_count = lax.axis_size("col")
@@ -101,10 +115,15 @@
     components, owned_height_lines, owned_depth_slices, period_extent_first = residual.shape
     ylength = owned_height_lines * row_count
     xpiece = period_extent_first // row_count
+    if partial is not None:
+        residual = with_pulse(residual, partial, 3)
     spectrum = jnp.einsum("kx,cyzx->cykz", xtable, residual, precision=PRECISE).reshape(
-        components, owned_height_lines, period_extent_first * owned_depth_slices
-    )
-    spectrum, partial = exchange(spectrum, partial, "row", 2, 1)
+        residual.shape[0], owned_height_lines, period_extent_first * owned_depth_slices
+    )
+    if partial is None:
+        spectrum, partial = exchange(spectrum, None, "row", 2, 1)
+    else:
+        spectrum, partial = carried(spectrum, "row", 2, 1)
     spectrum = jnp.einsum(
         "ky,cyxz->czkx",
         ytable,
@@ -124,8 +143,10 @@
     xpiece = period_extent_first // row_count
     zwide = widened(ztable, col_count)
     ywide = widened(ytable, row_count)
-    spectrum = jnp.einsum("kz,czm->ckm", zwide, filtered, precision=PRECISE)
-    spectrum, partial = exchange(spectrum, partial, "col", 1, 2)
+    spectrum = jnp.einsum(
+        "kz,czm->ckm", zwide, with_pulse(filtered, partial, 1), precision=PRECISE
+    )
+    spectrum, partial = carried(spectrum, "col", 1, 2)
     spectrum = jnp.einsum(
         "ky,czyx->ckxz",
         ywide,

time: 643 us -> 638 us (level)
  local copies, waits for them, and re-layouts: 220 us -> 211 us
    all_to_all x0 -> x6, blocking collectives: none -> 72.1 us  [carried(): moved = lax.all_to_all(cells, axis, split_axis, concat_axis, tiled=True)]
    all_to_all x10 -> x4, blocking collectives: 172 us -> 101 us  [exchange(): lax.all_to_all(jnp.concatenate([cells, rider], 0), axis, split_axis, conc...]
    unnamed x102 -> x94, local copies, waits for them, and re-layouts: 126 us -> 107 us
    reshape x2 -> x4, local copies, waits for them, and re-layouts: 8.64 us -> 17.4 us  [transform_forward(): jnp.einsum('kx,cyzx->cykz', xtable, residual, precision=PRECISE)]
where the time goes in v7:
time: 638 us; the launch traced here: 631 us
  blocking collectives  214 us (34%)
  local copies, waits for them, and re-layouts  211 us (33%)
  matrix products  78.4 us (12%)
  waiting for transfers between devices  44.3 us (7%)
  starting transfers between devices  36.6 us (6%)
  other arithmetic  35.8 us (6%)
  between operations  10.8 us (2%)
    unnamed x94, local copies, waits for them, and re-layouts  107 us
    all_to_all x4, blocking collectives, exchange(): lax.all_to_all(jnp.concatenate([cells, rider], 0), axis, split_axis, conc...  101 us
    all_to_all x6, blocking collectives, carried(): moved = lax.all_to_all(cells, axis, split_axis, concat_axis, tiled=True)  72.1 us
    dot_general x4, matrix products, transform_inverse(): jnp.einsum('kx,cyxz->cyzk', xtable, spectrum.reshape(components, owned_he...  36.7 us
    all_to_all x2, blocking collectives, exchange(): moved = lax.all_to_all(cells, axis, split_axis, concat_axis, tiled=True)  24.2 us
    all_to_all x1, blocking collectives, global_sum(): gathered = lax.all_to_all(spread, ('row', 'col'), 0, 0, tiled=True)  17.5 us
    reshape x4, local copies, waits for them, and re-layouts, transform_forward(): jnp.einsum('kx,cyzx->cykz', xtable, residual, precision=PRECISE)  17.4 us
    all_to_all x5, local copies, waits for them, and re-layouts, exchange(): moved = lax.all_to_all(cells, axis, split_axis, concat_axis, tiled=True)  15.6 us
  transfers between devices with their start and end apart: 9, of which 7 were waited for; matrix products, arithmetic and copies ran while one was open for 1% of the time, Pallas kernels for 0%

profile of v7, /device:TPU:1, one launch (start us, length us, event | category | flops | bytes accessed | tf_op | source)
XLA Modules:
  0.0 630.9 jit_solution(11685544009562456019)
XLA Ops:
  30.8 9.7 %all-to-all-start = ((f32[16,1,3072]{2,1,0:T(1,128)}), f32[16,1,3072]{2,1,0:T(1,128)S(1)}, u32[]{:S(2)}, u32[]{:S(2)}) async-start(f32[16,1,3072]{2,1,0:T(1,128)} %reshape.415), calls=%async_computation | async-start | bytes 393216 | tf_op jit(solution)/shard_map/all_to_all | solution.py:70
  43.3 7.3 %all-to-all-done = f32[16,1,3072]{2,1,0:T(1,128)S(1)} async-done(((f32[16,1,3072]{2,1,0:T(1,128)}), f32[16,1,3072]{2,1,0:T(1,128)S(1)}, u32[]{:S(2)}, u32[]{:S(2)}) %all-to-all-start) | async-done | bytes 196640 | tf_op jit(solution)/shard_map/all_to_all | solution.py:70
  63.1 5.9 fusion.8
  84.3 7.9 %all-to-all-done.1 = f32[16,1,3072]{2,1,0:T(1,128)S(1)} async-done(((f32[16,1,3072]{2,1,0:T(1,128)}), f32[16,1,3072]{2,1,0:T(1,128)S(1)}, u32[]{:S(2)}, u32[]{:S(2)}) %all-to-all-start.1) | async-done | bytes 196640 | tf_op jit(solution)/shard_map/all_to_all | solution.py:70
  103.9 10.7 %all_to_all.258 = f32[4,160,128]{2,0,1:T(4,128)S(1)} all-to-all(f32[4,160,128]{2,0,1:T(4,128)S(1)} %copy.244), channel_id=1, replica_groups=mesh['row'=16,'col'=16] {'col'}, dimensions={1} | all-to-all | bytes 655360 | tf_op jit(solution)/shard_map/all_to_all | solution.py:84
  120.8 25.2 %all_to_all.259 = f32[4,160,160]{2,0,1:T(4,128)S(1)} all-to-all(f32[4,160,160]{2,0,1:T(4,128)S(1)} %concatenate.183.clone), channel_id=1, replica_groups=mesh['row'=16,'col'=16] {'row'}, dimensions={1} | all-to-all | bytes 819200 | tf_op jit(solution)/shard_map/all_to_all | solution.py:74
  150.7 9.2 %fusion.51 = f32[3,10,10,256]{3,2,1,0:T(8,128)S(1)} fusion(f32[3,10,256,10]{3,2,1,0:T(8,128)} %reshape.374), kind=kOutput, calls=%fused_computation.74 | convolution fusion | flops 236912640 | bytes 614400 | tf_op jit(solution)/shard_map/kx,cyxz->cyzk/dot_general | solution.py:157
  168.3 6.5 %reshape.419 = f32[16,1,4096]{2,1,0:T(1,128)S(1)} reshape(f32[2048,4,8]{2,1,0:T(4,128)} %bitcast.537) | data formatting | bytes 524288
  174.8 14.2 %all_to_all.260 = f32[16,1,4096]{2,1,0:T(1,128)S(1)} all-to-all(f32[16,1,4096]{2,1,0:T(1,128)S(1)} %reshape.419), channel_id=1, replica_groups=mesh['row'=16,'col'=16] {'row'}, dimensions={0} | all-to-all | bytes 524288 | tf_op jit(solution)/shard_map/all_to_all | solution.py:84
  190.2 6.3 reshape.420
  214.2 7.1 %reshape.421 = f32[16,1,4096]{2,1,0:T(1,128)} reshape(f32[2048,4,8]{2,1,0:T(4,128)} %pad_bitcast_fusion.1) | data formatting | bytes 524288
  227.4 6.6 %all-to-all-done.5 = f32[16,1,4096]{2,1,0:T(1,128)S(1)} async-done(((f32[16,1,4096]{2,1,0:T(1,128)}), f32[16,1,4096]{2,1,0:T(1,128)S(1)}, u32[]{:S(2)}, u32[]{:S(2)}) %all-to-all-start.5) | async-done | bytes 262176 | tf_op jit(solution)/shard_map/all_to_all | solution.py:74
  235.2 6.3 reshape.422
  249.0 11.1 %all_to_all.261 = f32[4,160,128]{2,0,1:T(4,128)S(1)} all-to-all(f32[4,160,128]{2,0,1:T(4,128)S(1)} %copy.264), channel_id=1, replica_groups=mesh['row'=16,'col'=16] {'col'}, dimensions={1} | all-to-all | bytes 655360 | tf_op jit(solution)/shard_map/all_to_all | solution.py:84
  266.1 25.1 %all_to_all.262 = f32[4,160,160]{2,0,1:T(4,128)S(1)} all-to-all(f32[4,160,160]{2,0,1:T(4,128)S(1)} %concatenate.193.clone), channel_id=1, replica_groups=mesh['row'=16,'col'=16] {'row'}, dimensions={1} | all-to-all | bytes 819200 | tf_op jit(solution)/shard_map/all_to_all | solution.py:74
  297.3 9.2 %convolution_add_fusion.1 = f32[3,10,10,256]{3,2,1,0:T(8,128)S(1)} fusion(f32[3,10,256,10]{3,2,1,0:T(8,128)} %reshape.382, f32[3,10,10,256]{3,2,1,0:T(8,128)S(1)} %copy-done.2, f32[]{:T(128)S(6)} %div.64), kind=kOutput, calls=%fused_computation.10 | convolution fusion | flops 237066240 | bytes 921604 | tf_op jit(solution)/shard_map/kx,cyxz->cyzk/dot_general | solution.py:157
  315.2 12.4 %all-to-all-done.8 = f32[256,1,1]{2,1,0:T(1,128)S(1)} async-done(((f32[256,1,1]{2,1,0:T(1,128)}), f32[256,1,1]{2,1,0:T(1,128)S(1)}, u32[]{:S(2)}, u32[]{:S(2)}) %all-to-all-start.8) | async-done | bytes 1056 | tf_op jit(solution)/shard_map/all_to_all | solution.py:38
  341.5 13.6 %all_to_all.263 = f32[16,1,3072]{2,1,0:T(1,128)S(1)} all-to-all(f32[16,1,3072]{2,1,0:T(1,128)S(1)} %reshape.423), channel_id=1, replica_groups=mesh['row'=16,'col'=16] {'row'}, dimensions={0} | all-to-all | bytes 393216 | tf_op jit(solution)/shard_map/all_to_all | solution.py:70
  381.9 10.6 %all_to_all.264 = f32[16,1,3072]{2,1,0:T(1,128)S(1)} all-to-all(f32[16,1,3072]{2,1,0:T(1,128)S(1)} %reshape.425), channel_id=1, replica_groups=mesh['row'=16,'col'=16] {'col'}, dimensions={0} | all-to-all | bytes 393216 | tf_op jit(solution)/shard_map/all_to_all | solution.py:70
  404.1 10.9 %all_to_all.265 = f32[4,160,128]{2,0,1:T(4,128)S(1)} all-to-all(f32[4,160,128]{2,0,1:T(4,128)S(1)} %copy.285), channel_id=1, replica_groups=mesh['row'=16,'col'=16] {'col'}, dimensions={1} | all-to-all | bytes 655360 | tf_op jit(solution)/shard_map/all_to_all | solution.py:84
  420.9 25.1 %all_to_all.266 = f32[4,160,160]{2,0,1:T(4,128)S(1)} all-to-all(f32[4,160,160]{2,0,1:T(4,128)S(1)} %concatenate.208.clone), channel_id=1, replica_groups=mesh['row'=16,'col'=16] {'row'}, dimensions={1} | all-to-all | bytes 819200 | tf_op jit(solution)/shard_map/all_to_all | solution.py:74
  450.7 9.2 %fusion.46 = f32[3,10,10,256]{3,2,1,0:T(8,128)S(1)} fusion(f32[3,10,256,10]{3,2,1,0:T(8,128)} %reshape.390), kind=kOutput, calls=%fused_computation.69 | convolution fusion | flops 236912640 | bytes 614400 | tf_op jit(solution)/shard_map/kx,cyxz->cyzk/dot_general | solution.py:157
  468.2 6.5 %reshape.427 = f32[16,1,4096]{2,1,0:T(1,128)S(1)} reshape(f32[2048,4,8]{2,1,0:T(4,128)} %bitcast.544) | data formatting | bytes 524288
  474.7 14.2 %all_to_all.267 = f32[16,1,4096]{2,1,0:T(1,128)S(1)} all-to-all(f32[16,1,4096]{2,1,0:T(1,128)S(1)} %reshape.427), channel_id=1, replica_groups=mesh['row'=16,'col'=16] {'row'}, dimensions={0} | all-to-all | bytes 524288 | tf_op jit(solution)/shard_map/all_to_all | solution.py:84
  490.1 6.3 reshape.428
  514.2 7.1 %reshape.429 = f32[16,1,4096]{2,1,0:T(1,128)} reshape(f32[2048,4,8]{2,1,0:T(4,128)} %pad_bitcast_fusion) | data formatting | bytes 524288
  527.4 6.5 %all-to-all-done.14 = f32[16,1,4096]{2,1,0:T(1,128)S(1)} async-done(((f32[16,1,4096]{2,1,0:T(1,128)}), f32[16,1,4096]{2,1,0:T(1,128)S(1)}, u32[]{:S(2)}, u32[]{:S(2)}) %all-to-all-start.14) | async-done | bytes 262176 | tf_op jit(solution)/shard_map/all_to_all | solution.py:74
  535.2 6.3 reshape.430
  549.1 11.0 %all_to_all.268 = f32[4,160,128]{2,0,1:T(4,128)S(1)} all-to-all(f32[4,160,128]{2,0,1:T(4,128)S(1)} %copy.305), channel_id=1, replica_groups=mesh['row'=16,'col'=16] {'col'}, dimensions={1} | all-to-all | bytes 655360 | tf_op jit(solution)/shard_map/all_to_all | solution.py:84
  566.1 25.1 %all_to_all.269 = f32[4,160,160]{2,0,1:T(4,128)S(1)} all-to-all(f32[4,160,160]{2,0,1:T(4,128)S(1)} %concatenate.218.clone), channel_id=1, replica_groups=mesh['row'=16,'col'=16] {'row'}, dimensions={1} | all-to-all | bytes 819200 | tf_op jit(solution)/shard_map/all_to_all | solution.py:74
  597.4 9.2 %convolution_add_fusion = f32[3,10,10,256]{3,2,1,0:T(8,128)S(1)} fusion(f32[3,10,256,10]{3,2,1,0:T(8,128)} %reshape.398, f32[3,10,10,256]{3,2,1,0:T(8,128)S(1)} %copy-done.4, f32[]{:T(128)S(6)} %div.67), kind=kOutput, calls=%fused_computation.9 | convolution fusion | flops 237066240 | bytes 921604 | tf_op jit(solution)/shard_map/kx,cyxz->cyzk/dot_general | solution.py:157
  609.2 17.5 %all_to_all.270 = f32[256,1,1]{2,1,0:T(1,128)S(1)} all-to-all(f32[256,1,1]{2,1,0:T(1,128)S(1)} %broadcast_in_dim.86), channel_id=1, replica_groups=mesh['row'=16,'col'=16] {'row','col'}, dimensions={0} | all-to-all | bytes 2048 | tf_op jit(solution)/shard_map/all_to_all | solution.py:38
  (380 shorter events, 260.3 us)
Async XLA Ops:
  0.6 18.3 %copy-start = (f32[3,8,8,256]{3,2,1,0:T(8,128)S(1)}, f32[3,8,8,256]{3,2,1,0:T(8,128)}, u32[]{:S(2)}) copy-start(f32[3,8,8,256]{3,2,1,0:T(8,128)} %param.3) | copy-start | bytes 589828
  0.6 18.3 %copy-start.10 = (f32[8,8,256]{2,1,0:T(8,128)S(1)}, f32[8,8,256]{2,1,0:T(8,128)}, u32[]{:S(2)}) copy-start(f32[8,8,256]{2,1,0:T(8,128)} %param.5) | copy-start | bytes 196612
  0.7 18.3 %copy-start.13 = (f32[8,8,256]{2,1,0:T(8,128)S(1)}, f32[8,8,256]{2,1,0:T(8,128)}, u32[]{:S(2)}) copy-start(f32[8,8,256]{2,1,0:T(8,128)} %param.4) | copy-start | bytes 196612
  1.5 4.2 collective-permute-start
  4.6 3.4 collective-permute-start.1
  5.6 14.3 %copy-start.31 = (f32[1,8,8,256]{3,2,1,0:T(8,128)}, f32[1,8,8,256]{3,2,1,0:T(8,128)S(1)}, u32[]{:S(2)}) copy-start(f32[1,8,8,256]{3,2,1,0:T(8,128)S(1)} %add_bitcast_fusion) | copy-start | bytes 196612
  5.7 13.6 %copy-start.21 = (f32[5,1,8,256]{3,2,1,0:T(8,128)}, f32[5,1,8,256]{3,2,1,0:T(8,128)S(1)}, u32[]{:S(2)}) copy-start(f32[5,1,8,256]{3,2,1,0:T(8,128)S(1)} %collective-permute-done) | copy-start | bytes 122884
  8.0 11.4 %copy-start.23 = (f32[5,1,8,256]{3,2,1,0:T(8,128)}, f32[5,1,8,256]{3,2,1,0:T(8,128)S(1)}, u32[]{:S(2)}) copy-start(f32[5,1,8,256]{3,2,1,0:T(8,128)S(1)} %collective-permute-done.1) | copy-start | bytes 122884
  9.2 6.5 %collective-permute-start.2 = (f32[5,10,1,256]{3,2,1,0:T(1,128)S(1)}, f32[5,10,1,256]{3,2,1,0:T(1,128)S(1)}, u32[]{:S(2)}, u32[]{:S(2)}) collective-permute-start(f32[5,10,1,256]{3,2,1,0:T(1,128)S(1)} %get-tuple-element.56), channel_id=1, source_target_pairs={{0,1},{1,2},{2,3},{3,4},{4,5},{5,6},{6,7},{7,8},{8,9},{9,10},{10,1... | collective-permute-start | bytes 153608 | tf_op jit(solution)/shard_map/ppermute | solution.py:26
  10.6 6.1 collective-permute-start.3
  30.8 19.8 %all-to-all-start = ((f32[16,1,3072]{2,1,0:T(1,128)}), f32[16,1,3072]{2,1,0:T(1,128)S(1)}, u32[]{:S(2)}, u32[]{:S(2)}) async-start(f32[16,1,3072]{2,1,0:T(1,128)} %reshape.415), calls=%async_computation | async-start | bytes 393216 | tf_op jit(solution)/shard_map/all_to_all | solution.py:70
  69.0 15.1 %copy-start.33 = (f32[128]{0:T(128)S(1)}, f32[128]{0:T(128)}, u32[]{:S(2)}) copy-start(f32[128]{0:T(128)} %add.547) | copy-start | bytes 1540
  69.0 15.2 %copy-start.34 = (f32[128]{0:T(128)S(1)}, f32[128]{0:T(128)}, u32[]{:S(2)}) copy-start(f32[128]{0:T(128)} %multiply_subtract_fusion.2) | copy-start | bytes 1540
  78.6 13.5 %all-to-all-start.1 = ((f32[16,1,3072]{2,1,0:T(1,128)}), f32[16,1,3072]{2,1,0:T(1,128)S(1)}, u32[]{:S(2)}, u32[]{:S(2)}) async-start(f32[16,1,3072]{2,1,0:T(1,128)} %reshape.417), calls=%async_computation.1 | async-start | bytes 393216 | tf_op jit(solution)/shard_map/all_to_all | solution.py:70
  84.2 16.2 %copy-start.17 = (f32[128,128]{0,1:T(8,128)}, f32[128,128]{0,1:T(8,128)S(1)}, u32[]{:S(2)}) copy-start(f32[128,128]{0,1:T(8,128)S(1)} %add_divide_fusion) | copy-start | bytes 196612
  93.1 10.1 %copy-start.5 = (f32[160,128]{1,0:T(8,128)S(1)}, f32[160,128]{1,0:T(8,128)}, u32[]{:S(2)}) copy-start(f32[160,128]{1,0:T(8,128)} %gather_fusion) | copy-start | bytes 245764
  221.3 12.7 %all-to-all-start.5 = ((f32[16,1,4096]{2,1,0:T(1,128)}), f32[16,1,4096]{2,1,0:T(1,128)S(1)}, u32[]{:S(2)}, u32[]{:S(2)}) async-start(f32[16,1,4096]{2,1,0:T(1,128)} %reshape.421), calls=%async_computation.5 | async-start | bytes 524288 | tf_op jit(solution)/shard_map/all_to_all | solution.py:74
  235.1 11.2 %copy-start.18 = (f32[128,128]{0,1:T(8,128)S(1)}, f32[128,128]{0,1:T(8,128)}, u32[]{:S(2)}) copy-start(f32[128,128]{0,1:T(8,128)} %copy-done.17) | copy-start | bytes 196612
  235.1 11.2 %copy-start.28 = (f32[3,128,128]{1,2,0:T(8,128)S(1)}, f32[3,128,128]{1,2,0:T(8,128)}, u32[]{:S(2)}) copy-start(f32[3,128,128]{1,2,0:T(8,128)} %get-tuple-element.99) | copy-start | bytes 589828
  266.1 31.2 %copy-start.2 = (f32[3,10,10,256]{3,2,1,0:T(8,128)S(1)}, f32[3,10,10,256]{3,2,1,0:T(8,128)}, u32[]{:S(2)}) copy-start(f32[3,10,10,256]{3,2,1,0:T(8,128)} %copy-done.1) | copy-start | bytes 921604
  306.7 8.3 %copy-start.14 = (f32[8,8,256]{2,1,0:T(8,128)S(1)}, f32[8,8,256]{2,1,0:T(8,128)}, u32[]{:S(2)}) copy-start(f32[8,8,256]{2,1,0:T(8,128)} %param.4) | copy-start | bytes 196612
  306.7 8.3 %copy-start.22 = (f32[5,1,8,256]{3,2,1,0:T(8,128)S(1)}, f32[5,1,8,256]{3,2,1,0:T(8,128)}, u32[]{:S(2)}) copy-start(f32[5,1,8,256]{3,2,1,0:T(8,128)} %copy-done.21) | copy-start | bytes 122884
  306.7 8.3 %copy-start.24 = (f32[5,1,8,256]{3,2,1,0:T(8,128)S(1)}, f32[5,1,8,256]{3,2,1,0:T(8,128)}, u32[]{:S(2)}) copy-start(f32[5,1,8,256]{3,2,1,0:T(8,128)} %copy-done.23) | copy-start | bytes 122884
  306.7 8.3 %copy-start.26 = (f32[5,10,1,256]{3,2,1,0:T(1,128)S(1)}, f32[5,10,1,256]{3,2,1,0:T(1,128)}, u32[]{:S(2)}) copy-start(f32[5,10,1,256]{3,2,1,0:T(1,128)} %copy-done.25) | copy-start | bytes 153604
  309.8 17.7 %all-to-all-start.8 = ((f32[256,1,1]{2,1,0:T(1,128)}), f32[256,1,1]{2,1,0:T(1,128)S(1)}, u32[]{:S(2)}, u32[]{:S(2)}) async-start(f32[256,1,1]{2,1,0:T(1,128)} %broadcast_in_dim.82), calls=%async_computation.8 | async-start | bytes 262144 | tf_op jit(solution)/shard_map/all_to_all | solution.py:38
  315.0 15.5 %copy-start.16 = (f32[9,9,256]{2,1,0:T(8,128)S(1)}, f32[9,9,256]{2,1,0:T(8,128)}, u32[]{:S(2)}) copy-start(f32[9,9,256]{2,1,0:T(8,128)} %copy-done.15) | copy-start | bytes 248836
  393.5 9.9 %copy-start.7 = (f32[160,128]{1,0:T(8,128)S(1)}, f32[160,128]{1,0:T(8,128)}, u32[]{:S(2)}) copy-start(f32[160,128]{1,0:T(8,128)} %gather_fusion) | copy-start | bytes 245764
  521.3 12.7 %all-to-all-start.14 = ((f32[16,1,4096]{2,1,0:T(1,128)}), f32[16,1,4096]{2,1,0:T(1,128)S(1)}, u32[]{:S(2)}, u32[]{:S(2)}) async-start(f32[16,1,4096]{2,1,0:T(1,128)} %reshape.429), calls=%async_computation.14 | async-start | bytes 524288 | tf_op jit(solution)/shard_map/all_to_all | solution.py:74
  535.2 11.2 %copy-start.20 = (f32[128,128]{0,1:T(8,128)S(1)}, f32[128,128]{0,1:T(8,128)}, u32[]{:S(2)}) copy-start(f32[128,128]{0,1:T(8,128)} %copy-done.17) | copy-start | bytes 196612
  535.2 11.2 %copy-start.27 = (f32[3,128,128]{1,2,0:T(8,128)S(1)}, f32[3,128,128]{1,2,0:T(8,128)}, u32[]{:S(2)}) copy-start(f32[3,128,128]{1,2,0:T(8,128)} %get-tuple-element.100) | copy-start | bytes 589828
  566.1 31.3 %copy-start.4 = (f32[3,10,10,256]{3,2,1,0:T(8,128)S(1)}, f32[3,10,10,256]{3,2,1,0:T(8,128)}, u32[]{:S(2)}) copy-start(f32[3,10,10,256]{3,2,1,0:T(8,128)} %copy-done.3) | copy-start | bytes 921604
  606.9 22.0 %copy-start.9 = (f32[3,10,10,256]{3,2,1,0:T(8,128)S(1)}, f32[3,10,10,256]{3,2,1,0:T(8,128)}, u32[]{:S(2)}) copy-start(f32[3,10,10,256]{3,2,1,0:T(8,128)} %copy-done.8) | copy-start | bytes 921604
  (12 other events, 37.4 us)

commit v8 on v7

--- a/solution.py
+++ b/solution.py
@@ -121,16 +121,20 @@
         residual.shape[0], owned_height_lines, period_extent_first * owned_depth_slices
     )
     if partial is None:
-        spectrum, partial = exchange(spectrum, None, "row", 2, 1)
+        spectrum, _ = exchange(spectrum, None, "row", 2, 1)
+        lines = spectrum.reshape(components, ylength, xpiece, owned_depth_slices)
     else:
         spectrum, partial = carried(spectrum, "row", 2, 1)
-    spectrum = jnp.einsum(
-        "ky,cyxz->czkx",
-        ytable,
-        spectrum.reshape(components, ylength, xpiece, owned_depth_slices),
-        precision=PRECISE,
-    ).reshape(components, owned_depth_slices, ylength * xpiece)
-    spectrum, partial = exchange(spectrum, partial, "col", 2, 1)
+        lines = with_pulse(
+            spectrum.reshape(components, ylength, xpiece, owned_depth_slices), partial, 1
+        )
+    spectrum = jnp.einsum("ky,cyxz->czkx", ytable, lines, precision=PRECISE).reshape(
+        lines.shape[0], owned_depth_slices, ylength * xpiece
+    )
+    if partial is None:
+        spectrum, _ = exchange(spectrum, None, "col", 2, 1)
+    else:
+        spectrum, partial = carried(spectrum, "col", 2, 1)
     return jnp.einsum("kz,czm->ckm", ztable, spectrum, precision=PRECISE), partial
 
 
@@ -147,13 +151,13 @@
         "kz,czm->ckm", zwide, with_pulse(filtered, partial, 1), precision=PRECISE
     )
     spectrum, partial = carried(spectrum, "col", 1, 2)
-    spectrum = jnp.einsum(
-        "ky,czyx->ckxz",
-        ywide,
-        spectrum.reshape(components, owned_depth_slices + 2, ylength, xpiece),
-        precision=PRECISE,
-    ).reshape(components, row_count * (owned_height_lines + 2), xpiece * (owned_depth_slices + 2))
-    spectrum, partial = exchange(spectrum, partial, "row", 1, 2)
+    lines = with_pulse(
+        spectrum.reshape(components, owned_depth_slices + 2, ylength, xpiece), partial, 2
+    )
+    spectrum = jnp.einsum("ky,czyx->ckxz", ywide, lines, precision=PRECISE).reshape(
+        components + 1, row_count * (owned_height_lines + 2), xpiece * (owned_depth_slices + 2)
+    )
+    spectrum, partial = carried(spectrum, "row", 1, 2)
     return jnp.einsum(
         "kx,cyxz->cyzk",
         xtable,

time: 638 us -> 625 us (0.980)
  matrix products: 78.4 us -> 68.6 us
  local copies, waits for them, and re-layouts: 211 us -> 202 us
    all_to_all x4 -> x0, blocking collectives: 101 us -> none  [exchange(): lax.all_to_all(jnp.concatenate([cells, rider], 0), axis, split_axis, conc...]
    all_to_all x6 -> x10, blocking collectives: 72.1 us -> 172 us  [carried(): moved = lax.all_to_all(cells, axis, split_axis, concat_axis, tiled=True)]
    unnamed x94 -> x86, local copies, waits for them, and re-layouts: 107 us -> 89.4 us
    reshape x10, local copies, waits for them, and re-layouts: 9.76 us -> 22.5 us  [the longest x4 15.7 us: transform_forward(): jnp.einsum('ky,cyxz->czkx', ytable, lines, precision=PRECISE)]
    dot_general x8, matrix products: 27.5 us -> 17.7 us  [the longest x4 14.9 us: transform_forward(): jnp.einsum('ky,cyxz->czkx', ytable, lines, precision=PRECISE)]
    reshape x6 -> x4, local copies, waits for them, and re-layouts: 13.7 us -> 8.37 us  [transform_forward(): spectrum.reshape(components, ylength, xpiece, owned_depth_slices)]
where the time goes in v8:
time: 625 us; the launch traced here: 617 us
  blocking collectives  214 us (34%)
  local copies, waits for them, and re-layouts  202 us (32%)
  matrix products  68.6 us (11%)
  waiting for transfers between devices  45 us (7%)
  other arithmetic  41 us (7%)
  starting transfers between devices  36.6 us (6%)
  between operations  10.5 us (2%)
    all_to_all x10, blocking collectives, carried(): moved = lax.all_to_all(cells, axis, split_axis, concat_axis, tiled=True)  172 us
    unnamed x86, local copies, waits for them, and re-layouts  89.4 us
    dot_general x4, matrix products, transform_inverse(): jnp.einsum('kx,cyxz->cyzk', xtable, spectrum.reshape(components, owned_he...  36.7 us
    all_to_all x2, blocking collectives, exchange(): moved = lax.all_to_all(cells, axis, split_axis, concat_axis, tiled=True)  24.2 us
    all_to_all x1, blocking collectives, global_sum(): gathered = lax.all_to_all(spread, ('row', 'col'), 0, 0, tiled=True)  17.5 us
    reshape x4, local copies, waits for them, and re-layouts, transform_forward(): jnp.einsum('kx,cyzx->cykz', xtable, residual, precision=PRECISE)  17.4 us
    all_to_all x5, local copies, waits for them, and re-layouts, exchange(): moved = lax.all_to_all(cells, axis, split_axis, concat_axis, tiled=True)  15.7 us
    reshape x4, local copies, waits for them, and re-layouts, transform_forward(): jnp.einsum('ky,cyxz->czkx', ytable, lines, precision=PRECISE)  15.7 us
  transfers between devices with their start and end apart: 9, of which 7 were waited for; matrix products, arithmetic and copies ran while one was open for 1% of the time, Pallas kernels for 0%

profile of v8, /device:TPU:1, one launch (start us, length us, event | category | flops | bytes accessed | tf_op | source)
XLA Modules:
  0.0 617.5 jit_solution(9211417886308522012)
XLA Ops:
  30.8 9.7 %all-to-all-start = ((f32[16,1,3072]{2,1,0:T(1,128)}), f32[16,1,3072]{2,1,0:T(1,128)S(1)}, u32[]{:S(2)}, u32[]{:S(2)}) async-start(f32[16,1,3072]{2,1,0:T(1,128)} %reshape.415), calls=%async_computation | async-start | bytes 393216 | tf_op jit(solution)/shard_map/all_to_all | solution.py:70
  43.3 7.3 %all-to-all-done = f32[16,1,3072]{2,1,0:T(1,128)S(1)} async-done(((f32[16,1,3072]{2,1,0:T(1,128)}), f32[16,1,3072]{2,1,0:T(1,128)S(1)}, u32[]{:S(2)}, u32[]{:S(2)}) %all-to-all-start) | async-done | bytes 196640 | tf_op jit(solution)/shard_map/all_to_all | solution.py:70
  84.5 7.9 %all-to-all-done.1 = f32[16,1,3072]{2,1,0:T(1,128)S(1)} async-done(((f32[16,1,3072]{2,1,0:T(1,128)}), f32[16,1,3072]{2,1,0:T(1,128)S(1)}, u32[]{:S(2)}, u32[]{:S(2)}) %all-to-all-start.1) | async-done | bytes 196640 | tf_op jit(solution)/shard_map/all_to_all | solution.py:70
  104.2 10.7 %all_to_all.258 = f32[4,160,128]{2,0,1:T(4,128)S(1)} all-to-all(f32[4,160,128]{2,0,1:T(4,128)S(1)} %copy.328), channel_id=1, replica_groups=mesh['row'=16,'col'=16] {'col'}, dimensions={1} | all-to-all | bytes 655360 | tf_op jit(solution)/shard_map/all_to_all | solution.py:84
  119.2 25.2 %all_to_all.259 = f32[4,160,160]{2,0,1:T(4,128)S(1)} all-to-all(f32[4,160,160]{2,0,1:T(4,128)S(1)} %copy.333), channel_id=1, replica_groups=mesh['row'=16,'col'=16] {'row'}, dimensions={1} | all-to-all | bytes 819200 | tf_op jit(solution)/shard_map/all_to_all | solution.py:84
  149.0 9.2 %fusion.69 = f32[3,10,10,256]{3,2,1,0:T(8,128)S(1)} fusion(f32[3,10,256,10]{3,2,1,0:T(8,128)} %reshape.374), kind=kOutput, calls=%fused_computation.92 | convolution fusion | flops 236912640 | bytes 614400 | tf_op jit(solution)/shard_map/kx,cyxz->cyzk/dot_general | solution.py:161
  166.4 6.5 %reshape.419 = f32[16,1,4096]{2,1,0:T(1,128)S(1)} reshape(f32[2048,4,8]{2,1,0:T(4,128)} %bitcast.523) | data formatting | bytes 524288
  172.9 14.2 %all_to_all.260 = f32[16,1,4096]{2,1,0:T(1,128)S(1)} all-to-all(f32[16,1,4096]{2,1,0:T(1,128)S(1)} %reshape.419), channel_id=1, replica_groups=mesh['row'=16,'col'=16] {'row'}, dimensions={0} | all-to-all | bytes 524288 | tf_op jit(solution)/shard_map/all_to_all | solution.py:84
  188.4 6.3 %reshape.420 = f32[2048,4,8]{2,1,0:T(4,128)} reshape(f32[16,4096]{1,0:T(8,128)S(1)} %reduce.16) | data formatting | bytes 524288
  209.8 7.2 %reshape.421 = f32[16,1,4096]{2,1,0:T(1,128)} reshape(f32[2048,4,8]{2,1,0:T(4,128)} %bitcast.525) | data formatting | bytes 524288
  223.0 6.9 %all-to-all-done.5 = f32[16,1,4096]{2,1,0:T(1,128)S(1)} async-done(((f32[16,1,4096]{2,1,0:T(1,128)}), f32[16,1,4096]{2,1,0:T(1,128)S(1)}, u32[]{:S(2)}, u32[]{:S(2)}) %all-to-all-start.5) | async-done | bytes 262176 | tf_op jit(solution)/shard_map/all_to_all | solution.py:84
  231.3 6.3 %reshape.422 = f32[2048,4,8]{2,1,0:T(4,128)} reshape(f32[16,4096]{1,0:T(8,128)S(1)} %reduce.17) | data formatting | bytes 524288
  244.9 11.1 %all_to_all.261 = f32[4,160,128]{2,0,1:T(4,128)S(1)} all-to-all(f32[4,160,128]{2,0,1:T(4,128)S(1)} %copy.348), channel_id=1, replica_groups=mesh['row'=16,'col'=16] {'col'}, dimensions={1} | all-to-all | bytes 655360 | tf_op jit(solution)/shard_map/all_to_all | solution.py:84
  260.2 24.9 %all_to_all.262 = f32[4,160,160]{2,0,1:T(4,128)S(1)} all-to-all(f32[4,160,160]{2,0,1:T(4,128)S(1)} %copy.353), channel_id=1, replica_groups=mesh['row'=16,'col'=16] {'row'}, dimensions={1} | all-to-all | bytes 819200 | tf_op jit(solution)/shard_map/all_to_all | solution.py:84
  291.1 9.2 %convolution_add_fusion.1 = f32[3,10,10,256]{3,2,1,0:T(8,128)S(1)} fusion(f32[3,10,256,10]{3,2,1,0:T(8,128)} %reshape.382, f32[3,10,10,256]{3,2,1,0:T(8,128)S(1)} %copy-done.2, f32[]{:T(128)S(6)} %div.64), kind=kOutput, calls=%fused_computation.10 | convolution fusion | flops 237066240 | bytes 921604 | tf_op jit(solution)/shard_map/kx,cyxz->cyzk/dot_general | solution.py:161
  309.0 12.4 %all-to-all-done.8 = f32[256,1,1]{2,1,0:T(1,128)S(1)} async-done(((f32[256,1,1]{2,1,0:T(1,128)}), f32[256,1,1]{2,1,0:T(1,128)S(1)}, u32[]{:S(2)}, u32[]{:S(2)}) %all-to-all-start.8) | async-done | bytes 1056 | tf_op jit(solution)/shard_map/all_to_all | solution.py:38
  335.3 13.6 %all_to_all.263 = f32[16,1,3072]{2,1,0:T(1,128)S(1)} all-to-all(f32[16,1,3072]{2,1,0:T(1,128)S(1)} %reshape.423), channel_id=1, replica_groups=mesh['row'=16,'col'=16] {'row'}, dimensions={0} | all-to-all | bytes 393216 | tf_op jit(solution)/shard_map/all_to_all | solution.py:70
  360.9 5.9 fusion.11
  375.8 10.6 %all_to_all.264 = f32[16,1,3072]{2,1,0:T(1,128)S(1)} all-to-all(f32[16,1,3072]{2,1,0:T(1,128)S(1)} %reshape.425), channel_id=1, replica_groups=mesh['row'=16,'col'=16] {'col'}, dimensions={0} | all-to-all | bytes 393216 | tf_op jit(solution)/shard_map/all_to_all | solution.py:70
  398.2 10.7 %all_to_all.265 = f32[4,160,128]{2,0,1:T(4,128)S(1)} all-to-all(f32[4,160,128]{2,0,1:T(4,128)S(1)} %copy.369), channel_id=1, replica_groups=mesh['row'=16,'col'=16] {'col'}, dimensions={1} | all-to-all | bytes 655360 | tf_op jit(solution)/shard_map/all_to_all | solution.py:84
  413.0 25.2 %all_to_all.266 = f32[4,160,160]{2,0,1:T(4,128)S(1)} all-to-all(f32[4,160,160]{2,0,1:T(4,128)S(1)} %copy.374), channel_id=1, replica_groups=mesh['row'=16,'col'=16] {'row'}, dimensions={1} | all-to-all | bytes 819200 | tf_op jit(solution)/shard_map/all_to_all | solution.py:84
  442.8 9.2 %fusion.64 = f32[3,10,10,256]{3,2,1,0:T(8,128)S(1)} fusion(f32[3,10,256,10]{3,2,1,0:T(8,128)} %reshape.390), kind=kOutput, calls=%fused_computation.87 | convolution fusion | flops 236912640 | bytes 614400 | tf_op jit(solution)/shard_map/kx,cyxz->cyzk/dot_general | solution.py:161
  460.3 6.5 %reshape.427 = f32[16,1,4096]{2,1,0:T(1,128)S(1)} reshape(f32[2048,4,8]{2,1,0:T(4,128)} %bitcast.531) | data formatting | bytes 524288
  466.9 14.2 %all_to_all.267 = f32[16,1,4096]{2,1,0:T(1,128)S(1)} all-to-all(f32[16,1,4096]{2,1,0:T(1,128)S(1)} %reshape.427), channel_id=1, replica_groups=mesh['row'=16,'col'=16] {'row'}, dimensions={0} | all-to-all | bytes 524288 | tf_op jit(solution)/shard_map/all_to_all | solution.py:84
  482.4 6.3 %reshape.428 = f32[2048,4,8]{2,1,0:T(4,128)} reshape(f32[16,4096]{1,0:T(8,128)S(1)} %reduce.20) | data formatting | bytes 524288
  502.5 7.2 %reshape.429 = f32[16,1,4096]{2,1,0:T(1,128)} reshape(f32[2048,4,8]{2,1,0:T(4,128)} %bitcast.533) | data formatting | bytes 524288
  515.8 6.9 %all-to-all-done.14 = f32[16,1,4096]{2,1,0:T(1,128)S(1)} async-done(((f32[16,1,4096]{2,1,0:T(1,128)}), f32[16,1,4096]{2,1,0:T(1,128)S(1)}, u32[]{:S(2)}, u32[]{:S(2)}) %all-to-all-start.14) | async-done | bytes 262176 | tf_op jit(solution)/shard_map/all_to_all | solution.py:84
  524.0 6.3 %reshape.430 = f32[2048,4,8]{2,1,0:T(4,128)} reshape(f32[16,4096]{1,0:T(8,128)S(1)} %reduce.21) | data formatting | bytes 524288
  537.8 11.2 %all_to_all.268 = f32[4,160,128]{2,0,1:T(4,128)S(1)} all-to-all(f32[4,160,128]{2,0,1:T(4,128)S(1)} %copy.389), channel_id=1, replica_groups=mesh['row'=16,'col'=16] {'col'}, dimensions={1} | all-to-all | bytes 655360 | tf_op jit(solution)/shard_map/all_to_all | solution.py:84
  553.0 24.9 %all_to_all.269 = f32[4,160,160]{2,0,1:T(4,128)S(1)} all-to-all(f32[4,160,160]{2,0,1:T(4,128)S(1)} %copy.394), channel_id=1, replica_groups=mesh['row'=16,'col'=16] {'row'}, dimensions={1} | all-to-all | bytes 819200 | tf_op jit(solution)/shard_map/all_to_all | solution.py:84
  584.0 9.2 %convolution_add_fusion = f32[3,10,10,256]{3,2,1,0:T(8,128)S(1)} fusion(f32[3,10,256,10]{3,2,1,0:T(8,128)} %reshape.398, f32[3,10,10,256]{3,2,1,0:T(8,128)S(1)} %copy-done.4, f32[]{:T(128)S(6)} %div.67), kind=kOutput, calls=%fused_computation.9 | convolution fusion | flops 237066240 | bytes 921604 | tf_op jit(solution)/shard_map/kx,cyxz->cyzk/dot_general | solution.py:161
  595.7 17.5 %all_to_all.270 = f32[256,1,1]{2,1,0:T(1,128)S(1)} all-to-all(f32[256,1,1]{2,1,0:T(1,128)S(1)} %broadcast_in_dim.114), channel_id=1, replica_groups=mesh['row'=16,'col'=16] {'row','col'}, dimensions={0} | all-to-all | bytes 2048 | tf_op jit(solution)/shard_map/all_to_all | solution.py:38
  (386 shorter events, 246.6 us)
Async XLA Ops:
  0.6 18.3 %copy-start = (f32[3,8,8,256]{3,2,1,0:T(8,128)S(1)}, f32[3,8,8,256]{3,2,1,0:T(8,128)}, u32[]{:S(2)}) copy-start(f32[3,8,8,256]{3,2,1,0:T(8,128)} %param.3) | copy-start | bytes 589828
  0.6 18.3 %copy-start.10 = (f32[8,8,256]{2,1,0:T(8,128)S(1)}, f32[8,8,256]{2,1,0:T(8,128)}, u32[]{:S(2)}) copy-start(f32[8,8,256]{2,1,0:T(8,128)} %param.5) | copy-start | bytes 196612
  0.7 18.3 %copy-start.13 = (f32[8,8,256]{2,1,0:T(8,128)S(1)}, f32[8,8,256]{2,1,0:T(8,128)}, u32[]{:S(2)}) copy-start(f32[8,8,256]{2,1,0:T(8,128)} %param.4) | copy-start | bytes 196612
  1.5 4.2 collective-permute-start
  4.6 3.4 collective-permute-start.1
  5.6 14.3 %copy-start.31 = (f32[1,8,8,256]{3,2,1,0:T(8,128)}, f32[1,8,8,256]{3,2,1,0:T(8,128)S(1)}, u32[]{:S(2)}) copy-start(f32[1,8,8,256]{3,2,1,0:T(8,128)S(1)} %add_bitcast_fusion) | copy-start | bytes 196612
  5.7 13.6 %copy-start.21 = (f32[5,1,8,256]{3,2,1,0:T(8,128)}, f32[5,1,8,256]{3,2,1,0:T(8,128)S(1)}, u32[]{:S(2)}) copy-start(f32[5,1,8,256]{3,2,1,0:T(8,128)S(1)} %collective-permute-done) | copy-start | bytes 122884
  8.0 11.4 %copy-start.23 = (f32[5,1,8,256]{3,2,1,0:T(8,128)}, f32[5,1,8,256]{3,2,1,0:T(8,128)S(1)}, u32[]{:S(2)}) copy-start(f32[5,1,8,256]{3,2,1,0:T(8,128)S(1)} %collective-permute-done.1) | copy-start | bytes 122884
  9.2 6.5 %collective-permute-start.2 = (f32[5,10,1,256]{3,2,1,0:T(1,128)S(1)}, f32[5,10,1,256]{3,2,1,0:T(1,128)S(1)}, u32[]{:S(2)}, u32[]{:S(2)}) collective-permute-start(f32[5,10,1,256]{3,2,1,0:T(1,128)S(1)} %get-tuple-element.56), channel_id=1, source_target_pairs={{0,1},{1,2},{2,3},{3,4},{4,5},{5,6},{6,7},{7,8},{8,9},{9,10},{10,1... | collective-permute-start | bytes 153608 | tf_op jit(solution)/shard_map/ppermute | solution.py:26
  10.6 6.1 collective-permute-start.3
  30.8 19.8 %all-to-all-start = ((f32[16,1,3072]{2,1,0:T(1,128)}), f32[16,1,3072]{2,1,0:T(1,128)S(1)}, u32[]{:S(2)}, u32[]{:S(2)}) async-start(f32[16,1,3072]{2,1,0:T(1,128)} %reshape.415), calls=%async_computation | async-start | bytes 393216 | tf_op jit(solution)/shard_map/all_to_all | solution.py:70
  69.2 15.1 %copy-start.33 = (f32[128]{0:T(128)S(1)}, f32[128]{0:T(128)}, u32[]{:S(2)}) copy-start(f32[128]{0:T(128)} %add.535) | copy-start | bytes 1540
  69.2 15.2 %copy-start.34 = (f32[128]{0:T(128)S(1)}, f32[128]{0:T(128)}, u32[]{:S(2)}) copy-start(f32[128]{0:T(128)} %multiply_subtract_fusion.2) | copy-start | bytes 1540
  78.8 13.5 %all-to-all-start.1 = ((f32[16,1,3072]{2,1,0:T(1,128)}), f32[16,1,3072]{2,1,0:T(1,128)S(1)}, u32[]{:S(2)}, u32[]{:S(2)}) async-start(f32[16,1,3072]{2,1,0:T(1,128)} %reshape.417), calls=%async_computation.1 | async-start | bytes 393216 | tf_op jit(solution)/shard_map/all_to_all | solution.py:70
  84.5 16.4 %copy-start.17 = (f32[128,128]{0,1:T(8,128)}, f32[128,128]{0,1:T(8,128)S(1)}, u32[]{:S(2)}) copy-start(f32[128,128]{0,1:T(8,128)S(1)} %add_divide_fusion) | copy-start | bytes 196612
  93.5 10.1 %copy-start.5 = (f32[160,128]{1,0:T(8,128)S(1)}, f32[160,128]{1,0:T(8,128)}, u32[]{:S(2)}) copy-start(f32[160,128]{1,0:T(8,128)} %gather_fusion) | copy-start | bytes 245764
  216.9 13.0 %all-to-all-start.5 = ((f32[16,1,4096]{2,1,0:T(1,128)}), f32[16,1,4096]{2,1,0:T(1,128)S(1)}, u32[]{:S(2)}, u32[]{:S(2)}) async-start(f32[16,1,4096]{2,1,0:T(1,128)} %reshape.421), calls=%async_computation.5 | async-start | bytes 524288 | tf_op jit(solution)/shard_map/all_to_all | solution.py:84
  231.2 11.0 %copy-start.18 = (f32[128,128]{0,1:T(8,128)S(1)}, f32[128,128]{0,1:T(8,128)}, u32[]{:S(2)}) copy-start(f32[128,128]{0,1:T(8,128)} %copy-done.17) | copy-start | bytes 196612
  231.2 11.0 %copy-start.28 = (f32[3,128,128]{1,2,0:T(8,128)S(1)}, f32[3,128,128]{1,2,0:T(8,128)}, u32[]{:S(2)}) copy-start(f32[3,128,128]{1,2,0:T(8,128)} %get-tuple-element.99) | copy-start | bytes 589828
  260.1 31.0 %copy-start.2 = (f32[3,10,10,256]{3,2,1,0:T(8,128)S(1)}, f32[3,10,10,256]{3,2,1,0:T(8,128)}, u32[]{:S(2)}) copy-start(f32[3,10,10,256]{3,2,1,0:T(8,128)} %copy-done.1) | copy-start | bytes 921604
  300.5 8.3 %copy-start.14 = (f32[8,8,256]{2,1,0:T(8,128)S(1)}, f32[8,8,256]{2,1,0:T(8,128)}, u32[]{:S(2)}) copy-start(f32[8,8,256]{2,1,0:T(8,128)} %param.4) | copy-start | bytes 196612
  300.5 8.3 %copy-start.22 = (f32[5,1,8,256]{3,2,1,0:T(8,128)S(1)}, f32[5,1,8,256]{3,2,1,0:T(8,128)}, u32[]{:S(2)}) copy-start(f32[5,1,8,256]{3,2,1,0:T(8,128)} %copy-done.21) | copy-start | bytes 122884
  300.5 8.3 %copy-start.24 = (f32[5,1,8,256]{3,2,1,0:T(8,128)S(1)}, f32[5,1,8,256]{3,2,1,0:T(8,128)}, u32[]{:S(2)}) copy-start(f32[5,1,8,256]{3,2,1,0:T(8,128)} %copy-done.23) | copy-start | bytes 122884
  300.5 8.3 %copy-start.26 = (f32[5,10,1,256]{3,2,1,0:T(1,128)S(1)}, f32[5,10,1,256]{3,2,1,0:T(1,128)}, u32[]{:S(2)}) copy-start(f32[5,10,1,256]{3,2,1,0:T(1,128)} %copy-done.25) | copy-start | bytes 153604
  303.7 17.7 %all-to-all-start.8 = ((f32[256,1,1]{2,1,0:T(1,128)}), f32[256,1,1]{2,1,0:T(1,128)S(1)}, u32[]{:S(2)}, u32[]{:S(2)}) async-start(f32[256,1,1]{2,1,0:T(1,128)} %broadcast_in_dim.107), calls=%async_computation.8 | async-start | bytes 262144 | tf_op jit(solution)/shard_map/all_to_all | solution.py:38
  308.9 15.4 %copy-start.16 = (f32[9,9,256]{2,1,0:T(8,128)S(1)}, f32[9,9,256]{2,1,0:T(8,128)}, u32[]{:S(2)}) copy-start(f32[9,9,256]{2,1,0:T(8,128)} %copy-done.15) | copy-start | bytes 248836
  387.5 10.0 %copy-start.7 = (f32[160,128]{1,0:T(8,128)S(1)}, f32[160,128]{1,0:T(8,128)}, u32[]{:S(2)}) copy-start(f32[160,128]{1,0:T(8,128)} %gather_fusion) | copy-start | bytes 245764
  509.7 13.0 %all-to-all-start.14 = ((f32[16,1,4096]{2,1,0:T(1,128)}), f32[16,1,4096]{2,1,0:T(1,128)S(1)}, u32[]{:S(2)}, u32[]{:S(2)}) async-start(f32[16,1,4096]{2,1,0:T(1,128)} %reshape.429), calls=%async_computation.14 | async-start | bytes 524288 | tf_op jit(solution)/shard_map/all_to_all | solution.py:84
  524.0 11.1 %copy-start.20 = (f32[128,128]{0,1:T(8,128)S(1)}, f32[128,128]{0,1:T(8,128)}, u32[]{:S(2)}) copy-start(f32[128,128]{0,1:T(8,128)} %copy-done.17) | copy-start | bytes 196612
  524.0 11.1 %copy-start.27 = (f32[3,128,128]{1,2,0:T(8,128)S(1)}, f32[3,128,128]{1,2,0:T(8,128)}, u32[]{:S(2)}) copy-start(f32[3,128,128]{1,2,0:T(8,128)} %get-tuple-element.100) | copy-start | bytes 589828
  553.0 31.0 %copy-start.4 = (f32[3,10,10,256]{3,2,1,0:T(8,128)S(1)}, f32[3,10,10,256]{3,2,1,0:T(8,128)}, u32[]{:S(2)}) copy-start(f32[3,10,10,256]{3,2,1,0:T(8,128)} %copy-done.3) | copy-start | bytes 921604
  593.5 22.0 %copy-start.9 = (f32[3,10,10,256]{3,2,1,0:T(8,128)S(1)}, f32[3,10,10,256]{3,2,1,0:T(8,128)}, u32[]{:S(2)}) copy-start(f32[3,10,10,256]{3,2,1,0:T(8,128)} %copy-done.8) | copy-start | bytes 921604
  (12 other events, 37.1 us)

commit v9 on v8

--- a/solution.py
+++ b/solution.py
@@ -82,9 +82,13 @@
 def carried(cells, axis, split_axis, concat_axis):
     count = lax.axis_size(axis)
     moved = lax.all_to_all(cells, axis, split_axis, concat_axis, tiled=True)
-    arrived = jnp.moveaxis(moved[-1], concat_axis - 1, 0)
-    arrived = arrived.reshape(count, arrived.shape[0] // count, -1)[:, 0, 0]
-    return moved[:-1], jnp.sum(arrived)
+    rider = moved[-1]
+    pieces = rider.shape[concat_axis - 1] // count
+    picks = tuple(
+        slice(0, None, pieces) if dim == concat_axis - 1 else slice(0, 1)
+        for dim in range(rider.ndim)
+    )
+    return moved[:-1], jnp.sum(rider[picks])
 
 
 def with_pulse(cells, partial, dim):

time: 625 us -> 625 us (level)
    unnamed x86 -> x94, local copies, waits for them, and re-layouts: 89.4 us -> 89.6 us
where the time goes in v9:
time: 625 us; the launch traced here: 618 us
  blocking collectives  214 us (34%)
  local copies, waits for them, and re-layouts  202 us (32%)
  matrix products  68.6 us (11%)
  waiting for transfers between devices  44.4 us (7%)
  other arithmetic  41.1 us (7%)
  starting transfers between devices  36.6 us (6%)
  between operations  10.6 us (2%)
    all_to_all x10, blocking collectives, carried(): moved = lax.all_to_all(cells, axis, split_axis, concat_axis, tiled=True)  173 us
    unnamed x94, local copies, waits for them, and re-layouts  89.6 us
    dot_general x4, matrix products, transform_inverse(): jnp.einsum('kx,cyxz->cyzk', xtable, spectrum.reshape(components, owned_he...  36.7 us
    all_to_all x2, blocking collectives, exchange(): moved = lax.all_to_all(cells, axis, split_axis, concat_axis, tiled=True)  24.2 us
    all_to_all x1, blocking collectives, global_sum(): gathered = lax.all_to_all(spread, ('row', 'col'), 0, 0, tiled=True)  17.5 us
    reshape x4, local copies, waits for them, and re-layouts, transform_forward(): jnp.einsum('kx,cyzx->cykz', xtable, residual, precision=PRECISE)  17.4 us
    all_to_all x5, local copies, waits for them, and re-layouts, exchange(): moved = lax.all_to_all(cells, axis, split_axis, concat_axis, tiled=True)  15.7 us
    reshape x4, local copies, waits for them, and re-layouts, transform_forward(): jnp.einsum('ky,cyxz->czkx', ytable, lines, precision=PRECISE)  15.7 us
  transfers between devices with their start and end apart: 9, of which 7 were waited for; matrix products, arithmetic and copies ran while one was open for 1% of the time, Pallas kernels for 0%

profile of v9, /device:TPU:1, one launch (start us, length us, event | category | flops | bytes accessed | tf_op | source)
XLA Modules:
  0.0 617.9 jit_solution(16394165842449436848)
XLA Ops:
  30.8 9.7 %all-to-all-start = ((f32[16,1,3072]{2,1,0:T(1,128)}), f32[16,1,3072]{2,1,0:T(1,128)S(1)}, u32[]{:S(2)}, u32[]{:S(2)}) async-start(f32[16,1,3072]{2,1,0:T(1,128)} %reshape.383), calls=%async_computation | async-start | bytes 393216 | tf_op jit(solution)/shard_map/all_to_all | solution.py:70
  43.3 7.3 %all-to-all-done = f32[16,1,3072]{2,1,0:T(1,128)S(1)} async-done(((f32[16,1,3072]{2,1,0:T(1,128)}), f32[16,1,3072]{2,1,0:T(1,128)S(1)}, u32[]{:S(2)}, u32[]{:S(2)}) %all-to-all-start) | async-done | bytes 196640 | tf_op jit(solution)/shard_map/all_to_all | solution.py:70
  84.5 7.9 %all-to-all-done.1 = f32[16,1,3072]{2,1,0:T(1,128)S(1)} async-done(((f32[16,1,3072]{2,1,0:T(1,128)}), f32[16,1,3072]{2,1,0:T(1,128)S(1)}, u32[]{:S(2)}, u32[]{:S(2)}) %all-to-all-start.1) | async-done | bytes 196640 | tf_op jit(solution)/shard_map/all_to_all | solution.py:70
  104.2 10.7 %all_to_all.258 = f32[4,160,128]{2,0,1:T(4,128)S(1)} all-to-all(f32[4,160,128]{2,0,1:T(4,128)S(1)} %copy.344), channel_id=1, replica_groups=mesh['row'=16,'col'=16] {'col'}, dimensions={1} | all-to-all | bytes 655360 | tf_op jit(solution)/shard_map/all_to_all | solution.py:84
  119.3 25.2 %all_to_all.259 = f32[4,160,160]{2,0,1:T(4,128)S(1)} all-to-all(f32[4,160,160]{2,0,1:T(4,128)S(1)} %copy.349), channel_id=1, replica_groups=mesh['row'=16,'col'=16] {'row'}, dimensions={1} | all-to-all | bytes 819200 | tf_op jit(solution)/shard_map/all_to_all | solution.py:84
  149.2 9.2 %fusion.69 = f32[3,10,10,256]{3,2,1,0:T(8,128)S(1)} fusion(f32[3,10,256,10]{3,2,1,0:T(8,128)} %reshape.348), kind=kOutput, calls=%fused_computation.92 | convolution fusion | flops 236912640 | bytes 614400 | tf_op jit(solution)/shard_map/kx,cyxz->cyzk/dot_general | solution.py:165
  166.6 6.5 %reshape.387 = f32[16,1,4096]{2,1,0:T(1,128)S(1)} reshape(f32[2048,4,8]{2,1,0:T(4,128)} %bitcast.479) | data formatting | bytes 524288
  173.1 14.2 %all_to_all.260 = f32[16,1,4096]{2,1,0:T(1,128)S(1)} all-to-all(f32[16,1,4096]{2,1,0:T(1,128)S(1)} %reshape.387), channel_id=1, replica_groups=mesh['row'=16,'col'=16] {'row'}, dimensions={0} | all-to-all | bytes 524288 | tf_op jit(solution)/shard_map/all_to_all | solution.py:84
  188.6 6.3 %reshape.388 = f32[2048,4,8]{2,1,0:T(4,128)} reshape(f32[16,4096]{1,0:T(8,128)S(1)} %reduce.4) | data formatting | bytes 524288
  210.0 7.2 %reshape.389 = f32[16,1,4096]{2,1,0:T(1,128)} reshape(f32[2048,4,8]{2,1,0:T(4,128)} %bitcast.481) | data formatting | bytes 524288
  223.2 6.6 %all-to-all-done.5 = f32[16,1,4096]{2,1,0:T(1,128)S(1)} async-done(((f32[16,1,4096]{2,1,0:T(1,128)}), f32[16,1,4096]{2,1,0:T(1,128)S(1)}, u32[]{:S(2)}, u32[]{:S(2)}) %all-to-all-start.5) | async-done | bytes 262176 | tf_op jit(solution)/shard_map/all_to_all | solution.py:84
  231.1 6.3 %reshape.390 = f32[2048,4,8]{2,1,0:T(4,128)} reshape(f32[16,4096]{1,0:T(8,128)S(1)} %reduce.5) | data formatting | bytes 524288
  244.9 11.0 %all_to_all.261 = f32[4,160,128]{2,0,1:T(4,128)S(1)} all-to-all(f32[4,160,128]{2,0,1:T(4,128)S(1)} %copy.366), channel_id=1, replica_groups=mesh['row'=16,'col'=16] {'col'}, dimensions={1} | all-to-all | bytes 655360 | tf_op jit(solution)/shard_map/all_to_all | solution.py:84
  260.2 25.1 %all_to_all.262 = f32[4,160,160]{2,0,1:T(4,128)S(1)} all-to-all(f32[4,160,160]{2,0,1:T(4,128)S(1)} %copy.371), channel_id=1, replica_groups=mesh['row'=16,'col'=16] {'row'}, dimensions={1} | all-to-all | bytes 819200 | tf_op jit(solution)/shard_map/all_to_all | solution.py:84
  291.3 9.2 %convolution_add_fusion.1 = f32[3,10,10,256]{3,2,1,0:T(8,128)S(1)} fusion(f32[3,10,256,10]{3,2,1,0:T(8,128)} %reshape.354, f32[3,10,10,256]{3,2,1,0:T(8,128)S(1)} %copy-done.2, f32[]{:T(128)S(6)} %div.64), kind=kOutput, calls=%fused_computation.10 | convolution fusion | flops 237066240 | bytes 921604 | tf_op jit(solution)/shard_map/kx,cyxz->cyzk/dot_general | solution.py:165
  309.2 12.4 %all-to-all-done.8 = f32[256,1,1]{2,1,0:T(1,128)S(1)} async-done(((f32[256,1,1]{2,1,0:T(1,128)}), f32[256,1,1]{2,1,0:T(1,128)S(1)}, u32[]{:S(2)}, u32[]{:S(2)}) %all-to-all-start.8) | async-done | bytes 1056 | tf_op jit(solution)/shard_map/all_to_all | solution.py:38
  335.5 13.6 %all_to_all.263 = f32[16,1,3072]{2,1,0:T(1,128)S(1)} all-to-all(f32[16,1,3072]{2,1,0:T(1,128)S(1)} %reshape.391), channel_id=1, replica_groups=mesh['row'=16,'col'=16] {'row'}, dimensions={0} | all-to-all | bytes 393216 | tf_op jit(solution)/shard_map/all_to_all | solution.py:70
  361.1 5.9 fusion.11
  376.0 10.6 %all_to_all.264 = f32[16,1,3072]{2,1,0:T(1,128)S(1)} all-to-all(f32[16,1,3072]{2,1,0:T(1,128)S(1)} %reshape.393), channel_id=1, replica_groups=mesh['row'=16,'col'=16] {'col'}, dimensions={0} | all-to-all | bytes 393216 | tf_op jit(solution)/shard_map/all_to_all | solution.py:70
  398.4 10.7 %all_to_all.265 = f32[4,160,128]{2,0,1:T(4,128)S(1)} all-to-all(f32[4,160,128]{2,0,1:T(4,128)S(1)} %copy.387), channel_id=1, replica_groups=mesh['row'=16,'col'=16] {'col'}, dimensions={1} | all-to-all | bytes 655360 | tf_op jit(solution)/shard_map/all_to_all | solution.py:84
  413.3 25.2 %all_to_all.266 = f32[4,160,160]{2,0,1:T(4,128)S(1)} all-to-all(f32[4,160,160]{2,0,1:T(4,128)S(1)} %copy.392), channel_id=1, replica_groups=mesh['row'=16,'col'=16] {'row'}, dimensions={1} | all-to-all | bytes 819200 | tf_op jit(solution)/shard_map/all_to_all | solution.py:84
  443.2 9.2 %fusion.64 = f32[3,10,10,256]{3,2,1,0:T(8,128)S(1)} fusion(f32[3,10,256,10]{3,2,1,0:T(8,128)} %reshape.360), kind=kOutput, calls=%fused_computation.87 | convolution fusion | flops 236912640 | bytes 614400 | tf_op jit(solution)/shard_map/kx,cyxz->cyzk/dot_general | solution.py:165
  460.7 6.5 %reshape.395 = f32[16,1,4096]{2,1,0:T(1,128)S(1)} reshape(f32[2048,4,8]{2,1,0:T(4,128)} %bitcast.487) | data formatting | bytes 524288
  467.2 14.2 %all_to_all.267 = f32[16,1,4096]{2,1,0:T(1,128)S(1)} all-to-all(f32[16,1,4096]{2,1,0:T(1,128)S(1)} %reshape.395), channel_id=1, replica_groups=mesh['row'=16,'col'=16] {'row'}, dimensions={0} | all-to-all | bytes 524288 | tf_op jit(solution)/shard_map/all_to_all | solution.py:84
  482.7 6.3 %reshape.396 = f32[2048,4,8]{2,1,0:T(4,128)} reshape(f32[16,4096]{1,0:T(8,128)S(1)} %reduce.8) | data formatting | bytes 524288
  503.0 7.2 %reshape.397 = f32[16,1,4096]{2,1,0:T(1,128)} reshape(f32[2048,4,8]{2,1,0:T(4,128)} %bitcast.489) | data formatting | bytes 524288
  516.2 6.6 %all-to-all-done.14 = f32[16,1,4096]{2,1,0:T(1,128)S(1)} async-done(((f32[16,1,4096]{2,1,0:T(1,128)}), f32[16,1,4096]{2,1,0:T(1,128)S(1)}, u32[]{:S(2)}, u32[]{:S(2)}) %all-to-all-start.14) | async-done | bytes 262176 | tf_op jit(solution)/shard_map/all_to_all | solution.py:84
  524.1 6.3 %reshape.398 = f32[2048,4,8]{2,1,0:T(4,128)} reshape(f32[16,4096]{1,0:T(8,128)S(1)} %reduce.9) | data formatting | bytes 524288
  537.9 11.1 %all_to_all.268 = f32[4,160,128]{2,0,1:T(4,128)S(1)} all-to-all(f32[4,160,128]{2,0,1:T(4,128)S(1)} %copy.409), channel_id=1, replica_groups=mesh['row'=16,'col'=16] {'col'}, dimensions={1} | all-to-all | bytes 655360 | tf_op jit(solution)/shard_map/all_to_all | solution.py:84
  553.2 25.1 %all_to_all.269 = f32[4,160,160]{2,0,1:T(4,128)S(1)} all-to-all(f32[4,160,160]{2,0,1:T(4,128)S(1)} %copy.414), channel_id=1, replica_groups=mesh['row'=16,'col'=16] {'row'}, dimensions={1} | all-to-all | bytes 819200 | tf_op jit(solution)/shard_map/all_to_all | solution.py:84
  584.4 9.2 %convolution_add_fusion = f32[3,10,10,256]{3,2,1,0:T(8,128)S(1)} fusion(f32[3,10,256,10]{3,2,1,0:T(8,128)} %reshape.366, f32[3,10,10,256]{3,2,1,0:T(8,128)S(1)} %copy-done.4, f32[]{:T(128)S(6)} %div.67), kind=kOutput, calls=%fused_computation.9 | convolution fusion | flops 237066240 | bytes 921604 | tf_op jit(solution)/shard_map/kx,cyxz->cyzk/dot_general | solution.py:165
  596.2 17.5 %all_to_all.270 = f32[256,1,1]{2,1,0:T(1,128)S(1)} all-to-all(f32[256,1,1]{2,1,0:T(1,128)S(1)} %broadcast_in_dim.114), channel_id=1, replica_groups=mesh['row'=16,'col'=16] {'row','col'}, dimensions={0} | all-to-all | bytes 2048 | tf_op jit(solution)/shard_map/all_to_all | solution.py:38
  (402 shorter events, 247.4 us)
Async XLA Ops:
  0.6 18.3 %copy-start = (f32[3,8,8,256]{3,2,1,0:T(8,128)S(1)}, f32[3,8,8,256]{3,2,1,0:T(8,128)}, u32[]{:S(2)}) copy-start(f32[3,8,8,256]{3,2,1,0:T(8,128)} %param.3) | copy-start | bytes 589828
  0.6 18.3 %copy-start.10 = (f32[8,8,256]{2,1,0:T(8,128)S(1)}, f32[8,8,256]{2,1,0:T(8,128)}, u32[]{:S(2)}) copy-start(f32[8,8,256]{2,1,0:T(8,128)} %param.5) | copy-start | bytes 196612
  0.7 18.3 %copy-start.13 = (f32[8,8,256]{2,1,0:T(8,128)S(1)}, f32[8,8,256]{2,1,0:T(8,128)}, u32[]{:S(2)}) copy-start(f32[8,8,256]{2,1,0:T(8,128)} %param.4) | copy-start | bytes 196612
  1.5 4.2 collective-permute-start
  4.6 3.4 collective-permute-start.1
  5.6 14.3 %copy-start.31 = (f32[1,8,8,256]{3,2,1,0:T(8,128)}, f32[1,8,8,256]{3,2,1,0:T(8,128)S(1)}, u32[]{:S(2)}) copy-start(f32[1,8,8,256]{3,2,1,0:T(8,128)S(1)} %add_bitcast_fusion) | copy-start | bytes 196612
  5.7 13.6 %copy-start.21 = (f32[5,1,8,256]{3,2,1,0:T(8,128)}, f32[5,1,8,256]{3,2,1,0:T(8,128)S(1)}, u32[]{:S(2)}) copy-start(f32[5,1,8,256]{3,2,1,0:T(8,128)S(1)} %collective-permute-done) | copy-start | bytes 122884
  8.0 11.4 %copy-start.23 = (f32[5,1,8,256]{3,2,1,0:T(8,128)}, f32[5,1,8,256]{3,2,1,0:T(8,128)S(1)}, u32[]{:S(2)}) copy-start(f32[5,1,8,256]{3,2,1,0:T(8,128)S(1)} %collective-permute-done.1) | copy-start | bytes 122884
  9.2 6.5 %collective-permute-start.2 = (f32[5,10,1,256]{3,2,1,0:T(1,128)S(1)}, f32[5,10,1,256]{3,2,1,0:T(1,128)S(1)}, u32[]{:S(2)}, u32[]{:S(2)}) collective-permute-start(f32[5,10,1,256]{3,2,1,0:T(1,128)S(1)} %get-tuple-element.56), channel_id=1, source_target_pairs={{0,1},{1,2},{2,3},{3,4},{4,5},{5,6},{6,7},{7,8},{8,9},{9,10},{10,1... | collective-permute-start | bytes 153608 | tf_op jit(solution)/shard_map/ppermute | solution.py:26
  10.6 6.1 collective-permute-start.3
  30.8 19.8 %all-to-all-start = ((f32[16,1,3072]{2,1,0:T(1,128)}), f32[16,1,3072]{2,1,0:T(1,128)S(1)}, u32[]{:S(2)}, u32[]{:S(2)}) async-start(f32[16,1,3072]{2,1,0:T(1,128)} %reshape.383), calls=%async_computation | async-start | bytes 393216 | tf_op jit(solution)/shard_map/all_to_all | solution.py:70
  69.2 15.1 %copy-start.33 = (f32[128]{0:T(128)S(1)}, f32[128]{0:T(128)}, u32[]{:S(2)}) copy-start(f32[128]{0:T(128)} %add.535) | copy-start | bytes 1540
  69.2 15.2 %copy-start.34 = (f32[128]{0:T(128)S(1)}, f32[128]{0:T(128)}, u32[]{:S(2)}) copy-start(f32[128]{0:T(128)} %multiply_subtract_fusion.2) | copy-start | bytes 1540
  78.8 13.5 %all-to-all-start.1 = ((f32[16,1,3072]{2,1,0:T(1,128)}), f32[16,1,3072]{2,1,0:T(1,128)S(1)}, u32[]{:S(2)}, u32[]{:S(2)}) async-start(f32[16,1,3072]{2,1,0:T(1,128)} %reshape.385), calls=%async_computation.1 | async-start | bytes 393216 | tf_op jit(solution)/shard_map/all_to_all | solution.py:70
  84.5 16.4 %copy-start.17 = (f32[128,128]{0,1:T(8,128)}, f32[128,128]{0,1:T(8,128)S(1)}, u32[]{:S(2)}) copy-start(f32[128,128]{0,1:T(8,128)S(1)} %add_divide_fusion) | copy-start | bytes 196612
  93.5 10.1 %copy-start.5 = (f32[160,128]{1,0:T(8,128)S(1)}, f32[160,128]{1,0:T(8,128)}, u32[]{:S(2)}) copy-start(f32[160,128]{1,0:T(8,128)} %gather_fusion) | copy-start | bytes 245764
  217.2 12.7 %all-to-all-start.5 = ((f32[16,1,4096]{2,1,0:T(1,128)}), f32[16,1,4096]{2,1,0:T(1,128)S(1)}, u32[]{:S(2)}, u32[]{:S(2)}) async-start(f32[16,1,4096]{2,1,0:T(1,128)} %reshape.389), calls=%async_computation.5 | async-start | bytes 524288 | tf_op jit(solution)/shard_map/all_to_all | solution.py:84
  231.1 11.1 %copy-start.18 = (f32[128,128]{0,1:T(8,128)S(1)}, f32[128,128]{0,1:T(8,128)}, u32[]{:S(2)}) copy-start(f32[128,128]{0,1:T(8,128)} %copy-done.17) | copy-start | bytes 196612
  231.1 11.1 %copy-start.28 = (f32[3,128,128]{1,2,0:T(8,128)S(1)}, f32[3,128,128]{1,2,0:T(8,128)}, u32[]{:S(2)}) copy-start(f32[3,128,128]{1,2,0:T(8,128)} %get-tuple-element.99) | copy-start | bytes 589828
  260.1 31.2 %copy-start.2 = (f32[3,10,10,256]{3,2,1,0:T(8,128)S(1)}, f32[3,10,10,256]{3,2,1,0:T(8,128)}, u32[]{:S(2)}) copy-start(f32[3,10,10,256]{3,2,1,0:T(8,128)} %copy-done.1) | copy-start | bytes 921604
  300.7 8.3 %copy-start.14 = (f32[8,8,256]{2,1,0:T(8,128)S(1)}, f32[8,8,256]{2,1,0:T(8,128)}, u32[]{:S(2)}) copy-start(f32[8,8,256]{2,1,0:T(8,128)} %param.4) | copy-start | bytes 196612
  300.7 8.3 %copy-start.22 = (f32[5,1,8,256]{3,2,1,0:T(8,128)S(1)}, f32[5,1,8,256]{3,2,1,0:T(8,128)}, u32[]{:S(2)}) copy-start(f32[5,1,8,256]{3,2,1,0:T(8,128)} %copy-done.21) | copy-start | bytes 122884
  300.7 8.3 %copy-start.24 = (f32[5,1,8,256]{3,2,1,0:T(8,128)S(1)}, f32[5,1,8,256]{3,2,1,0:T(8,128)}, u32[]{:S(2)}) copy-start(f32[5,1,8,256]{3,2,1,0:T(8,128)} %copy-done.23) | copy-start | bytes 122884
  300.7 8.3 %copy-start.26 = (f32[5,10,1,256]{3,2,1,0:T(1,128)S(1)}, f32[5,10,1,256]{3,2,1,0:T(1,128)}, u32[]{:S(2)}) copy-start(f32[5,10,1,256]{3,2,1,0:T(1,128)} %copy-done.25) | copy-start | bytes 153604
  303.9 17.7 %all-to-all-start.8 = ((f32[256,1,1]{2,1,0:T(1,128)}), f32[256,1,1]{2,1,0:T(1,128)S(1)}, u32[]{:S(2)}, u32[]{:S(2)}) async-start(f32[256,1,1]{2,1,0:T(1,128)} %broadcast_in_dim.107), calls=%async_computation.8 | async-start | bytes 262144 | tf_op jit(solution)/shard_map/all_to_all | solution.py:38
  309.1 15.4 %copy-start.16 = (f32[9,9,256]{2,1,0:T(8,128)S(1)}, f32[9,9,256]{2,1,0:T(8,128)}, u32[]{:S(2)}) copy-start(f32[9,9,256]{2,1,0:T(8,128)} %copy-done.15) | copy-start | bytes 248836
  387.8 10.0 %copy-start.7 = (f32[160,128]{1,0:T(8,128)S(1)}, f32[160,128]{1,0:T(8,128)}, u32[]{:S(2)}) copy-start(f32[160,128]{1,0:T(8,128)} %gather_fusion) | copy-start | bytes 245764
  510.1 12.7 %all-to-all-start.14 = ((f32[16,1,4096]{2,1,0:T(1,128)}), f32[16,1,4096]{2,1,0:T(1,128)S(1)}, u32[]{:S(2)}, u32[]{:S(2)}) async-start(f32[16,1,4096]{2,1,0:T(1,128)} %reshape.397), calls=%async_computation.14 | async-start | bytes 524288 | tf_op jit(solution)/shard_map/all_to_all | solution.py:84
  524.1 11.2 %copy-start.20 = (f32[128,128]{0,1:T(8,128)S(1)}, f32[128,128]{0,1:T(8,128)}, u32[]{:S(2)}) copy-start(f32[128,128]{0,1:T(8,128)} %copy-done.17) | copy-start | bytes 196612
  524.1 11.2 %copy-start.27 = (f32[3,128,128]{1,2,0:T(8,128)S(1)}, f32[3,128,128]{1,2,0:T(8,128)}, u32[]{:S(2)}) copy-start(f32[3,128,128]{1,2,0:T(8,128)} %get-tuple-element.100) | copy-start | bytes 589828
  553.2 31.2 %copy-start.4 = (f32[3,10,10,256]{3,2,1,0:T(8,128)S(1)}, f32[3,10,10,256]{3,2,1,0:T(8,128)}, u32[]{:S(2)}) copy-start(f32[3,10,10,256]{3,2,1,0:T(8,128)} %copy-done.3) | copy-start | bytes 921604
  593.9 22.0 %copy-start.9 = (f32[3,10,10,256]{3,2,1,0:T(8,128)S(1)}, f32[3,10,10,256]{3,2,1,0:T(8,128)}, u32[]{:S(2)}) copy-start(f32[3,10,10,256]{3,2,1,0:T(8,128)} %copy-done.8) | copy-start | bytes 921604
  (12 other events, 37.2 us)
